TPU v7x, 32 devices: a whole 2x2x4 slice. The times are simulated.
32 devices in a mesh: copies: 2 (over y), dom: 8 (over z, x), cls: 2 (over core).
Axes of the slice: x: 2, y: 2, z: 4, core: 2. Of those that a mesh axis runs over, the one named last changes fastest.
Arguments:
- images: bfloat16 [512, 256, 256], P(('copies', 'dom', 'cls')), parts along dimension 0, may hold values from -100 to 100
- references: bfloat16 [128, 2, 128, 128], P(('copies', 'dom')), parts along dimension 0, may hold values from -6 to 6
- particle_class: int32 [512], P(('copies', 'dom', 'cls')), parts along dimension 0, may hold values from 0 to 63, as said below
- rotation: int32 [512], P(('copies', 'dom', 'cls')), parts along dimension 0, may hold values from 0 to 7
- defocus_bin: int32 [512], P(('copies', 'dom', 'cls')), parts along dimension 0, may hold values from 0 to 15
- window_anchor: int32 [2, 512], P(None, ('copies', 'dom', 'cls')), parts along dimension 1, may hold values from -12 to 12
Outputs:
- new_references: float32 [128, 2, 128, 128], P(('copies', 'dom'), None, 'cls'), parts along dimension 0
- particle_stats: float32 [3, 512], P(None, ('copies', 'dom', 'cls')), parts along dimension 1
There are 2 independent parts, one for each index of `copies`. A program takes and returns all parts, laid end to end along the dimension named above; each array names one. Nothing has to cross between parts.
Inputs may be any that keep to these rules, and one draw needn't show every extreme that they name: `particle_class`: among the particles of one device, at most 4 have classes c with the same c // 8; in every draw some value of c // 8 is taken by exactly 4 particles of every device.
All inputs are finite; a program needn't handle non-finite values.
Results may differ from a plain program's by a relative error of at most 0.012.
The roundings to bfloat16 on the way count: a program that leaves them out, or rounds other values in their place, can miss the bound.
Values may be sent and summed in bfloat16 or wider, within the bound.
No kernel may reach another device: no remote copies, remote signals or barrier semaphores. Data moves between devices by JAX's collectives and lax.ppermute only.
A program may use at most 128 MiB of HBM per device.

v0:
```python
import math

import jax
import jax.numpy as jnp
from jax import lax
from jax.experimental import pallas as pl
from jax.experimental.pallas import tpu as pltpu
from jax.sharding import PartitionSpec as P

TW = 8


score_scale = 0.02
ridge_term = 1.0
highest = lax.Precision.HIGHEST


def freq_ids(win_side):
    return jnp.arange(win_side, dtype=jnp.int32) - win_side // 2


def dft_tables(img_side, win_side):
    phase_int = (
        freq_ids(win_side)[:, None] * jnp.arange(img_side, dtype=jnp.int32)[None, :] % img_side
    )
    angles = phase_int.astype(jnp.float32) * (2.0 * math.pi / img_side)
    scale_by = 1.0 / math.sqrt(img_side)
    return (
        (jnp.cos(angles) * scale_by).astype(jnp.bfloat16),
        (-jnp.sin(angles) * scale_by).astype(jnp.bfloat16),
    )


def shift_tables(anchor, img_side, win_side, span_len):
    shifts = anchor[:, None] + jnp.arange(span_len, dtype=jnp.int32)[None, :] - span_len // 2
    phase_int = freq_ids(win_side)[None, :, None] * shifts[:, None, :] % img_side
    angles = phase_int.astype(jnp.float32) * (2.0 * math.pi / img_side)
    return (
        jnp.cos(angles).astype(jnp.bfloat16),
        jnp.sin(angles).astype(jnp.bfloat16),
        shifts.astype(jnp.float32),
    )


def ctf_table(bin_ids, win_side):
    freqs = freq_ids(win_side).astype(jnp.float32)
    radius = (freqs[:, None] * freqs[:, None] + freqs[None, :] * freqs[None, :]) / float(
        win_side * win_side
    )
    strength = 20.0 + 6.0 * bin_ids.astype(jnp.float32)
    return -jnp.sin(strength[:, None, None] * radius[None, :, :] + 0.1)


def rotate_grid(stack_in, rot_ids):
    flag_bits = rot_ids[:, None, None]
    result = jnp.where(flag_bits & 4 != 0, jnp.swapaxes(stack_in, 1, 2), stack_in)
    result = jnp.where(flag_bits & 1 != 0, result[:, ::-1, :], result)
    return jnp.where(flag_bits & 2 != 0, result[:, :, ::-1], result)


def transform(images, rot_ids, dft_cos, dft_sin):
    win_side = dft_cos.shape[0]
    stacked = jnp.concatenate([dft_cos, dft_sin], axis=0)
    flag_bits = rot_ids[:, None, None]
    col_table = jnp.where(flag_bits & 2 != 0, stacked[None, :, ::-1], stacked[None])
    plain = jnp.einsum("nyx,nkx->nyk", images, col_table, preferred_element_type=jnp.float32)
    turned = jnp.einsum("nxy,nkx->nyk", images, col_table, preferred_element_type=jnp.float32)
    half_done = jnp.where(flag_bits & 4 != 0, turned, plain).astype(jnp.bfloat16)
    row_cos = jnp.where(flag_bits & 1 != 0, dft_cos[None, :, ::-1], dft_cos[None])
    row_sin = jnp.where(flag_bits & 1 != 0, dft_sin[None, :, ::-1], dft_sin[None])
    from_cos = jnp.einsum("njy,nyk->njk", row_cos, half_done, preferred_element_type=jnp.float32)
    from_sin = jnp.einsum("njy,nyk->njk", row_sin, half_done, preferred_element_type=jnp.float32)
    real_part = from_cos[..., :win_side] - from_sin[..., win_side:]
    imag_part = from_cos[..., win_side:] + from_sin[..., :win_side]
    return jnp.stack([real_part, imag_part], axis=1).astype(jnp.bfloat16)


def evaluate(fourier, chosen, ctf_map, row_cos, row_sin, col_cos, col_sin, row_shift, col_shift):
    span_len = col_cos.shape[2]
    coef_re = fourier[:, 0].astype(jnp.float32)
    coef_im = fourier[:, 1].astype(jnp.float32)
    pred_re = ctf_map * chosen[:, 0].astype(jnp.float32)
    pred_im = ctf_map * chosen[:, 1].astype(jnp.float32)
    prod_re = (coef_re * pred_re + coef_im * pred_im).astype(jnp.bfloat16)
    prod_im = (coef_im * pred_re - coef_re * pred_im).astype(jnp.bfloat16)
    shift_col = jnp.concatenate([col_cos, col_sin], axis=2)
    from_real = jnp.einsum("nuv,nvb->nub", prod_re, shift_col, preferred_element_type=jnp.float32)
    from_imag = jnp.einsum("nuv,nvb->nub", prod_im, shift_col, preferred_element_type=jnp.float32)
    part_re = from_real[..., :span_len] - from_imag[..., span_len:]
    part_im = from_real[..., span_len:] + from_imag[..., :span_len]
    cos_rows = row_cos.astype(jnp.float32)
    sin_rows = row_sin.astype(jnp.float32)
    cos_cols = col_cos.astype(jnp.float32)
    sin_cols = col_sin.astype(jnp.float32)
    correl = jnp.einsum("nua,nub->nab", cos_rows, part_re, precision=highest) - jnp.einsum(
        "nua,nub->nab", sin_rows, part_im, precision=highest
    )
    score = score_scale * correl.reshape(fourier.shape[0], span_len * span_len)
    peak = jnp.max(score, axis=1, keepdims=True)
    evidence = peak[:, 0] + jnp.log(jnp.sum(jnp.exp(score - peak), axis=1))
    weight = jnp.exp(score - evidence[:, None]).reshape(fourier.shape[0], span_len, span_len)
    mean_row = jnp.sum(jnp.sum(weight, axis=2) * row_shift, axis=1)
    mean_col = jnp.sum(jnp.sum(weight, axis=1) * col_shift, axis=1)
    qpart_re = jnp.einsum("nab,nvb->nav", weight, cos_cols, precision=highest)
    qpart_im = jnp.einsum("nab,nvb->nav", weight, sin_cols, precision=highest)
    rows_both = jnp.concatenate([cos_rows, sin_rows], axis=2)
    for_real = jnp.concatenate([qpart_re, -qpart_im], axis=1)
    for_imag = jnp.concatenate([qpart_im, qpart_re], axis=1)
    back_re = jnp.einsum("nua,nav->nuv", rows_both, for_real, precision=highest)
    back_im = jnp.einsum("nua,nav->nuv", rows_both, for_imag, precision=highest)
    term_re = ctf_map * (coef_re * back_re - coef_im * back_im)
    term_im = ctf_map * (coef_re * back_im + coef_im * back_re)
    class_terms = jnp.stack([term_re, term_im, ctf_map * ctf_map], axis=1)
    particle_info = jnp.stack([evidence, mean_row, mean_col], axis=1)
    return (class_terms, particle_info)


def _slot_kernel(meta_ref, coef_ref, ref_ref, ctf_ref, pack_ref, total_ref, info_ref):
    s = pl.program_id(0)
    span = 8

    @pl.when(s == 0)
    def _():
        total_ref[...] = jnp.zeros(total_ref.shape, total_ref.dtype)

    valid = meta_ref[0, s] > 0
    info_ref[...] = jnp.zeros(info_ref.shape, info_ref.dtype)

    @pl.when(valid)
    def _():
        cls = jnp.maximum(meta_ref[0, s] - 1, 0)
        coef_re = coef_ref[0, 0].astype(jnp.float32)
        coef_im = coef_ref[0, 1].astype(jnp.float32)
        ctf = ctf_ref[0]
        pred_re = ctf * ref_ref[0, 0].astype(jnp.float32)
        pred_im = ctf * ref_ref[0, 1].astype(jnp.float32)
        prod_re = (coef_re * pred_re + coef_im * pred_im).astype(jnp.bfloat16)
        prod_im = (coef_im * pred_re - coef_re * pred_im).astype(jnp.bfloat16)
        rows = pack_ref[0, 0]
        rows_t = pack_ref[0, 1].astype(jnp.float32)
        cols = pack_ref[0, 2]
        cols_b = pack_ref[0, 3]
        both = jnp.concatenate([prod_re, prod_im], axis=1)
        mix = jnp.concatenate([cols, cols_b], axis=0)
        part = jnp.dot(both, mix, preferred_element_type=jnp.float32)
        corr = jnp.dot(rows_t[0:16], part, precision=highest, preferred_element_type=jnp.float32)
        upper = corr[0:8]
        lower = pltpu.roll(corr[8:16], 128 - span, 1)
        lane = lax.broadcasted_iota(jnp.int32, (8, 128), 1)
        sub = lax.broadcasted_iota(jnp.int32, (8, 128), 0)
        inside = lane < span
        score = jnp.where(inside, score_scale * (upper - lower), -jnp.inf)
        peak = jnp.max(jnp.max(score, axis=1, keepdims=True), axis=0, keepdims=True)
        total = jnp.sum(jnp.sum(jnp.exp(score - peak), axis=1, keepdims=True), axis=0, keepdims=True)
        evidence = peak + jnp.log(total)
        weight = jnp.where(inside, jnp.exp(score - evidence), 0.0)
        row_shift = (jnp.full((8, 128), meta_ref[2, s], jnp.int32) + sub - span // 2).astype(jnp.float32)
        col_shift = (jnp.full((8, 128), meta_ref[3, s], jnp.int32) + lane - span // 2).astype(jnp.float32)
        by_row = jnp.sum(weight, axis=1, keepdims=True)
        mean_row = jnp.sum(by_row * row_shift[:, 0:1], axis=0, keepdims=True)
        by_col = jnp.sum(weight, axis=0, keepdims=True)
        mean_col = jnp.sum(jnp.where(inside[0:1], by_col * col_shift[0:1], 0.0), axis=1, keepdims=True)
        lane1 = lane[0:1]
        info_ref[0] = jnp.where(
            sub == 0,
            jnp.where(lane == 0, evidence, jnp.where(lane == 1, mean_row, jnp.where(lane == 2, mean_col, 0.0))),
            0.0,
        )
        shifted = pltpu.roll(weight, span, 1)
        stacked_w = jnp.concatenate([weight, shifted], axis=0)
        cols_f = cols.astype(jnp.float32)
        qpart = lax.dot_general(
            stacked_w, cols_f, (((1,), (1,)), ((), ())), precision=highest,
            preferred_element_type=jnp.float32,
        )
        q_re = qpart[0:8]
        q_im = qpart[8:16]
        pad = jnp.zeros((112, 128), jnp.float32)
        for_re = jnp.concatenate([q_re, -q_im, pad], axis=0)
        for_im = jnp.concatenate([q_im, q_re, pad], axis=0)
        rows_f = rows.astype(jnp.float32)
        back_re = jnp.dot(rows_f, for_re, precision=highest, preferred_element_type=jnp.float32)
        back_im = jnp.dot(rows_f, for_im, precision=highest, preferred_element_type=jnp.float32)
        term_re = ctf * (coef_re * back_re - coef_im * back_im)
        term_im = ctf * (coef_re * back_im + coef_im * back_re)
        total_ref[cls, 0] = total_ref[cls, 0] + term_re
        total_ref[cls, 1] = total_ref[cls, 1] + term_im
        total_ref[cls, 2] = total_ref[cls, 2] + ctf * ctf


def slot_eval(meta, coef, refs, ctf_tab, pack, interpret=False):
    slots = coef.shape[0]
    per_owner = refs.shape[0]
    win = coef.shape[2]
    bins = ctf_tab.shape[0]

    def coef_map(s, meta):
        return (s, 0, 0, 0)

    def ref_map(s, meta):
        return (jnp.clip(meta[0, s] - 1, 0, per_owner - 1), 0, 0, 0)

    def ctf_map(s, meta):
        return (jnp.clip(meta[1, s], 0, bins - 1), 0, 0)

    grid_spec = pltpu.PrefetchScalarGridSpec(
        num_scalar_prefetch=1,
        grid=(slots,),
        in_specs=[
            pl.BlockSpec((1, 2, win, win), coef_map),
            pl.BlockSpec((1, 2, win, win), ref_map),
            pl.BlockSpec((1, win, win), ctf_map),
            pl.BlockSpec((1, 4, win, win), coef_map),
        ],
        out_specs=[
            pl.BlockSpec((per_owner, 3, win, win), lambda s, meta: (0, 0, 0, 0)),
            pl.BlockSpec((1, 8, 128), lambda s, meta: (s, 0, 0)),
        ],
    )
    return pl.pallas_call(
        _slot_kernel,
        grid_spec=grid_spec,
        out_shape=[
            jax.ShapeDtypeStruct((per_owner, 3, win, win), jnp.float32),
            jax.ShapeDtypeStruct((slots, 8, 128), jnp.float32),
        ],
        compiler_params=pltpu.CompilerParams(dimension_semantics=("arbitrary",)),
        interpret=interpret,
    )(meta, coef, refs, ctf_tab, pack)


def phase_pack(tag_flat, img_side, win_side):
    rc, rs, _ = shift_tables(tag_flat[:, 2], img_side, win_side, TW)
    cc, cs, _ = shift_tables(tag_flat[:, 3], img_side, win_side, TW)
    spare = jnp.zeros(rc.shape[:2] + (win_side - 2 * TW,), jnp.bfloat16)
    rows = jnp.concatenate([rc, rs, spare], axis=2)
    cols = jnp.concatenate([cc, cs, spare], axis=2)
    cols_b = jnp.concatenate([-cs, cc, spare], axis=2)
    return jnp.stack([rows, jnp.swapaxes(rows, 1, 2), cols, cols_b], axis=1)


def on_device(images, references, particle_class, rotation, defocus_bin, window_anchor):
    part_count = images.shape[0]
    img_side = images.shape[1]
    win_side = references.shape[2]
    per_owner = references.shape[0]
    owners = lax.axis_size("dom")
    capacity = max(2, 2 * part_count // owners)
    slot_count = owners * capacity
    target = particle_class // per_owner
    local_class = particle_class - target * per_owner
    positions = jnp.arange(part_count, dtype=jnp.int32)
    same_owner = (target[:, None] == target[None, :]) & (positions[None, :] < positions[:, None])
    slot_rank = jnp.sum(same_owner.astype(jnp.int32), axis=1)
    slot_place = target * capacity + slot_rank
    slot_tags = jnp.stack(
        [local_class + 1, defocus_bin, window_anchor[0], window_anchor[1]], axis=1
    ).astype(jnp.bfloat16)
    tag_buffer = (
        jnp.zeros((slot_count, 4), jnp.bfloat16)
        .at[slot_place]
        .set(slot_tags)
        .reshape(owners, capacity, 4)
    )
    dft_cos, dft_sin = dft_tables(img_side, win_side)
    fourier_own = transform(images, rotation, dft_cos, dft_sin)
    buffer = (
        jnp.zeros((slot_count, 2, win_side, win_side), jnp.bfloat16).at[slot_place].set(fourier_own)
    )
    buffer = buffer.reshape(owners, capacity, 2, win_side, win_side)
    ctf_bins = ctf_table(jnp.arange(16, dtype=jnp.int32), win_side)
    coeff_block = lax.all_to_all(buffer, "dom", split_axis=0, concat_axis=0, tiled=True)
    tag_block = lax.all_to_all(tag_buffer, "dom", split_axis=0, concat_axis=0, tiled=True)
    tag_flat = tag_block.reshape(slot_count, 4).astype(jnp.int32)
    pack = phase_pack(tag_flat, img_side, win_side)
    partial_value, info = slot_eval(
        tag_flat.T,
        coeff_block.reshape(slot_count, 2, win_side, win_side),
        references,
        ctf_bins,
        pack,
    )
    returned = lax.all_to_all(
        info[:, 0, :3].reshape(owners, capacity, 3), "dom", split_axis=0, concat_axis=0, tiled=True
    )
    summed = lax.psum_scatter(partial_value, "cls", scatter_dimension=2, tiled=True)
    divisor = summed[:, 2] + ridge_term
    new_refs = summed[:, :2] / divisor[:, None]
    particle_info = returned.reshape(slot_count, 3)[slot_place]
    return (new_refs, particle_info.T)


def solution(mesh):
    return jax.shard_map(
        on_device,
        mesh=mesh,
        in_specs=(
            P(("copies", "dom", "cls"), None, None),
            P(("copies", "dom"), None, None, None),
            P(("copies", "dom", "cls")),
            P(("copies", "dom", "cls")),
            P(("copies", "dom", "cls")),
            P(None, ("copies", "dom", "cls")),
        ),
        out_specs=(P(("copies", "dom"), None, "cls", None), P(None, ("copies", "dom", "cls"))),
        check_vma=False,
    )
```

profile of v0, /device:TPU:0, one launch (start us, length us, event | category | flops | bytes accessed | tf_op | source)
XLA Modules:
  0.0 151.7 jit_solution(8496412812045180076)
XLA Ops:
  7.2 0.8 convert_bitcast_fusion.1
  8.0 0.2 convert_reduce_fusion
  8.2 0.7 convert.27
  8.9 0.7 convert_bitcast_fusion
  9.6 0.1 copy.49
  9.7 0.6 scatter_custom_fusion
  10.3 0.7 copy.51
  11.0 7.3 %all-to-all-start = ((bf16[8,4,4]{1,2,0:T(4,128)(2,1)}), bf16[8,4,4]{1,2,0:T(4,128)(2,1)S(1)}, u32[]{:S(2)}, u32[]{:S(2)}) async-start(bf16[8,4,4]{1,2,0:T(4,128)(2,1)} %copy.51), calls=%async_computation | async-start | bytes 16384 | tf_op jit(solution)/shard_map/all_to_all | solution.py:273
  18.3 0.6 multiply_convert_fusion.1
  18.9 0.2 rev.11
  19.2 0.2 rev.9
  19.4 0.4 rev.10
  19.9 0.7 and_compare_fusion.2
  20.5 0.8 fusion
  21.3 0.8 select_convert_fusion
  22.1 0.8 fusion.10
  23.0 0.8 fusion.16
  23.8 0.4 fusion.20
  24.2 0.1 pad_maximum_fusion.1
  24.3 0.1 copy.54
  24.4 1.9 %broadcast_in_dim.111 = bf16[32,2,128,128]{3,2,1,0:T(8,128)(2,1)} broadcast(bf16[]{:T(256)} %constant.37.clone.1), dimensions={} | broadcast | bytes 2097154 | tf_op jit(solution)/shard_map/broadcast_in_dim | solution.py:268
  26.2 3.0 %scatter_fusion = bf16[32,2,128,128]{3,2,1,0:T(8,128)(2,1)} fusion(bf16[32,2,128,128]{3,2,1,0:T(8,128)(2,1)} %broadcast_in_dim.111, s32[16]{0:T(128)S(1)} %compare_select_fusion, bf16[16,2,128,128]{3,2,1,0:T(8,128)(2,1)S(1)} %copy.54), kind=kCustom, calls=%fused_computation.2 | custom fusion | bytes 3145792 | tf_op jit(solution)/shard_map/scatter | solution.py:268
  29.2 6.0 %all-to-all-start.1 = ((bf16[8,4,2,128,128]{4,3,2,1,0:T(8,128)(2,1)}), bf16[8,4,2,128,128]{4,3,2,1,0:T(8,128)(2,1)}, u32[]{:S(2)}, u32[]{:S(2)}) async-start(bf16[8,4,2,128,128]{4,3,2,1,0:T(8,128)(2,1)} %bitcast.45), calls=%async_computation.1 | async-start | bytes 4194304 | tf_op jit(solution)/shard_map/all_to_all | solution.py:272
  35.2 0.2 reduce-scatter.2.cloned.1.call-start
  35.6 4.4 %sine_negate_fusion.ctf_ref = f32[16,128,128]{2,1,0:T(8,128)} fusion(f32[128,128]{1,0:T(8,128)S(1)} %add_multiply_fusion, f32[16]{0:T(128)S(1)} %multiply_add_fusion), kind=kLoop, calls=%fused_computation.23 | loop fusion | flops 786432 | bytes 1114176 | tf_op jit(solution)/shard_map/neg | solution.py:51
  40.0 0.1 copy.52
  40.1 0.1 copy.53
  40.2 0.1 reshape.186
  40.4 0.2 fusion.30
  40.6 1.9 %copy.56 = f32[32,128,8]{2,1,0:T(8,128)} copy(f32[32,128,8]{1,2,0:T(8,128)S(1)} %get-tuple-element.33) | data formatting | bytes 262144 | tf_op jit(solution)/shard_map/convert_element_type | solution.py:37
  42.5 1.9 %copy.55 = f32[32,128,8]{2,1,0:T(8,128)} copy(f32[32,128,8]{1,2,0:T(8,128)S(1)} %get-tuple-element.32) | data formatting | bytes 262144 | tf_op jit(solution)/shard_map/convert_element_type | solution.py:37
  44.5 8.0 %cosine_convert_fusion = bf16[32,128,8]{2,1,0:T(8,128)(2,1)S(1)} fusion(f32[32,128,8]{2,1,0:T(8,128)} %copy.56), kind=kLoop, calls=%fused_computation.10 | loop fusion | flops 65536 | bytes 196608 | tf_op jit(solution)/shard_map/convert_element_type | solution.py:39
  52.5 7.0 %fusion.42 = (bf16[32,128,8]{2,1,0:T(8,128)(2,1)S(1)}, bf16[32,128,8]{2,1,0:T(8,128)(2,1)S(1)}) fusion(f32[32,128,8]{2,1,0:T(8,128)S(1)} %copy-done.1), kind=kLoop, calls=%fused_computation.98 | loop fusion | flops 163840 | bytes 262144 | tf_op jit(solution)/shard_map/neg | solution.py:238
  59.5 7.6 %cosine_convert_fusion.1 = (bf16[32,128,8]{2,1,0:T(8,128)(2,1)S(1)}, bf16[32,128,8]{2,1,0:T(8,128)(2,1)S(1)}) fusion(f32[32,128,8]{2,1,0:T(8,128)S(1)} %copy-done.2), kind=kLoop, calls=%fused_computation.12 | loop fusion | flops 98304 | bytes 262144 | tf_op jit(solution)/shard_map/convert_element_type | solution.py:39
  67.1 3.6 %fusion.38 = (bf16[32,1,128,128]{3,2,1,0:T(8,128)(2,1)}, bf16[32,1,128,128]{2,3,0,1:T(8,128)(2,1)S(1)}, bf16[32,1,128,128]{3,2,1,0:T(8,128)(2,1)}, bf16[32,1,128,128]{3,2,1,0:T(8,128)(2,1)}) fusion(bf16[128]{0:T(256)(128)(2,1)S(1)} %pad.12.clone, bf16[32,128,8]{2,1,0:T(8,128)(2,1)S(1)} %get-tuple-element.25, bf16[32,128,8]{2,1,0:T(8,128)(2,1)S(1)} %get-tuple-element.24, ...), kind=kLoop, calls=%fused_computation.71 | loop fusion | flops 8388608 | bytes 4522240 | tf_op jit(solution)/shard_map/stack | solution.py:239
  70.7 1.3 copy.58
  72.0 3.7 %pad_maximum_fusion.pack_ref = bf16[32,4,128,128]{3,2,1,0:T(8,128)(2,1)} fusion(bf16[32,1,128,128]{3,2,1,0:T(8,128)(2,1)} %get-tuple-element.30, bf16[32,1,128,128]{3,2,1,0:T(8,128)(2,1)} %get-tuple-element.31, bf16[32,1,128,128]{3,2,1,0:T(8,128)(2,1)} %copy.58, bf16[32,1,128,128]{3,2,1,0:T(8,128)(2,1)} %get-tuple-element.22), kind=kLoop, calls=%fused_computation.3 | loop fusion | flops 6291456 | bytes 8388608 | tf_op jit(solution)/shard_map/stack | solution.py:239
  75.7 7.2 %all-to-all-done.1 = bf16[8,4,2,128,128]{4,3,2,1,0:T(8,128)(2,1)} async-done(((bf16[8,4,2,128,128]{4,3,2,1,0:T(8,128)(2,1)}), bf16[8,4,2,128,128]{4,3,2,1,0:T(8,128)(2,1)}, u32[]{:S(2)}, u32[]{:S(2)}) %all-to-all-start.1) | async-done | bytes 2097184 | tf_op jit(solution)/shard_map/all_to_all | solution.py:272
  83.0 24.7 %shard_map.77 = (f32[8,3,128,128]{3,2,1,0:T(8,128)}, f32[32,8,128]{2,1,0:T(8,128)}) custom-call(s32[4,32]{1,0:T(4,128)} %bitcast.50, bf16[32,2,128,128]{3,2,1,0:T(8,128)(2,1)} %bitcast.9.coef_ref, bf16[8,2,128,128]{3,2,1,0:T(8,128)(2,1)} %ref_ref.1, f32[16,128,128]{2,1,0:T(8,128)} %sine_negate_fusion.ctf_ref, bf16[32,4,128,128]{3,2,1,0:T(8,128)(2,1)} %pad_maximum_fusion.pack_ref), custom_call_target="tpu_custom_call" | custom-call | tf_op jit(solution)/shard_map/pallas_call | solution.py:220
  107.7 0.9 slice.45
  108.6 0.7 copy.61
  109.3 24.7 %all-to-all-start.2 = ((f32[8,4,3]{1,2,0:T(4,128)}), f32[8,4,3]{1,2,0:T(4,128)S(1)}, u32[]{:S(2)}, u32[]{:S(2)}) async-start(f32[8,4,3]{1,2,0:T(4,128)} %copy.61), calls=%async_computation.3 | async-start | bytes 32768 | tf_op jit(solution)/shard_map/all_to_all | solution.py:283
  134.1 6.6 %all-to-all-done.2 = f32[8,4,3]{1,2,0:T(4,128)S(1)} async-done(((f32[8,4,3]{1,2,0:T(4,128)}), f32[8,4,3]{1,2,0:T(4,128)S(1)}, u32[]{:S(2)}, u32[]{:S(2)}) %all-to-all-start.2) | async-done | bytes 416 | tf_op jit(solution)/shard_map/all_to_all | solution.py:283
  140.7 0.1 copy.69
  140.8 0.6 gather_fusion
  141.3 0.7 copy.64
  142.0 1.0 fusion.26
  143.0 1.9 %slice_divide_fusion = f32[8,2,64,128]{3,2,1,0:T(8,128)} fusion(f32[8,3,64,128]{3,2,1,0:T(8,128)} %reduce-scatter.2.cloned.1.call-done, f32[8,64,128]{2,1,0:T(8,128)S(1)} %fusion.26), kind=kLoop, calls=%fused_computation.36 | loop fusion | flops 131072 | bytes 1310720 | tf_op jit(solution)/shard_map/div | solution.py:288
  (25 shorter events, 0.4 us)
Async XLA Ops:
  7.2 13.4 %copy-start = (bf16[16,256,256]{2,1,0:T(8,128)(2,1)S(1)}, bf16[16,256,256]{2,1,0:T(8,128)(2,1)}, u32[]{:S(2)}) copy-start(bf16[16,256,256]{2,1,0:T(8,128)(2,1)} %param.6) | copy-start | bytes 6291460
  11.0 18.2 %all-to-all-start = ((bf16[8,4,4]{1,2,0:T(4,128)(2,1)}), bf16[8,4,4]{1,2,0:T(4,128)(2,1)S(1)}, u32[]{:S(2)}, u32[]{:S(2)}) async-start(bf16[8,4,4]{1,2,0:T(4,128)(2,1)} %copy.51), calls=%async_computation | async-start | bytes 16384 | tf_op jit(solution)/shard_map/all_to_all | solution.py:273
  29.2 53.8 %all-to-all-start.1 = ((bf16[8,4,2,128,128]{4,3,2,1,0:T(8,128)(2,1)}), bf16[8,4,2,128,128]{4,3,2,1,0:T(8,128)(2,1)}, u32[]{:S(2)}, u32[]{:S(2)}) async-start(bf16[8,4,2,128,128]{4,3,2,1,0:T(8,128)(2,1)} %bitcast.45), calls=%async_computation.1 | async-start | bytes 4194304 | tf_op jit(solution)/shard_map/all_to_all | solution.py:272
  35.2 106.8 %reduce-scatter.2.cloned.1.call-start = ((), (), s32[]{:S(2)}) async-start(), calls=%async_computation.4 | async-start | bytes 2359296 | tf_op jit(solution)/shard_map/reduce_scatter | solution.py:286
  40.3 4.2 %copy-start.3 = (s32[32,4]{0,1:T(4,128)}, s32[32,4]{0,1:T(4,128)S(1)}, u32[]{:S(2)}) copy-start(s32[32,4]{0,1:T(4,128)S(1)} %reshape.186) | copy-start | bytes 1540
  44.5 8.0 %copy-start.1 = (f32[32,128,8]{2,1,0:T(8,128)S(1)}, f32[32,128,8]{2,1,0:T(8,128)}, u32[]{:S(2)}) copy-start(f32[32,128,8]{2,1,0:T(8,128)} %copy.56) | copy-start | bytes 393220
  52.5 7.0 %copy-start.2 = (f32[32,128,8]{2,1,0:T(8,128)S(1)}, f32[32,128,8]{2,1,0:T(8,128)}, u32[]{:S(2)}) copy-start(f32[32,128,8]{2,1,0:T(8,128)} %copy.55) | copy-start | bytes 393220
  109.3 31.3 %all-to-all-start.2 = ((f32[8,4,3]{1,2,0:T(4,128)}), f32[8,4,3]{1,2,0:T(4,128)S(1)}, u32[]{:S(2)}, u32[]{:S(2)}) async-start(f32[8,4,3]{1,2,0:T(4,128)} %copy.61), calls=%async_computation.3 | async-start | bytes 32768 | tf_op jit(solution)/shard_map/all_to_all | solution.py:283
Sparse Core Ops, SparseCore 0:
  107.8 28.4 reduce-scatter.1
where the time goes:
time: 152 us
  other arithmetic  41.7 us (27%)
  starting transfers between devices  38.2 us (25%)
  Pallas kernels  24.7 us (16%)
  local copies, waits for them, and re-layouts  15.9 us (10%)
  between operations  14.2 us (9%)
  waiting for transfers between devices  13.8 us (9%)
  matrix products  3.21 us (2%)
    all_to_all x1, starting transfers between devices, on_device(): lax.all_to_all(info[:, 0, :3].reshape(owners, capacity, 3), 'dom', split_...  24.7 us
    pallas_call x1, Pallas kernels, slot_eval(): pl.pallas_call(_slot_kernel, grid_spec=grid_spec, out_shape=[jax.ShapeDty...  24.7 us
    convert_element_type x2, other arithmetic, shift_tables(): jnp.cos(angles).astype(jnp.bfloat16)  15.6 us
    another operation x2, other arithmetic, phase_pack(): return jnp.stack([rows, jnp.swapaxes(rows, 1, 2), cols, cols_b], axis=1)  7.29 us
    all_to_all x1, starting transfers between devices, on_device(): lax.all_to_all(tag_buffer, 'dom', split_axis=0, concat_axis=0, tiled=True)  7.28 us
    all_to_all x1, waiting for transfers between devices, on_device(): lax.all_to_all(buffer, 'dom', split_axis=0, concat_axis=0, tiled=True)  7.24 us
    neg x1, other arithmetic, phase_pack(): cols_b = jnp.concatenate([-cs, cc, spare], axis=2)  7.01 us
    all_to_all x1, waiting for transfers between devices, on_device(): lax.all_to_all(info[:, 0, :3].reshape(owners, capacity, 3), 'dom', split_...  6.57 us
  transfers between devices with their start and end apart: 4, of which 2 were waited for; matrix products, arithmetic and copies ran while one was open for 36% of the time, Pallas kernels for 0%

commit v1 on v0

--- a/solution.py
+++ b/solution.py
@@ -115,6 +115,22 @@
     return (class_terms, particle_info)
 
 
+def _split3(value):
+    high = value.astype(jnp.bfloat16)
+    rest = value - high.astype(jnp.float32)
+    middle = rest.astype(jnp.bfloat16)
+    low = (rest - middle.astype(jnp.float32)).astype(jnp.bfloat16)
+    return high, middle, low
+
+
+def _exact_dot(lhs, rhs):
+    if lhs.dtype == jnp.bfloat16:
+        parts = [jnp.dot(lhs, piece, preferred_element_type=jnp.float32) for piece in _split3(rhs)]
+    else:
+        parts = [jnp.dot(piece, rhs, preferred_element_type=jnp.float32) for piece in _split3(lhs)]
+    return parts[0] + parts[1] + parts[2]
+
+
 def _slot_kernel(meta_ref, coef_ref, ref_ref, ctf_ref, pack_ref, total_ref, info_ref):
     s = pl.program_id(0)
     span = 8
@@ -137,13 +153,13 @@
         prod_re = (coef_re * pred_re + coef_im * pred_im).astype(jnp.bfloat16)
         prod_im = (coef_im * pred_re - coef_re * pred_im).astype(jnp.bfloat16)
         rows = pack_ref[0, 0]
-        rows_t = pack_ref[0, 1].astype(jnp.float32)
-        cols = pack_ref[0, 2]
-        cols_b = pack_ref[0, 3]
+        cols = pack_ref[0, 1]
+        cols_b = pack_ref[0, 2]
+        flat = pack_ref[0, 3]
         both = jnp.concatenate([prod_re, prod_im], axis=1)
         mix = jnp.concatenate([cols, cols_b], axis=0)
         part = jnp.dot(both, mix, preferred_element_type=jnp.float32)
-        corr = jnp.dot(rows_t[0:16], part, precision=highest, preferred_element_type=jnp.float32)
+        corr = _exact_dot(flat[0:16], part)
         upper = corr[0:8]
         lower = pltpu.roll(corr[8:16], 128 - span, 1)
         lane = lax.broadcasted_iota(jnp.int32, (8, 128), 1)
@@ -160,7 +176,6 @@
         mean_row = jnp.sum(by_row * row_shift[:, 0:1], axis=0, keepdims=True)
         by_col = jnp.sum(weight, axis=0, keepdims=True)
         mean_col = jnp.sum(jnp.where(inside[0:1], by_col * col_shift[0:1], 0.0), axis=1, keepdims=True)
-        lane1 = lane[0:1]
         info_ref[0] = jnp.where(
             sub == 0,
             jnp.where(lane == 0, evidence, jnp.where(lane == 1, mean_row, jnp.where(lane == 2, mean_col, 0.0))),
@@ -168,19 +183,16 @@
         )
         shifted = pltpu.roll(weight, span, 1)
         stacked_w = jnp.concatenate([weight, shifted], axis=0)
-        cols_f = cols.astype(jnp.float32)
-        qpart = lax.dot_general(
-            stacked_w, cols_f, (((1,), (1,)), ((), ())), precision=highest,
-            preferred_element_type=jnp.float32,
-        )
+        pad = jnp.zeros((112, 128), jnp.bfloat16)
+        col_rows = jnp.concatenate([flat[16:32], pad], axis=0)
+        qpart = _exact_dot(stacked_w, col_rows)
         q_re = qpart[0:8]
         q_im = qpart[8:16]
-        pad = jnp.zeros((112, 128), jnp.float32)
-        for_re = jnp.concatenate([q_re, -q_im, pad], axis=0)
-        for_im = jnp.concatenate([q_im, q_re, pad], axis=0)
-        rows_f = rows.astype(jnp.float32)
-        back_re = jnp.dot(rows_f, for_re, precision=highest, preferred_element_type=jnp.float32)
-        back_im = jnp.dot(rows_f, for_im, precision=highest, preferred_element_type=jnp.float32)
+        zeros = jnp.zeros((112, 128), jnp.float32)
+        for_re = jnp.concatenate([q_re, -q_im, zeros], axis=0)
+        for_im = jnp.concatenate([q_im, q_re, zeros], axis=0)
+        back_re = _exact_dot(rows, for_re)
+        back_im = _exact_dot(rows, for_im)
         term_re = ctf * (coef_re * back_re - coef_im * back_im)
         term_im = ctf * (coef_re * back_im + coef_im * back_re)
         total_ref[cls, 0] = total_ref[cls, 0] + term_re
@@ -229,14 +241,26 @@
     )(meta, coef, refs, ctf_tab, pack)
 
 
+def phase_rows(anchor, img_side, win_side):
+    shifts = anchor[:, None] + jnp.arange(TW, dtype=jnp.int32)[None, :] - TW // 2
+    phase_int = shifts[:, :, None] * freq_ids(win_side)[None, None, :] % img_side
+    angles = phase_int.astype(jnp.float32) * (2.0 * math.pi / img_side)
+    return jnp.concatenate(
+        [jnp.cos(angles).astype(jnp.bfloat16), jnp.sin(angles).astype(jnp.bfloat16)], axis=1
+    )
+
+
 def phase_pack(tag_flat, img_side, win_side):
-    rc, rs, _ = shift_tables(tag_flat[:, 2], img_side, win_side, TW)
-    cc, cs, _ = shift_tables(tag_flat[:, 3], img_side, win_side, TW)
-    spare = jnp.zeros(rc.shape[:2] + (win_side - 2 * TW,), jnp.bfloat16)
-    rows = jnp.concatenate([rc, rs, spare], axis=2)
-    cols = jnp.concatenate([cc, cs, spare], axis=2)
-    cols_b = jnp.concatenate([-cs, cc, spare], axis=2)
-    return jnp.stack([rows, jnp.swapaxes(rows, 1, 2), cols, cols_b], axis=1)
+    rows_t = phase_rows(tag_flat[:, 2], img_side, win_side)
+    cols_t = phase_rows(tag_flat[:, 3], img_side, win_side)
+    cols_bt = jnp.concatenate([-cols_t[:, TW:], cols_t[:, :TW]], axis=1)
+    spare = jnp.zeros((rows_t.shape[0], win_side - 4 * TW, win_side), jnp.bfloat16)
+    flat = jnp.concatenate([rows_t, cols_t, spare], axis=1)
+    planes = [
+        jnp.pad(jnp.swapaxes(t, 1, 2), ((0, 0), (0, 0), (0, win_side - 2 * TW)))
+        for t in (rows_t, cols_t, cols_bt)
+    ]
+    return jnp.stack(planes + [flat], axis=1)
 
 
 def on_device(images, references, particle_class, rotation, defocus_bin, window_anchor):

time: 152 us -> 143 us (0.941)
  other arithmetic: 41.7 us -> 21.5 us
  starting transfers between devices: 38.2 us -> 18.2 us
  waiting for transfers between devices: 13.8 us -> 33.6 us
  Pallas kernels: 24.7 us -> 34.9 us
    all_to_all x1, starting transfers between devices: 24.7 us -> 4.71 us  [on_device(): lax.all_to_all(info[:, 0, :3].reshape(owners, capacity, 3), 'dom', split_...]
    all_to_all x1, waiting for transfers between devices: 7.24 us -> 27 us  [on_device(): lax.all_to_all(buffer, 'dom', split_axis=0, concat_axis=0, tiled=True)]
    convert_element_type x3 -> x1, other arithmetic: 15.7 us -> 1.21 us  [phase_rows(): jnp.cos(angles).astype(jnp.bfloat16)]
    pallas_call x1, Pallas kernels: 24.7 us -> 34.9 us  [slot_eval(): pl.pallas_call(_slot_kernel, grid_spec=grid_spec, out_shape=[jax.ShapeDty...]
    neg x1, other arithmetic: 7.01 us -> 1.21 us  [phase_pack(): cols_bt = jnp.concatenate([-cols_t[:, TW:], cols_t[:, :TW]], axis=1)]
    convert_element_type x2 -> x0, local copies, waits for them, and re-layouts: 3.87 us -> none  [shift_tables(): angles = phase_int.astype(jnp.float32) * (2.0 * math.pi / img_side)]
    unnamed x0 -> x3, other arithmetic: none -> 3.65 us
    another operation x3 -> x2, other arithmetic: 7.98 us -> 4.4 us  [the longest x1 3.72 us: phase_pack(): return jnp.stack(planes + [flat], axis=1)]
  transfers between devices with their start and end apart: 4 -> 4, of which waited for: 2 -> 2; matrix products, arithmetic and copies ran while one was open for 36% -> 24% of each run, Pallas kernels for 0% -> 0%
where the time goes in v1:
time: 143 us; the launch traced here: 142 us
  Pallas kernels  34.9 us (24%)
  waiting for transfers between devices  33.6 us (23%)
  other arithmetic  21.5 us (15%)
  starting transfers between devices  18.2 us (13%)
  local copies, waits for them, and re-layouts  16.3 us (11%)
  between operations  14.2 us (10%)
  matrix products  3.21 us (2%)
    pallas_call x1, Pallas kernels, slot_eval(): pl.pallas_call(_slot_kernel, grid_spec=grid_spec, out_shape=[jax.ShapeDty...  34.9 us
    all_to_all x1, waiting for transfers between devices, on_device(): lax.all_to_all(buffer, 'dom', split_axis=0, concat_axis=0, tiled=True)  27 us
    all_to_all x1, starting transfers between devices, on_device(): lax.all_to_all(tag_buffer, 'dom', split_axis=0, concat_axis=0, tiled=True)  7.28 us
    all_to_all x1, waiting for transfers between devices, on_device(): lax.all_to_all(info[:, 0, :3].reshape(owners, capacity, 3), 'dom', split_...  6.57 us
    all_to_all x1, starting transfers between devices, on_device(): lax.all_to_all(buffer, 'dom', split_axis=0, concat_axis=0, tiled=True)  5.96 us
    all_to_all x1, starting transfers between devices, on_device(): lax.all_to_all(info[:, 0, :3].reshape(owners, capacity, 3), 'dom', split_...  4.71 us
    another operation x6, local copies, waits for them, and re-layouts, phase_pack(): return jnp.stack(planes + [flat], axis=1)  4.62 us
    neg x1, other arithmetic, ctf_table(): return -jnp.sin(strength[:, None, None] * radius[None, :, :] + 0.1)  4.45 us
  transfers between devices with their start and end apart: 4, of which 2 were waited for; matrix products, arithmetic and copies ran while one was open for 24% of the time, Pallas kernels for 0%

profile of v1, /device:TPU:0, one launch (start us, length us, event | category | flops | bytes accessed | tf_op | source)
XLA Modules:
  0.0 141.9 jit_solution(13607420313516466715)
XLA Ops:
  7.2 0.8 convert_bitcast_fusion.1
  8.0 0.2 convert_reduce_fusion
  8.2 0.7 convert.27
  8.9 0.7 convert_bitcast_fusion
  9.7 0.6 scatter_custom_fusion
  10.3 0.7 copy.51
  11.0 7.3 %all-to-all-start = ((bf16[8,4,4]{1,2,0:T(4,128)(2,1)}), bf16[8,4,4]{1,2,0:T(4,128)(2,1)S(1)}, u32[]{:S(2)}, u32[]{:S(2)}) async-start(bf16[8,4,4]{1,2,0:T(4,128)(2,1)} %copy.51), calls=%async_computation | async-start | bytes 16384 | tf_op jit(solution)/shard_map/all_to_all | solution.py:297
  18.3 0.6 multiply_convert_fusion.1
  18.9 0.2 rev.11
  19.2 0.2 rev.9
  19.4 0.4 rev.10
  19.9 0.7 and_compare_fusion.2
  20.5 0.8 fusion
  21.3 0.8 select_convert_fusion
  22.1 0.8 fusion.10
  23.0 0.8 fusion.16
  23.8 0.4 fusion.20
  24.3 0.1 copy.54
  24.4 1.8 %broadcast_in_dim.111 = bf16[32,2,128,128]{3,2,1,0:T(8,128)(2,1)} broadcast(bf16[]{:T(256)} %constant.66.clone.1), dimensions={} | broadcast | bytes 2097154 | tf_op jit(solution)/shard_map/broadcast_in_dim | solution.py:292
  26.2 3.0 %scatter_fusion = bf16[32,2,128,128]{3,2,1,0:T(8,128)(2,1)} fusion(bf16[32,2,128,128]{3,2,1,0:T(8,128)(2,1)} %broadcast_in_dim.111, s32[16]{0:T(128)S(1)} %compare_select_fusion, bf16[16,2,128,128]{3,2,1,0:T(8,128)(2,1)S(1)} %copy.54), kind=kCustom, calls=%fused_computation.2 | custom fusion | bytes 3145792 | tf_op jit(solution)/shard_map/scatter | solution.py:292
  29.2 6.0 %all-to-all-start.1 = ((bf16[8,4,2,128,128]{4,3,2,1,0:T(8,128)(2,1)}), bf16[8,4,2,128,128]{4,3,2,1,0:T(8,128)(2,1)}, u32[]{:S(2)}, u32[]{:S(2)}) async-start(bf16[8,4,2,128,128]{4,3,2,1,0:T(8,128)(2,1)} %bitcast.44), calls=%async_computation.1 | async-start | bytes 4194304 | tf_op jit(solution)/shard_map/all_to_all | solution.py:296
  35.2 0.2 reduce-scatter.2.cloned.1.call-start
  35.5 4.4 %sine_negate_fusion.ctf_ref = f32[16,128,128]{2,1,0:T(8,128)} fusion(f32[128,128]{1,0:T(8,128)S(1)} %add_multiply_fusion, f32[16]{0:T(128)S(1)} %multiply_add_fusion), kind=kLoop, calls=%fused_computation.19 | loop fusion | flops 786432 | bytes 1114176 | tf_op jit(solution)/shard_map/neg | solution.py:51
  40.0 0.1 copy.52
  40.4 1.2 constant_dynamic-update-slice_fusion.3
  41.6 1.2 constant_dynamic-update-slice_fusion.2
  42.8 1.2 constant_dynamic-update-slice_fusion.1
  44.0 1.2 fusion.42
  45.2 1.2 cosine_convert_fusion.1
  46.5 0.2 pad_bitcast_fusion.1
  46.7 1.3 copy.56
  48.0 0.2 pad_bitcast_fusion
  48.3 1.3 copy.57
  49.6 0.2 pad_bitcast_fusion.2
  49.8 1.3 copy.55
  51.2 1.1 broadcast_dynamic-update-slice_fusion
  52.2 3.7 %pad_maximum_fusion.pack_ref = bf16[32,4,128,128]{3,2,1,0:T(8,128)(2,1)} fusion(bf16[32,1,128,128]{3,2,1,0:T(8,128)(2,1)} %bitcast.45, bf16[32,1,128,128]{3,2,1,0:T(8,128)(2,1)} %copy.57, bf16[32,1,128,128]{3,2,1,0:T(8,128)(2,1)} %copy.56, bf16[32,1,128,128]{3,2,1,0:T(8,128)(2,1)} %copy.55), kind=kLoop, calls=%fused_computation.3 | loop fusion | flops 6291456 | bytes 8388608 | tf_op jit(solution)/shard_map/stack | solution.py:263
  55.9 27.0 %all-to-all-done.1 = bf16[8,4,2,128,128]{4,3,2,1,0:T(8,128)(2,1)} async-done(((bf16[8,4,2,128,128]{4,3,2,1,0:T(8,128)(2,1)}), bf16[8,4,2,128,128]{4,3,2,1,0:T(8,128)(2,1)}, u32[]{:S(2)}, u32[]{:S(2)}) %all-to-all-start.1) | async-done | bytes 2097184 | tf_op jit(solution)/shard_map/all_to_all | solution.py:296
  83.0 34.9 %shard_map.77 = (f32[8,3,128,128]{3,2,1,0:T(8,128)}, f32[32,8,128]{2,1,0:T(8,128)}) custom-call(s32[4,32]{1,0:T(4,128)} %bitcast.50, bf16[32,2,128,128]{3,2,1,0:T(8,128)(2,1)} %bitcast.9.coef_ref, bf16[8,2,128,128]{3,2,1,0:T(8,128)(2,1)} %ref_ref.1, f32[16,128,128]{2,1,0:T(8,128)} %sine_negate_fusion.ctf_ref, bf16[32,4,128,128]{3,2,1,0:T(8,128)(2,1)} %pad_maximum_fusion.pack_ref), custom_call_target="tpu_custom_call" | custom-call | tf_op jit(solution)/shard_map/pallas_call | solution.py:232
  117.9 0.9 slice.51
  118.8 0.7 copy.59
  119.6 4.7 %all-to-all-start.2 = ((f32[8,4,3]{1,2,0:T(4,128)}), f32[8,4,3]{1,2,0:T(4,128)S(1)}, u32[]{:S(2)}, u32[]{:S(2)}) async-start(f32[8,4,3]{1,2,0:T(4,128)} %copy.59), calls=%async_computation.3 | async-start | bytes 32768 | tf_op jit(solution)/shard_map/all_to_all | solution.py:307
  124.3 6.6 %all-to-all-done.2 = f32[8,4,3]{1,2,0:T(4,128)S(1)} async-done(((f32[8,4,3]{1,2,0:T(4,128)}), f32[8,4,3]{1,2,0:T(4,128)S(1)}, u32[]{:S(2)}, u32[]{:S(2)}) %all-to-all-start.2) | async-done | bytes 416 | tf_op jit(solution)/shard_map/all_to_all | solution.py:307
  130.9 0.1 copy.67
  131.0 0.6 gather_fusion
  131.6 0.7 copy.62
  132.2 1.0 fusion.26
  133.2 1.9 %slice_divide_fusion = f32[8,2,64,128]{3,2,1,0:T(8,128)} fusion(f32[8,3,64,128]{3,2,1,0:T(8,128)} %reduce-scatter.2.cloned.1.call-done, f32[8,64,128]{2,1,0:T(8,128)S(1)} %fusion.26), kind=kLoop, calls=%fused_computation.32 | loop fusion | flops 131072 | bytes 1310720 | tf_op jit(solution)/shard_map/div | solution.py:312
  (25 shorter events, 0.7 us)
Async XLA Ops:
  7.2 13.4 %copy-start = (bf16[16,256,256]{2,1,0:T(8,128)(2,1)S(1)}, bf16[16,256,256]{2,1,0:T(8,128)(2,1)}, u32[]{:S(2)}) copy-start(bf16[16,256,256]{2,1,0:T(8,128)(2,1)} %param.6) | copy-start | bytes 6291460
  11.0 18.2 %all-to-all-start = ((bf16[8,4,4]{1,2,0:T(4,128)(2,1)}), bf16[8,4,4]{1,2,0:T(4,128)(2,1)S(1)}, u32[]{:S(2)}, u32[]{:S(2)}) async-start(bf16[8,4,4]{1,2,0:T(4,128)(2,1)} %copy.51), calls=%async_computation | async-start | bytes 16384 | tf_op jit(solution)/shard_map/all_to_all | solution.py:297
  29.2 53.8 %all-to-all-start.1 = ((bf16[8,4,2,128,128]{4,3,2,1,0:T(8,128)(2,1)}), bf16[8,4,2,128,128]{4,3,2,1,0:T(8,128)(2,1)}, u32[]{:S(2)}, u32[]{:S(2)}) async-start(bf16[8,4,2,128,128]{4,3,2,1,0:T(8,128)(2,1)} %bitcast.44), calls=%async_computation.1 | async-start | bytes 4194304 | tf_op jit(solution)/shard_map/all_to_all | solution.py:296
  35.2 97.0 %reduce-scatter.2.cloned.1.call-start = ((), (), s32[]{:S(2)}) async-start(), calls=%async_computation.4 | async-start | bytes 2359296 | tf_op jit(solution)/shard_map/reduce_scatter | solution.py:310
  40.3 7.8 %copy-start.1 = (s32[32,4]{0,1:T(4,128)}, s32[32,4]{0,1:T(4,128)S(1)}, u32[]{:S(2)}) copy-start(s32[32,4]{0,1:T(4,128)S(1)} %reshape.194) | copy-start | bytes 1540
  119.6 11.3 %all-to-all-start.2 = ((f32[8,4,3]{1,2,0:T(4,128)}), f32[8,4,3]{1,2,0:T(4,128)S(1)}, u32[]{:S(2)}, u32[]{:S(2)}) async-start(f32[8,4,3]{1,2,0:T(4,128)} %copy.59), calls=%async_computation.3 | async-start | bytes 32768 | tf_op jit(solution)/shard_map/all_to_all | solution.py:307
Sparse Core Ops, SparseCore 0:
  118.0 10.0 reduce-scatter.1

commit v2 on v1

--- a/solution.py
+++ b/solution.py
@@ -131,106 +131,116 @@
     return parts[0] + parts[1] + parts[2]
 
 
-def _slot_kernel(meta_ref, coef_ref, ref_ref, ctf_ref, pack_ref, total_ref, info_ref):
-    s = pl.program_id(0)
+def _one_slot(meta_ref, slot, coef_ref, ref_ref, ctf_ref, pack_ref, j, total_ref, info_ref):
     span = 8
-
-    @pl.when(s == 0)
+    per_owner = ref_ref.shape[0]
+    bins = ctf_ref.shape[0]
+    tag = meta_ref[0, slot]
+    cls = jnp.minimum(jnp.maximum(tag - 1, 0), per_owner - 1)
+    bin_id = jnp.minimum(jnp.maximum(meta_ref[1, slot], 0), bins - 1)
+    keep = (jnp.full((1, 128), tag, jnp.int32) > 0).astype(jnp.float32)
+    coef_re = coef_ref[0, 0].astype(jnp.float32)
+    coef_im = coef_ref[0, 1].astype(jnp.float32)
+    ctf = ctf_ref[bin_id]
+    pred_re = ctf * ref_ref[cls, 0].astype(jnp.float32)
+    pred_im = ctf * ref_ref[cls, 1].astype(jnp.float32)
+    prod_re = (coef_re * pred_re + coef_im * pred_im).astype(jnp.bfloat16)
+    prod_im = (coef_im * pred_re - coef_re * pred_im).astype(jnp.bfloat16)
+    rows = pack_ref[j, 0]
+    cols = pack_ref[j, 1]
+    cols_b = pack_ref[j, 2]
+    flat = pack_ref[j, 3]
+    both = jnp.concatenate([prod_re, prod_im], axis=1)
+    mix = jnp.concatenate([cols, cols_b], axis=0)
+    part = jnp.dot(both, mix, preferred_element_type=jnp.float32)
+    corr = _exact_dot(flat[0:16], part)
+    upper = corr[0:8]
+    lower = pltpu.roll(corr[8:16], 128 - span, 1)
+    lane = lax.broadcasted_iota(jnp.int32, (8, 128), 1)
+    sub = lax.broadcasted_iota(jnp.int32, (8, 128), 0)
+    inside = lane < span
+    score = jnp.where(inside, score_scale * (upper - lower), -jnp.inf)
+    peak = jnp.max(jnp.max(score, axis=1, keepdims=True), axis=0, keepdims=True)
+    total = jnp.sum(jnp.sum(jnp.exp(score - peak), axis=1, keepdims=True), axis=0, keepdims=True)
+    evidence = peak + jnp.log(total)
+    weight = jnp.where(inside, jnp.exp(score - evidence), 0.0)
+    row_shift = (jnp.full((8, 128), meta_ref[2, slot], jnp.int32) + sub - span // 2).astype(jnp.float32)
+    col_shift = (jnp.full((8, 128), meta_ref[3, slot], jnp.int32) + lane - span // 2).astype(jnp.float32)
+    by_row = jnp.sum(weight, axis=1, keepdims=True)
+    mean_row = jnp.sum(by_row * row_shift[:, 0:1], axis=0, keepdims=True)
+    by_col = jnp.sum(weight, axis=0, keepdims=True)
+    mean_col = jnp.sum(jnp.where(inside[0:1], by_col * col_shift[0:1], 0.0), axis=1, keepdims=True)
+    info_ref[j] = jnp.where(
+        sub == 0,
+        jnp.where(lane == 0, evidence, jnp.where(lane == 1, mean_row, jnp.where(lane == 2, mean_col, 0.0))),
+        0.0,
+    )
+    shifted = pltpu.roll(weight, span, 1)
+    stacked_w = jnp.concatenate([weight, shifted], axis=0)
+    pad = jnp.zeros((112, 128), jnp.bfloat16)
+    col_rows = jnp.concatenate([flat[16:32], pad], axis=0)
+    qpart = _exact_dot(stacked_w, col_rows)
+    q_re = qpart[0:8]
+    q_im = qpart[8:16]
+    zeros = jnp.zeros((112, 128), jnp.float32)
+    for_re = jnp.concatenate([q_re, -q_im, zeros], axis=0)
+    for_im = jnp.concatenate([q_im, q_re, zeros], axis=0)
+    back_re = _exact_dot(rows, for_re)
+    back_im = _exact_dot(rows, for_im)
+    term_re = ctf * (coef_re * back_re - coef_im * back_im)
+    term_im = ctf * (coef_re * back_im + coef_im * back_re)
+    total_ref[cls, 0] = total_ref[cls, 0] + term_re * keep
+    total_ref[cls, 1] = total_ref[cls, 1] + term_im * keep
+    total_ref[cls, 2] = total_ref[cls, 2] + ctf * ctf * keep
+
+
+def _group_kernel(meta_ref, *refs):
+    group = len(refs) - 5
+    coef_refs = refs[:group]
+    ref_ref, ctf_ref, pack_ref, total_ref, info_ref = refs[group:]
+    g = pl.program_id(0)
+
+    @pl.when(g == 0)
     def _():
         total_ref[...] = jnp.zeros(total_ref.shape, total_ref.dtype)
 
-    valid = meta_ref[0, s] > 0
     info_ref[...] = jnp.zeros(info_ref.shape, info_ref.dtype)
 
-    @pl.when(valid)
+    @pl.when(g * group < meta_ref[4, 0])
     def _():
-        cls = jnp.maximum(meta_ref[0, s] - 1, 0)
-        coef_re = coef_ref[0, 0].astype(jnp.float32)
-        coef_im = coef_ref[0, 1].astype(jnp.float32)
-        ctf = ctf_ref[0]
-        pred_re = ctf * ref_ref[0, 0].astype(jnp.float32)
-        pred_im = ctf * ref_ref[0, 1].astype(jnp.float32)
-        prod_re = (coef_re * pred_re + coef_im * pred_im).astype(jnp.bfloat16)
-        prod_im = (coef_im * pred_re - coef_re * pred_im).astype(jnp.bfloat16)
-        rows = pack_ref[0, 0]
-        cols = pack_ref[0, 1]
-        cols_b = pack_ref[0, 2]
-        flat = pack_ref[0, 3]
-        both = jnp.concatenate([prod_re, prod_im], axis=1)
-        mix = jnp.concatenate([cols, cols_b], axis=0)
-        part = jnp.dot(both, mix, preferred_element_type=jnp.float32)
-        corr = _exact_dot(flat[0:16], part)
-        upper = corr[0:8]
-        lower = pltpu.roll(corr[8:16], 128 - span, 1)
-        lane = lax.broadcasted_iota(jnp.int32, (8, 128), 1)
-        sub = lax.broadcasted_iota(jnp.int32, (8, 128), 0)
-        inside = lane < span
-        score = jnp.where(inside, score_scale * (upper - lower), -jnp.inf)
-        peak = jnp.max(jnp.max(score, axis=1, keepdims=True), axis=0, keepdims=True)
-        total = jnp.sum(jnp.sum(jnp.exp(score - peak), axis=1, keepdims=True), axis=0, keepdims=True)
-        evidence = peak + jnp.log(total)
-        weight = jnp.where(inside, jnp.exp(score - evidence), 0.0)
-        row_shift = (jnp.full((8, 128), meta_ref[2, s], jnp.int32) + sub - span // 2).astype(jnp.float32)
-        col_shift = (jnp.full((8, 128), meta_ref[3, s], jnp.int32) + lane - span // 2).astype(jnp.float32)
-        by_row = jnp.sum(weight, axis=1, keepdims=True)
-        mean_row = jnp.sum(by_row * row_shift[:, 0:1], axis=0, keepdims=True)
-        by_col = jnp.sum(weight, axis=0, keepdims=True)
-        mean_col = jnp.sum(jnp.where(inside[0:1], by_col * col_shift[0:1], 0.0), axis=1, keepdims=True)
-        info_ref[0] = jnp.where(
-            sub == 0,
-            jnp.where(lane == 0, evidence, jnp.where(lane == 1, mean_row, jnp.where(lane == 2, mean_col, 0.0))),
-            0.0,
-        )
-        shifted = pltpu.roll(weight, span, 1)
-        stacked_w = jnp.concatenate([weight, shifted], axis=0)
-        pad = jnp.zeros((112, 128), jnp.bfloat16)
-        col_rows = jnp.concatenate([flat[16:32], pad], axis=0)
-        qpart = _exact_dot(stacked_w, col_rows)
-        q_re = qpart[0:8]
-        q_im = qpart[8:16]
-        zeros = jnp.zeros((112, 128), jnp.float32)
-        for_re = jnp.concatenate([q_re, -q_im, zeros], axis=0)
-        for_im = jnp.concatenate([q_im, q_re, zeros], axis=0)
-        back_re = _exact_dot(rows, for_re)
-        back_im = _exact_dot(rows, for_im)
-        term_re = ctf * (coef_re * back_re - coef_im * back_im)
-        term_im = ctf * (coef_re * back_im + coef_im * back_re)
-        total_ref[cls, 0] = total_ref[cls, 0] + term_re
-        total_ref[cls, 1] = total_ref[cls, 1] + term_im
-        total_ref[cls, 2] = total_ref[cls, 2] + ctf * ctf
-
-
-def slot_eval(meta, coef, refs, ctf_tab, pack, interpret=False):
+        for j in range(group):
+            _one_slot(
+                meta_ref, g * group + j, coef_refs[j], ref_ref, ctf_ref, pack_ref, j,
+                total_ref, info_ref,
+            )
+
+
+def group_eval(meta, order, coef, refs, ctf_tab, pack, group, interpret=False):
     slots = coef.shape[0]
     per_owner = refs.shape[0]
     win = coef.shape[2]
     bins = ctf_tab.shape[0]
-
-    def coef_map(s, meta):
-        return (s, 0, 0, 0)
-
-    def ref_map(s, meta):
-        return (jnp.clip(meta[0, s] - 1, 0, per_owner - 1), 0, 0, 0)
-
-    def ctf_map(s, meta):
-        return (jnp.clip(meta[1, s], 0, bins - 1), 0, 0)
+    table = jnp.concatenate([meta, order[None]], axis=0)
+
+    def coef_map(j):
+        return lambda g, table: (table[5, g * group + j], 0, 0, 0)
 
     grid_spec = pltpu.PrefetchScalarGridSpec(
         num_scalar_prefetch=1,
-        grid=(slots,),
-        in_specs=[
-            pl.BlockSpec((1, 2, win, win), coef_map),
-            pl.BlockSpec((1, 2, win, win), ref_map),
-            pl.BlockSpec((1, win, win), ctf_map),
-            pl.BlockSpec((1, 4, win, win), coef_map),
+        grid=(slots // group,),
+        in_specs=[pl.BlockSpec((1, 2, win, win), coef_map(j)) for j in range(group)]
+        + [
+            pl.BlockSpec((per_owner, 2, win, win), lambda g, table: (0, 0, 0, 0)),
+            pl.BlockSpec((bins, win, win), lambda g, table: (0, 0, 0)),
+            pl.BlockSpec((group, 4, win, win), lambda g, table: (g, 0, 0, 0)),
         ],
         out_specs=[
-            pl.BlockSpec((per_owner, 3, win, win), lambda s, meta: (0, 0, 0, 0)),
-            pl.BlockSpec((1, 8, 128), lambda s, meta: (s, 0, 0)),
+            pl.BlockSpec((per_owner, 3, win, win), lambda g, table: (0, 0, 0, 0)),
+            pl.BlockSpec((group, 8, 128), lambda g, table: (g, 0, 0)),
         ],
     )
     return pl.pallas_call(
-        _slot_kernel,
+        _group_kernel,
         grid_spec=grid_spec,
         out_shape=[
             jax.ShapeDtypeStruct((per_owner, 3, win, win), jnp.float32),
@@ -238,7 +248,7 @@
         ],
         compiler_params=pltpu.CompilerParams(dimension_semantics=("arbitrary",)),
         interpret=interpret,
-    )(meta, coef, refs, ctf_tab, pack)
+    )(table, *([coef] * group), refs, ctf_tab, pack)
 
 
 def phase_rows(anchor, img_side, win_side):
@@ -296,16 +306,27 @@
     coeff_block = lax.all_to_all(buffer, "dom", split_axis=0, concat_axis=0, tiled=True)
     tag_block = lax.all_to_all(tag_buffer, "dom", split_axis=0, concat_axis=0, tiled=True)
     tag_flat = tag_block.reshape(slot_count, 4).astype(jnp.int32)
-    pack = phase_pack(tag_flat, img_side, win_side)
-    partial_value, info = slot_eval(
-        tag_flat.T,
+    live = (tag_flat[:, 0] > 0).astype(jnp.int32)
+    order = jnp.argsort(1 - live, stable=True).astype(jnp.int32)
+    tag_sorted = tag_flat[order]
+    count = jnp.sum(live)
+    meta = jnp.concatenate(
+        [tag_sorted.T, jnp.full((1, slot_count), count, jnp.int32)], axis=0
+    )
+    pack = phase_pack(tag_sorted, img_side, win_side)
+    group = 4 if slot_count % 4 == 0 else 1
+    partial_value, info_sorted = group_eval(
+        meta,
+        order,
         coeff_block.reshape(slot_count, 2, win_side, win_side),
         references,
         ctf_bins,
         pack,
-    )
+        group,
+    )
+    info = jnp.zeros((slot_count, 3), jnp.float32).at[order].set(info_sorted[:, 0, :3])
     returned = lax.all_to_all(
-        info[:, 0, :3].reshape(owners, capacity, 3), "dom", split_axis=0, concat_axis=0, tiled=True
+        info.reshape(owners, capacity, 3), "dom", split_axis=0, concat_axis=0, tiled=True
     )
     summed = lax.psum_scatter(partial_value, "cls", scatter_dimension=2, tiled=True)
     divisor = summed[:, 2] + ridge_term

time: 143 us -> 139 us (0.972); the launches traced: 142 us -> 140 us
  Pallas kernels: 34.9 us -> 14.5 us
  starting transfers between devices: 18.2 us -> 35.4 us
  waiting for transfers between devices: 33.6 us -> 29.1 us
  other arithmetic: 21.5 us -> 24.4 us
  local copies, waits for them, and re-layouts: 16.3 us -> 18.6 us
    pallas_call x1, Pallas kernels: 34.9 us -> 14.5 us  [group_eval(): pl.pallas_call(_group_kernel, grid_spec=grid_spec, out_shape=[jax.ShapeDt...]
    all_to_all x1, starting transfers between devices: 4.71 us -> 21.9 us  [on_device(): lax.all_to_all(info.reshape(owners, capacity, 3), 'dom', split_axis=0, co...]
    all_to_all x1, waiting for transfers between devices: 27 us -> 22.6 us  [on_device(): lax.all_to_all(buffer, 'dom', split_axis=0, concat_axis=0, tiled=True)]
    sort x0 -> x1, other arithmetic: none -> 1.61 us  [on_device(): order = jnp.argsort(1 - live, stable=True).astype(jnp.int32)]
  transfers between devices with their start and end apart: 4 -> 4, of which waited for: 2 -> 2; matrix products, arithmetic and copies ran while one was open for 24% -> 28% of each run, Pallas kernels for 0% -> 0%
where the time goes in v2:
time: 139 us; the launch traced here: 140 us
  starting transfers between devices  35.4 us (25%)
  waiting for transfers between devices  29.1 us (21%)
  other arithmetic  24.4 us (18%)
  local copies, waits for them, and re-layouts  18.6 us (13%)
  Pallas kernels  14.5 us (10%)
  between operations  14.2 us (10%)
  matrix products  3.22 us (2%)
    all_to_all x1, waiting for transfers between devices, on_device(): lax.all_to_all(buffer, 'dom', split_axis=0, concat_axis=0, tiled=True)  22.6 us
    all_to_all x1, starting transfers between devices, on_device(): lax.all_to_all(info.reshape(owners, capacity, 3), 'dom', split_axis=0, co...  21.9 us
    pallas_call x1, Pallas kernels, group_eval(): pl.pallas_call(_group_kernel, grid_spec=grid_spec, out_shape=[jax.ShapeDt...  14.5 us
    all_to_all x1, starting transfers between devices, on_device(): lax.all_to_all(tag_buffer, 'dom', split_axis=0, concat_axis=0, tiled=True)  7.28 us
    all_to_all x1, waiting for transfers between devices, on_device(): lax.all_to_all(info.reshape(owners, capacity, 3), 'dom', split_axis=0, co...  6.57 us
    all_to_all x1, starting transfers between devices, on_device(): lax.all_to_all(buffer, 'dom', split_axis=0, concat_axis=0, tiled=True)  5.99 us
    another operation x6, local copies, waits for them, and re-layouts, phase_pack(): return jnp.stack(planes + [flat], axis=1)  4.63 us
    neg x1, other arithmetic, ctf_table(): return -jnp.sin(strength[:, None, None] * radius[None, :, :] + 0.1)  4.49 us
  transfers between devices with their start and end apart: 4, of which 2 were waited for; matrix products, arithmetic and copies ran while one was open for 28% of the time, Pallas kernels for 0%

profile of v2, /device:TPU:0, one launch (start us, length us, event | category | flops | bytes accessed | tf_op | source)
XLA Modules:
  0.0 139.6 jit_solution(14951432627318013266)
XLA Ops:
  7.2 0.8 convert_bitcast_fusion.1
  8.2 0.7 convert.27
  8.9 0.7 convert_bitcast_fusion
  9.7 0.6 scatter_custom_fusion
  10.3 0.7 copy.65
  11.0 7.3 %all-to-all-start = ((bf16[8,4,4]{1,2,0:T(4,128)(2,1)}), bf16[8,4,4]{1,2,0:T(4,128)(2,1)S(1)}, u32[]{:S(2)}, u32[]{:S(2)}) async-start(bf16[8,4,4]{1,2,0:T(4,128)(2,1)} %copy.65), calls=%async_computation | async-start | bytes 16384 | tf_op jit(solution)/shard_map/all_to_all | solution.py:307
  18.3 0.6 multiply_convert_fusion.1
  18.9 0.2 rev.11
  19.2 0.2 rev.9
  19.4 0.4 rev.10
  19.9 0.7 and_compare_fusion.2
  20.6 0.8 fusion
  21.3 0.8 select_convert_fusion
  22.1 0.8 fusion.10
  23.0 0.8 fusion.16
  23.9 0.4 fusion.20
  24.5 1.9 %broadcast_in_dim.127 = bf16[32,2,128,128]{3,2,1,0:T(8,128)(2,1)} broadcast(bf16[]{:T(256)} %constant.35.clone.1), dimensions={} | broadcast | bytes 2097154 | tf_op jit(solution)/shard_map/broadcast_in_dim | solution.py:302
  26.3 3.0 %scatter_fusion = bf16[32,2,128,128]{3,2,1,0:T(8,128)(2,1)} fusion(bf16[32,2,128,128]{3,2,1,0:T(8,128)(2,1)} %broadcast_in_dim.127, s32[16]{0:T(128)S(1)} %compare_select_fusion.1, bf16[16,2,128,128]{3,2,1,0:T(8,128)(2,1)S(1)} %copy.70), kind=kCustom, calls=%fused_computation.3 | custom fusion | bytes 3145792 | tf_op jit(solution)/shard_map/scatter | solution.py:302
  29.3 6.0 %all-to-all-start.1 = ((bf16[8,4,2,128,128]{4,3,2,1,0:T(8,128)(2,1)}), bf16[8,4,2,128,128]{4,3,2,1,0:T(8,128)(2,1)}, u32[]{:S(2)}, u32[]{:S(2)}) async-start(bf16[8,4,2,128,128]{4,3,2,1,0:T(8,128)(2,1)} %bitcast.45), calls=%async_computation.1 | async-start | bytes 4194304 | tf_op jit(solution)/shard_map/all_to_all | solution.py:306
  35.5 4.5 %sine_negate_fusion.refs_5_ = f32[16,128,128]{2,1,0:T(8,128)} fusion(f32[128,128]{1,0:T(8,128)S(1)} %add_multiply_fusion, f32[16]{0:T(128)S(1)} %multiply_add_fusion), kind=kLoop, calls=%fused_computation.21 | loop fusion | flops 786432 | bytes 1114176 | tf_op jit(solution)/shard_map/neg | solution.py:51
  40.4 0.6 fusion.45
  41.1 1.6 %sort.17 = (s32[32]{0:T(128)}, s32[32]{0:T(128)S(1)}) sort(s32[32]{0:T(128)S(1)} %get-tuple-element.33, s32[32]{0:T(128)S(1)} %iota.72), dimensions={0}, to_apply=%region_2.3 | sort | flops 160 | bytes 512 | tf_op jit(solution)/shard_map/jit(argsort)/sort | solution.py:310
  42.7 0.6 gather_fusion
  43.6 1.2 constant_dynamic-update-slice_fusion.3
  44.8 1.2 constant_dynamic-update-slice_fusion.2
  46.0 1.2 constant_dynamic-update-slice_fusion.1
  47.3 1.2 fusion.44
  48.5 1.2 cosine_convert_fusion.1
  49.8 0.2 pad_bitcast_fusion.1
  50.0 1.3 copy.72
  51.6 1.3 copy.73
  52.9 0.2 pad_bitcast_fusion.2
  53.1 1.3 copy.71
  54.4 0.7 pad.28.clone
  55.2 1.0 broadcast_dynamic-update-slice_fusion
  56.2 0.7 pad_add_fusion.meta_ref
  56.9 3.7 %pad_maximum_fusion.refs_6_ = bf16[32,4,128,128]{3,2,1,0:T(8,128)(2,1)} fusion(bf16[32,1,128,128]{3,2,1,0:T(8,128)(2,1)} %bitcast.46, bf16[32,1,128,128]{3,2,1,0:T(8,128)(2,1)} %copy.73, bf16[32,1,128,128]{3,2,1,0:T(8,128)(2,1)} %copy.72, bf16[32,1,128,128]{3,2,1,0:T(8,128)(2,1)} %copy.71), kind=kLoop, calls=%fused_computation.5 | loop fusion | flops 6291456 | bytes 8388608 | tf_op jit(solution)/shard_map/stack | solution.py:273
  60.6 22.6 %all-to-all-done.1 = bf16[8,4,2,128,128]{4,3,2,1,0:T(8,128)(2,1)} async-done(((bf16[8,4,2,128,128]{4,3,2,1,0:T(8,128)(2,1)}), bf16[8,4,2,128,128]{4,3,2,1,0:T(8,128)(2,1)}, u32[]{:S(2)}, u32[]{:S(2)}) %all-to-all-start.1) | async-done | bytes 2097184 | tf_op jit(solution)/shard_map/all_to_all | solution.py:306
  83.1 14.5 %shard_map.77 = (f32[8,3,128,128]{3,2,1,0:T(8,128)}, f32[32,8,128]{2,1,0:T(8,128)}) custom-call(s32[6,32]{1,0:T(8,128)} %pad_add_fusion.meta_ref, bf16[32,2,128,128]{3,2,1,0:T(8,128)(2,1)} %bitcast.11.refs_0_.refs_1_.refs_2_.refs_3_, bf16[32,2,128,128]{3,2,1,0:T(8,128)(2,1)} %bitcast.11.refs_0_.refs_1_.refs_2_.refs_3_, ...), custom_call_target="tpu_custom_call" | custom-call | tf_op jit(solution)/shard_map/pallas_call | solution.py:242
  97.7 0.9 slice.55
  98.6 0.7 scatter_custom_fusion.2
  99.3 0.7 copy.77
  100.0 21.9 %all-to-all-start.2 = ((f32[8,4,3]{1,2,0:T(4,128)}), f32[8,4,3]{1,2,0:T(4,128)S(1)}, u32[]{:S(2)}, u32[]{:S(2)}) async-start(f32[8,4,3]{1,2,0:T(4,128)} %copy.77), calls=%async_computation.3 | async-start | bytes 32768 | tf_op jit(solution)/shard_map/all_to_all | solution.py:328
  121.9 6.6 %all-to-all-done.2 = f32[8,4,3]{1,2,0:T(4,128)S(1)} async-done(((f32[8,4,3]{1,2,0:T(4,128)}), f32[8,4,3]{1,2,0:T(4,128)S(1)}, u32[]{:S(2)}, u32[]{:S(2)}) %all-to-all-start.2) | async-done | bytes 416 | tf_op jit(solution)/shard_map/all_to_all | solution.py:328
  128.6 0.6 gather_fusion.1
  129.2 0.7 copy.80
  129.9 1.0 fusion.26
  130.8 1.9 %slice_divide_fusion = f32[8,2,64,128]{3,2,1,0:T(8,128)} fusion(f32[8,3,64,128]{3,2,1,0:T(8,128)} %reduce-scatter.2.cloned.1.call-done, f32[8,64,128]{2,1,0:T(8,128)S(1)} %fusion.26), kind=kLoop, calls=%fused_computation.34 | loop fusion | flops 131072 | bytes 1310720 | tf_op jit(solution)/shard_map/div | solution.py:333
  (34 shorter events, 2.0 us)
Async XLA Ops:
  7.2 13.4 %copy-start = (bf16[16,256,256]{2,1,0:T(8,128)(2,1)S(1)}, bf16[16,256,256]{2,1,0:T(8,128)(2,1)}, u32[]{:S(2)}) copy-start(bf16[16,256,256]{2,1,0:T(8,128)(2,1)} %param.6) | copy-start | bytes 6291460
  11.0 18.3 %all-to-all-start = ((bf16[8,4,4]{1,2,0:T(4,128)(2,1)}), bf16[8,4,4]{1,2,0:T(4,128)(2,1)S(1)}, u32[]{:S(2)}, u32[]{:S(2)}) async-start(bf16[8,4,4]{1,2,0:T(4,128)(2,1)} %copy.65), calls=%async_computation | async-start | bytes 16384 | tf_op jit(solution)/shard_map/all_to_all | solution.py:307
  29.3 53.8 %all-to-all-start.1 = ((bf16[8,4,2,128,128]{4,3,2,1,0:T(8,128)(2,1)}), bf16[8,4,2,128,128]{4,3,2,1,0:T(8,128)(2,1)}, u32[]{:S(2)}, u32[]{:S(2)}) async-start(bf16[8,4,2,128,128]{4,3,2,1,0:T(8,128)(2,1)} %bitcast.45), calls=%async_computation.1 | async-start | bytes 4194304 | tf_op jit(solution)/shard_map/all_to_all | solution.py:306
  35.3 94.5 %reduce-scatter.2.cloned.1.call-start = ((), (), s32[]{:S(2)}) async-start(), calls=%async_computation.4 | async-start | bytes 2359296 | tf_op jit(solution)/shard_map/reduce_scatter | solution.py:331
  100.0 28.5 %all-to-all-start.2 = ((f32[8,4,3]{1,2,0:T(4,128)}), f32[8,4,3]{1,2,0:T(4,128)S(1)}, u32[]{:S(2)}, u32[]{:S(2)}) async-start(f32[8,4,3]{1,2,0:T(4,128)} %copy.77), calls=%async_computation.3 | async-start | bytes 32768 | tf_op jit(solution)/shard_map/all_to_all | solution.py:328
Sparse Core Ops, SparseCore 0:
  97.8 25.3 reduce-scatter.1

commit v3 on v2

--- a/solution.py
+++ b/solution.py
@@ -131,74 +131,14 @@
     return parts[0] + parts[1] + parts[2]
 
 
-def _one_slot(meta_ref, slot, coef_ref, ref_ref, ctf_ref, pack_ref, j, total_ref, info_ref):
-    span = 8
-    per_owner = ref_ref.shape[0]
-    bins = ctf_ref.shape[0]
-    tag = meta_ref[0, slot]
-    cls = jnp.minimum(jnp.maximum(tag - 1, 0), per_owner - 1)
-    bin_id = jnp.minimum(jnp.maximum(meta_ref[1, slot], 0), bins - 1)
-    keep = (jnp.full((1, 128), tag, jnp.int32) > 0).astype(jnp.float32)
-    coef_re = coef_ref[0, 0].astype(jnp.float32)
-    coef_im = coef_ref[0, 1].astype(jnp.float32)
-    ctf = ctf_ref[bin_id]
-    pred_re = ctf * ref_ref[cls, 0].astype(jnp.float32)
-    pred_im = ctf * ref_ref[cls, 1].astype(jnp.float32)
-    prod_re = (coef_re * pred_re + coef_im * pred_im).astype(jnp.bfloat16)
-    prod_im = (coef_im * pred_re - coef_re * pred_im).astype(jnp.bfloat16)
-    rows = pack_ref[j, 0]
-    cols = pack_ref[j, 1]
-    cols_b = pack_ref[j, 2]
-    flat = pack_ref[j, 3]
-    both = jnp.concatenate([prod_re, prod_im], axis=1)
-    mix = jnp.concatenate([cols, cols_b], axis=0)
-    part = jnp.dot(both, mix, preferred_element_type=jnp.float32)
-    corr = _exact_dot(flat[0:16], part)
-    upper = corr[0:8]
-    lower = pltpu.roll(corr[8:16], 128 - span, 1)
-    lane = lax.broadcasted_iota(jnp.int32, (8, 128), 1)
-    sub = lax.broadcasted_iota(jnp.int32, (8, 128), 0)
-    inside = lane < span
-    score = jnp.where(inside, score_scale * (upper - lower), -jnp.inf)
-    peak = jnp.max(jnp.max(score, axis=1, keepdims=True), axis=0, keepdims=True)
-    total = jnp.sum(jnp.sum(jnp.exp(score - peak), axis=1, keepdims=True), axis=0, keepdims=True)
-    evidence = peak + jnp.log(total)
-    weight = jnp.where(inside, jnp.exp(score - evidence), 0.0)
-    row_shift = (jnp.full((8, 128), meta_ref[2, slot], jnp.int32) + sub - span // 2).astype(jnp.float32)
-    col_shift = (jnp.full((8, 128), meta_ref[3, slot], jnp.int32) + lane - span // 2).astype(jnp.float32)
-    by_row = jnp.sum(weight, axis=1, keepdims=True)
-    mean_row = jnp.sum(by_row * row_shift[:, 0:1], axis=0, keepdims=True)
-    by_col = jnp.sum(weight, axis=0, keepdims=True)
-    mean_col = jnp.sum(jnp.where(inside[0:1], by_col * col_shift[0:1], 0.0), axis=1, keepdims=True)
-    info_ref[j] = jnp.where(
-        sub == 0,
-        jnp.where(lane == 0, evidence, jnp.where(lane == 1, mean_row, jnp.where(lane == 2, mean_col, 0.0))),
-        0.0,
-    )
-    shifted = pltpu.roll(weight, span, 1)
-    stacked_w = jnp.concatenate([weight, shifted], axis=0)
-    pad = jnp.zeros((112, 128), jnp.bfloat16)
-    col_rows = jnp.concatenate([flat[16:32], pad], axis=0)
-    qpart = _exact_dot(stacked_w, col_rows)
-    q_re = qpart[0:8]
-    q_im = qpart[8:16]
-    zeros = jnp.zeros((112, 128), jnp.float32)
-    for_re = jnp.concatenate([q_re, -q_im, zeros], axis=0)
-    for_im = jnp.concatenate([q_im, q_re, zeros], axis=0)
-    back_re = _exact_dot(rows, for_re)
-    back_im = _exact_dot(rows, for_im)
-    term_re = ctf * (coef_re * back_re - coef_im * back_im)
-    term_im = ctf * (coef_re * back_im + coef_im * back_re)
-    total_ref[cls, 0] = total_ref[cls, 0] + term_re * keep
-    total_ref[cls, 1] = total_ref[cls, 1] + term_im * keep
-    total_ref[cls, 2] = total_ref[cls, 2] + ctf * ctf * keep
-
-
 def _group_kernel(meta_ref, *refs):
     group = len(refs) - 5
     coef_refs = refs[:group]
     ref_ref, ctf_ref, pack_ref, total_ref, info_ref = refs[group:]
     g = pl.program_id(0)
+    span = 8
+    per_owner = ref_ref.shape[0]
+    bins = ctf_ref.shape[0]
 
     @pl.when(g == 0)
     def _():
@@ -208,11 +148,79 @@
 
     @pl.when(g * group < meta_ref[4, 0])
     def _():
+        lane = lax.broadcasted_iota(jnp.int32, (8, 128), 1)
+        sub = lax.broadcasted_iota(jnp.int32, (8, 128), 0)
+        inside = lane < span
+        st = []
         for j in range(group):
-            _one_slot(
-                meta_ref, g * group + j, coef_refs[j], ref_ref, ctf_ref, pack_ref, j,
-                total_ref, info_ref,
+            slot = g * group + j
+            tag = meta_ref[0, slot]
+            cls = jnp.minimum(jnp.maximum(tag - 1, 0), per_owner - 1)
+            bin_id = jnp.minimum(jnp.maximum(meta_ref[1, slot], 0), bins - 1)
+            keep = (jnp.full((1, 128), tag, jnp.int32) > 0).astype(jnp.float32)
+            coef_re = coef_refs[j][0, 0].astype(jnp.float32)
+            coef_im = coef_refs[j][0, 1].astype(jnp.float32)
+            ctf = ctf_ref[bin_id]
+            pred_re = ctf * ref_ref[cls, 0].astype(jnp.float32)
+            pred_im = ctf * ref_ref[cls, 1].astype(jnp.float32)
+            prod_re = (coef_re * pred_re + coef_im * pred_im).astype(jnp.bfloat16)
+            prod_im = (coef_im * pred_re - coef_re * pred_im).astype(jnp.bfloat16)
+            both = jnp.concatenate([prod_re, prod_im], axis=1)
+            mix = jnp.concatenate([pack_ref[j, 1], pack_ref[j, 2]], axis=0)
+            part = jnp.dot(both, mix, preferred_element_type=jnp.float32)
+            st.append(dict(slot=slot, cls=cls, keep=keep, ctf=ctf, coef_re=coef_re, coef_im=coef_im, part=part))
+        for j, d in enumerate(st):
+            p_hi, p_mid, p_lo = [piece.astype(jnp.float32) for piece in _split3(d["part"])]
+            packed = (p_hi + pltpu.roll(p_mid, 2 * span, 1) + pltpu.roll(p_lo, 4 * span, 1)).astype(jnp.bfloat16)
+            d["corr3"] = jnp.dot(pack_ref[j, 3][0:16], packed, preferred_element_type=jnp.float32)
+        for j, d in enumerate(st):
+            corr3 = d["corr3"]
+            corr = (corr3 + pltpu.roll(corr3, 128 - 2 * span, 1)) + pltpu.roll(corr3, 128 - 4 * span, 1)
+            upper = corr[0:8]
+            lower = pltpu.roll(corr[8:16], 128 - span, 1)
+            score = jnp.where(inside, score_scale * (upper - lower), -jnp.inf)
+            peak = jnp.max(jnp.max(score, axis=1, keepdims=True), axis=0, keepdims=True)
+            total = jnp.sum(jnp.sum(jnp.exp(score - peak), axis=1, keepdims=True), axis=0, keepdims=True)
+            evidence = peak + jnp.log(total)
+            weight = jnp.where(inside, jnp.exp(score - evidence), 0.0)
+            slot = d["slot"]
+            row_shift = (jnp.full((8, 128), meta_ref[2, slot], jnp.int32) + sub - span // 2).astype(jnp.float32)
+            col_shift = (jnp.full((8, 128), meta_ref[3, slot], jnp.int32) + lane - span // 2).astype(jnp.float32)
+            by_row = jnp.sum(weight, axis=1, keepdims=True)
+            mean_row = jnp.sum(by_row * row_shift[:, 0:1], axis=0, keepdims=True)
+            by_col = jnp.sum(weight, axis=0, keepdims=True)
+            mean_col = jnp.sum(jnp.where(inside[0:1], by_col * col_shift[0:1], 0.0), axis=1, keepdims=True)
+            info_ref[j] = jnp.where(
+                sub == 0,
+                jnp.where(lane == 0, evidence, jnp.where(lane == 1, mean_row, jnp.where(lane == 2, mean_col, 0.0))),
+                0.0,
             )
+            shifted = pltpu.roll(weight, span, 1)
+            stacked_w = jnp.concatenate([weight, shifted], axis=0)
+            pad = jnp.zeros((112, 128), jnp.bfloat16)
+            col_rows = jnp.concatenate([pack_ref[j, 3][16:32], pad], axis=0)
+            w_pieces = jnp.concatenate(_split3(stacked_w), axis=0)
+            d["q3"] = jnp.dot(w_pieces, col_rows, preferred_element_type=jnp.float32)
+        for j, d in enumerate(st):
+            q3 = d["q3"]
+            qpart = (q3[0:16] + q3[16:32]) + q3[32:48]
+            q_re = qpart[0:8]
+            q_im = qpart[8:16]
+            spare = jnp.zeros((80, 128), jnp.bfloat16)
+            rhs_re = jnp.concatenate(list(_split3(jnp.concatenate([q_re, -q_im], axis=0))) + [spare], axis=0)
+            rhs_im = jnp.concatenate(list(_split3(jnp.concatenate([q_im, q_re], axis=0))) + [spare], axis=0)
+            d["back"] = jnp.dot(
+                pack_ref[j, 0], jnp.concatenate([rhs_re, rhs_im], axis=1), preferred_element_type=jnp.float32
+            )
+        for d in st:
+            back_re = d["back"][:, 0:128]
+            back_im = d["back"][:, 128:256]
+            ctf, coef_re, coef_im, keep, cls = d["ctf"], d["coef_re"], d["coef_im"], d["keep"], d["cls"]
+            term_re = ctf * (coef_re * back_re - coef_im * back_im)
+            term_im = ctf * (coef_re * back_im + coef_im * back_re)
+            total_ref[cls, 0] = total_ref[cls, 0] + term_re * keep
+            total_ref[cls, 1] = total_ref[cls, 1] + term_im * keep
+            total_ref[cls, 2] = total_ref[cls, 2] + ctf * ctf * keep
 
 
 def group_eval(meta, order, coef, refs, ctf_tab, pack, group, interpret=False):
@@ -266,9 +274,10 @@
     cols_bt = jnp.concatenate([-cols_t[:, TW:], cols_t[:, :TW]], axis=1)
     spare = jnp.zeros((rows_t.shape[0], win_side - 4 * TW, win_side), jnp.bfloat16)
     flat = jnp.concatenate([rows_t, cols_t, spare], axis=1)
+    rows3 = jnp.concatenate([rows_t, rows_t, rows_t], axis=1)
     planes = [
-        jnp.pad(jnp.swapaxes(t, 1, 2), ((0, 0), (0, 0), (0, win_side - 2 * TW)))
-        for t in (rows_t, cols_t, cols_bt)
+        jnp.pad(jnp.swapaxes(t, 1, 2), ((0, 0), (0, 0), (0, win_side - t.shape[1])))
+        for t in (rows3, cols_t, cols_bt)
     ]
     return jnp.stack(planes + [flat], axis=1)
 

time: 139 us -> 126 us (0.906)
  starting transfers between devices: 35.4 us -> 17.1 us
  other arithmetic: 24.4 us -> 27 us
  local copies, waits for them, and re-layouts: 18.6 us -> 20 us
    all_to_all x1, starting transfers between devices: 21.9 us -> 3.64 us  [on_device(): lax.all_to_all(info.reshape(owners, capacity, 3), 'dom', split_axis=0, co...]
    unnamed x3 -> x6, other arithmetic: 3.66 us -> 4.92 us
  transfers between devices with their start and end apart: 4 -> 4, of which waited for: 2 -> 2; matrix products, arithmetic and copies ran while one was open for 28% -> 34% of each run, Pallas kernels for 0% -> 0%
where the time goes in v3:
time: 126 us; the launch traced here: 125 us
  waiting for transfers between devices  29.8 us (24%)
  other arithmetic  27 us (21%)
  local copies, waits for them, and re-layouts  20 us (16%)
  starting transfers between devices  17.1 us (14%)
  between operations  14.2 us (11%)
  Pallas kernels  14 us (11%)
  matrix products  3.22 us (3%)
    all_to_all x1, waiting for transfers between devices, on_device(): lax.all_to_all(buffer, 'dom', split_axis=0, concat_axis=0, tiled=True)  23.2 us
    pallas_call x1, Pallas kernels, group_eval(): pl.pallas_call(_group_kernel, grid_spec=grid_spec, out_shape=[jax.ShapeDt...  14 us
    all_to_all x1, starting transfers between devices, on_device(): lax.all_to_all(tag_buffer, 'dom', split_axis=0, concat_axis=0, tiled=True)  7.28 us
    all_to_all x1, waiting for transfers between devices, on_device(): lax.all_to_all(info.reshape(owners, capacity, 3), 'dom', split_axis=0, co...  6.57 us
    all_to_all x1, starting transfers between devices, on_device(): lax.all_to_all(buffer, 'dom', split_axis=0, concat_axis=0, tiled=True)  6 us
    another operation x6, local copies, waits for them, and re-layouts, phase_pack(): return jnp.stack(planes + [flat], axis=1)  5.49 us
    unnamed x6, other arithmetic  4.92 us
    neg x1, other arithmetic, ctf_table(): return -jnp.sin(strength[:, None, None] * radius[None, :, :] + 0.1)  4.49 us
  transfers between devices with their start and end apart: 4, of which 2 were waited for; matrix products, arithmetic and copies ran while one was open for 34% of the time, Pallas kernels for 0%

profile of v3, /device:TPU:0, one launch (start us, length us, event | category | flops | bytes accessed | tf_op | source)
XLA Modules:
  0.0 125.3 jit_solution(4843323787815972795)
XLA Ops:
  7.2 0.8 convert_bitcast_fusion.1
  8.2 0.7 convert.27
  8.9 0.7 convert_bitcast_fusion
  9.7 0.6 scatter_custom_fusion
  10.3 0.7 copy.65
  11.0 7.3 %all-to-all-start = ((bf16[8,4,4]{1,2,0:T(4,128)(2,1)}), bf16[8,4,4]{1,2,0:T(4,128)(2,1)S(1)}, u32[]{:S(2)}, u32[]{:S(2)}) async-start(bf16[8,4,4]{1,2,0:T(4,128)(2,1)} %copy.65), calls=%async_computation | async-start | bytes 16384 | tf_op jit(solution)/shard_map/all_to_all | solution.py:316
  18.3 0.6 multiply_convert_fusion.1
  19.9 0.7 and_compare_fusion.2
  20.6 0.8 fusion
  21.3 0.8 select_convert_fusion
  22.1 0.8 fusion.10
  23.0 0.8 fusion.16
  24.3 4.5 %sine_negate_fusion.refs_5_ = f32[16,128,128]{2,1,0:T(8,128)} fusion(f32[128,128]{1,0:T(8,128)S(1)} %add_multiply_fusion, f32[16]{0:T(128)S(1)} %multiply_add_fusion), kind=kLoop, calls=%fused_computation.21 | loop fusion | flops 786432 | bytes 1114176 | tf_op jit(solution)/shard_map/neg | solution.py:51
  29.0 1.9 %broadcast_in_dim.127 = bf16[32,2,128,128]{3,2,1,0:T(8,128)(2,1)} broadcast(bf16[]{:T(256)} %constant.35.clone.1), dimensions={} | broadcast | bytes 2097154 | tf_op jit(solution)/shard_map/broadcast_in_dim | solution.py:311
  30.8 3.0 %scatter_fusion = bf16[32,2,128,128]{3,2,1,0:T(8,128)(2,1)} fusion(bf16[32,2,128,128]{3,2,1,0:T(8,128)(2,1)} %broadcast_in_dim.127, s32[16]{0:T(128)S(1)} %compare_select_fusion.1, bf16[16,2,128,128]{3,2,1,0:T(8,128)(2,1)S(1)} %copy.70), kind=kCustom, calls=%fused_computation.3 | custom fusion | bytes 3145792 | tf_op jit(solution)/shard_map/scatter | solution.py:311
  33.8 6.0 %all-to-all-start.1 = ((bf16[8,4,2,128,128]{4,3,2,1,0:T(8,128)(2,1)}), bf16[8,4,2,128,128]{4,3,2,1,0:T(8,128)(2,1)}, u32[]{:S(2)}, u32[]{:S(2)}) async-start(bf16[8,4,2,128,128]{4,3,2,1,0:T(8,128)(2,1)} %bitcast.44), calls=%async_computation.1 | async-start | bytes 4194304 | tf_op jit(solution)/shard_map/all_to_all | solution.py:315
  40.3 0.6 fusion.53
  41.0 1.6 %sort.17 = (s32[32]{0:T(128)}, s32[32]{0:T(128)S(1)}) sort(s32[32]{0:T(128)S(1)} %get-tuple-element.35, s32[32]{0:T(128)S(1)} %iota.72), dimensions={0}, to_apply=%region_2.3 | sort | flops 160 | bytes 512 | tf_op jit(solution)/shard_map/jit(argsort)/sort | solution.py:319
  43.1 0.6 gather_fusion
  44.0 0.6 fusion.40
  44.6 0.6 fusion.44
  45.2 0.6 fusion.39
  45.8 0.6 fusion.43
  46.4 1.3 %fusion.42 = (bf16[32,48,128]{2,1,0:T(8,128)(2,1)S(1)}, bf16[32,128,128]{2,1,0:T(8,128)(2,1)}) fusion(bf16[32,48,128]{2,1,0:T(8,128)(2,1)S(1)} %fusion.43, s32[128]{0:T(128)S(1)} %iota_add_fusion, s32[32,8]{1,0:T(8,128)S(1)} %get-tuple-element.44), kind=kLoop, calls=%fused_computation.79 | loop fusion | flops 491519 | bytes 147968
  47.7 1.3 %fusion.46 = (bf16[32,48,128]{2,1,0:T(8,128)(2,1)S(1)}, bf16[32,128,128]{2,1,0:T(8,128)(2,1)}) fusion(bf16[32,48,128]{2,1,0:T(8,128)(2,1)S(1)} %get-tuple-element.28, s32[128]{0:T(128)S(1)} %iota_add_fusion, s32[32,8]{1,0:T(8,128)S(1)} %get-tuple-element.44, bf16[32,128,128]{2,1,0:T(8,128)(2,1)} %get-tuple-element.29), kind=kLoop, calls=%fused_computation.83 | loop fusion | flops 491520 | bytes 147968 | tf_op jit(solution)/shard_map/concatenate | solution.py:277
  48.9 1.2 constant_dynamic-update-slice_fusion.1
  50.2 0.6 sine_convert_fusion
  50.8 1.2 fusion.52
  52.0 0.7 maximum_bitcast_fusion
  52.9 1.3 %copy.72 = bf16[32,1,128,128]{3,2,1,0:T(8,128)(2,1)} copy(bf16[32,1,128,128]{2,3,0,1:T(8,128)(2,1)S(1)} %pad_bitcast_fusion.1) | data formatting | bytes 2097152 | tf_op jit(solution)/shard_map/stack | solution.py:282
  54.3 1.1 pad_bitcast_fusion
  55.4 1.3 %copy.73 = bf16[32,1,128,128]{3,2,1,0:T(8,128)(2,1)} copy(bf16[32,1,128,128]{2,3,0,1:T(8,128)(2,1)S(1)} %pad_bitcast_fusion) | data formatting | bytes 2097152 | tf_op jit(solution)/shard_map/stack | solution.py:282
  56.9 1.3 %copy.71 = bf16[32,1,128,128]{3,2,1,0:T(8,128)(2,1)} copy(bf16[32,1,128,128]{2,3,0,1:T(8,128)(2,1)S(1)} %pad_bitcast_fusion.2) | data formatting | bytes 2097152 | tf_op jit(solution)/shard_map/stack | solution.py:282
  58.2 0.7 pad.27.clone
  58.9 1.0 broadcast_dynamic-update-slice_fusion
  60.0 0.7 pad_add_fusion.meta_ref
  60.6 3.7 %pad_maximum_fusion.refs_6_ = bf16[32,4,128,128]{3,2,1,0:T(8,128)(2,1)} fusion(bf16[32,1,128,128]{3,2,1,0:T(8,128)(2,1)} %bitcast.45, bf16[32,1,128,128]{3,2,1,0:T(8,128)(2,1)} %copy.73, bf16[32,1,128,128]{3,2,1,0:T(8,128)(2,1)} %copy.72, bf16[32,1,128,128]{3,2,1,0:T(8,128)(2,1)} %copy.71), kind=kLoop, calls=%fused_computation.5 | loop fusion | flops 6291456 | bytes 8388608 | tf_op jit(solution)/shard_map/stack | solution.py:282
  64.3 23.2 %all-to-all-done.1 = bf16[8,4,2,128,128]{4,3,2,1,0:T(8,128)(2,1)} async-done(((bf16[8,4,2,128,128]{4,3,2,1,0:T(8,128)(2,1)}), bf16[8,4,2,128,128]{4,3,2,1,0:T(8,128)(2,1)}, u32[]{:S(2)}, u32[]{:S(2)}) %all-to-all-start.1) | async-done | bytes 2097184 | tf_op jit(solution)/shard_map/all_to_all | solution.py:315
  87.6 14.0 %shard_map.77 = (f32[8,3,128,128]{3,2,1,0:T(8,128)}, f32[32,8,128]{2,1,0:T(8,128)}) custom-call(s32[6,32]{1,0:T(8,128)} %pad_add_fusion.meta_ref, bf16[32,2,128,128]{3,2,1,0:T(8,128)(2,1)} %bitcast.11.refs_0_.refs_1_.refs_2_.refs_3_, bf16[32,2,128,128]{3,2,1,0:T(8,128)(2,1)} %bitcast.11.refs_0_.refs_1_.refs_2_.refs_3_, ...), custom_call_target="tpu_custom_call" | custom-call | tf_op jit(solution)/shard_map/pallas_call | solution.py:250
  101.6 0.9 slice.55
  102.5 0.8 scatter_custom_fusion.2
  103.3 0.7 copy.77
  104.1 3.6 %all-to-all-start.2 = ((f32[8,4,3]{1,2,0:T(4,128)}), f32[8,4,3]{1,2,0:T(4,128)S(1)}, u32[]{:S(2)}, u32[]{:S(2)}) async-start(f32[8,4,3]{1,2,0:T(4,128)} %copy.77), calls=%async_computation.3 | async-start | bytes 32768 | tf_op jit(solution)/shard_map/all_to_all | solution.py:337
  107.7 6.6 %all-to-all-done.2 = f32[8,4,3]{1,2,0:T(4,128)S(1)} async-done(((f32[8,4,3]{1,2,0:T(4,128)}), f32[8,4,3]{1,2,0:T(4,128)S(1)}, u32[]{:S(2)}, u32[]{:S(2)}) %all-to-all-start.2) | async-done | bytes 416 | tf_op jit(solution)/shard_map/all_to_all | solution.py:337
  114.4 0.6 gather_fusion.1
  115.0 0.7 copy.80
  115.6 1.0 fusion.26
  116.6 1.9 %slice_divide_fusion = f32[8,2,64,128]{3,2,1,0:T(8,128)} fusion(f32[8,3,64,128]{3,2,1,0:T(8,128)} %reduce-scatter.2.cloned.1.call-done, f32[8,64,128]{2,1,0:T(8,128)S(1)} %fusion.26), kind=kLoop, calls=%fused_computation.34 | loop fusion | flops 131072 | bytes 1310720 | tf_op jit(solution)/shard_map/div | solution.py:342
  (39 shorter events, 3.8 us)
Async XLA Ops:
  7.2 13.4 %copy-start = (bf16[16,256,256]{2,1,0:T(8,128)(2,1)S(1)}, bf16[16,256,256]{2,1,0:T(8,128)(2,1)}, u32[]{:S(2)}) copy-start(bf16[16,256,256]{2,1,0:T(8,128)(2,1)} %param.6) | copy-start | bytes 6291460
  11.0 22.8 %all-to-all-start = ((bf16[8,4,4]{1,2,0:T(4,128)(2,1)}), bf16[8,4,4]{1,2,0:T(4,128)(2,1)S(1)}, u32[]{:S(2)}, u32[]{:S(2)}) async-start(bf16[8,4,4]{1,2,0:T(4,128)(2,1)} %copy.65), calls=%async_computation | async-start | bytes 16384 | tf_op jit(solution)/shard_map/all_to_all | solution.py:316
  33.8 53.8 %all-to-all-start.1 = ((bf16[8,4,2,128,128]{4,3,2,1,0:T(8,128)(2,1)}), bf16[8,4,2,128,128]{4,3,2,1,0:T(8,128)(2,1)}, u32[]{:S(2)}, u32[]{:S(2)}) async-start(bf16[8,4,2,128,128]{4,3,2,1,0:T(8,128)(2,1)} %bitcast.44), calls=%async_computation.1 | async-start | bytes 4194304 | tf_op jit(solution)/shard_map/all_to_all | solution.py:315
  39.8 75.8 %reduce-scatter.2.cloned.1.call-start = ((), (), s32[]{:S(2)}) async-start(), calls=%async_computation.4 | async-start | bytes 2359296 | tf_op jit(solution)/shard_map/reduce_scatter | solution.py:340
  42.6 0.5 copy-start.1
  104.1 10.2 %all-to-all-start.2 = ((f32[8,4,3]{1,2,0:T(4,128)}), f32[8,4,3]{1,2,0:T(4,128)S(1)}, u32[]{:S(2)}, u32[]{:S(2)}) async-start(f32[8,4,3]{1,2,0:T(4,128)} %copy.77), calls=%async_computation.3 | async-start | bytes 32768 | tf_op jit(solution)/shard_map/all_to_all | solution.py:337
Sparse Core Ops, SparseCore 0:
  101.7 8.0 reduce-scatter.1

commit v4 on v3

--- a/solution.py
+++ b/solution.py
@@ -7,12 +7,12 @@
 from jax.experimental.pallas import tpu as pltpu
 from jax.sharding import PartitionSpec as P
 
+
 TW = 8
 
 
 score_scale = 0.02
 ridge_term = 1.0
-highest = lax.Precision.HIGHEST
 
 
 def freq_ids(win_side):
@@ -31,17 +31,6 @@
     )
 
 
-def shift_tables(anchor, img_side, win_side, span_len):
-    shifts = anchor[:, None] + jnp.arange(span_len, dtype=jnp.int32)[None, :] - span_len // 2
-    phase_int = freq_ids(win_side)[None, :, None] * shifts[:, None, :] % img_side
-    angles = phase_int.astype(jnp.float32) * (2.0 * math.pi / img_side)
-    return (
-        jnp.cos(angles).astype(jnp.bfloat16),
-        jnp.sin(angles).astype(jnp.bfloat16),
-        shifts.astype(jnp.float32),
-    )
-
-
 def ctf_table(bin_ids, win_side):
     freqs = freq_ids(win_side).astype(jnp.float32)
     radius = (freqs[:, None] * freqs[:, None] + freqs[None, :] * freqs[None, :]) / float(
@@ -49,13 +38,6 @@
     )
     strength = 20.0 + 6.0 * bin_ids.astype(jnp.float32)
     return -jnp.sin(strength[:, None, None] * radius[None, :, :] + 0.1)
-
-
-def rotate_grid(stack_in, rot_ids):
-    flag_bits = rot_ids[:, None, None]
-    result = jnp.where(flag_bits & 4 != 0, jnp.swapaxes(stack_in, 1, 2), stack_in)
-    result = jnp.where(flag_bits & 1 != 0, result[:, ::-1, :], result)
-    return jnp.where(flag_bits & 2 != 0, result[:, :, ::-1], result)
 
 
 def transform(images, rot_ids, dft_cos, dft_sin):
@@ -75,60 +57,12 @@
     return jnp.stack([real_part, imag_part], axis=1).astype(jnp.bfloat16)
 
 
-def evaluate(fourier, chosen, ctf_map, row_cos, row_sin, col_cos, col_sin, row_shift, col_shift):
-    span_len = col_cos.shape[2]
-    coef_re = fourier[:, 0].astype(jnp.float32)
-    coef_im = fourier[:, 1].astype(jnp.float32)
-    pred_re = ctf_map * chosen[:, 0].astype(jnp.float32)
-    pred_im = ctf_map * chosen[:, 1].astype(jnp.float32)
-    prod_re = (coef_re * pred_re + coef_im * pred_im).astype(jnp.bfloat16)
-    prod_im = (coef_im * pred_re - coef_re * pred_im).astype(jnp.bfloat16)
-    shift_col = jnp.concatenate([col_cos, col_sin], axis=2)
-    from_real = jnp.einsum("nuv,nvb->nub", prod_re, shift_col, preferred_element_type=jnp.float32)
-    from_imag = jnp.einsum("nuv,nvb->nub", prod_im, shift_col, preferred_element_type=jnp.float32)
-    part_re = from_real[..., :span_len] - from_imag[..., span_len:]
-    part_im = from_real[..., span_len:] + from_imag[..., :span_len]
-    cos_rows = row_cos.astype(jnp.float32)
-    sin_rows = row_sin.astype(jnp.float32)
-    cos_cols = col_cos.astype(jnp.float32)
-    sin_cols = col_sin.astype(jnp.float32)
-    correl = jnp.einsum("nua,nub->nab", cos_rows, part_re, precision=highest) - jnp.einsum(
-        "nua,nub->nab", sin_rows, part_im, precision=highest
-    )
-    score = score_scale * correl.reshape(fourier.shape[0], span_len * span_len)
-    peak = jnp.max(score, axis=1, keepdims=True)
-    evidence = peak[:, 0] + jnp.log(jnp.sum(jnp.exp(score - peak), axis=1))
-    weight = jnp.exp(score - evidence[:, None]).reshape(fourier.shape[0], span_len, span_len)
-    mean_row = jnp.sum(jnp.sum(weight, axis=2) * row_shift, axis=1)
-    mean_col = jnp.sum(jnp.sum(weight, axis=1) * col_shift, axis=1)
-    qpart_re = jnp.einsum("nab,nvb->nav", weight, cos_cols, precision=highest)
-    qpart_im = jnp.einsum("nab,nvb->nav", weight, sin_cols, precision=highest)
-    rows_both = jnp.concatenate([cos_rows, sin_rows], axis=2)
-    for_real = jnp.concatenate([qpart_re, -qpart_im], axis=1)
-    for_imag = jnp.concatenate([qpart_im, qpart_re], axis=1)
-    back_re = jnp.einsum("nua,nav->nuv", rows_both, for_real, precision=highest)
-    back_im = jnp.einsum("nua,nav->nuv", rows_both, for_imag, precision=highest)
-    term_re = ctf_map * (coef_re * back_re - coef_im * back_im)
-    term_im = ctf_map * (coef_re * back_im + coef_im * back_re)
-    class_terms = jnp.stack([term_re, term_im, ctf_map * ctf_map], axis=1)
-    particle_info = jnp.stack([evidence, mean_row, mean_col], axis=1)
-    return (class_terms, particle_info)
-
-
 def _split3(value):
     high = value.astype(jnp.bfloat16)
     rest = value - high.astype(jnp.float32)
     middle = rest.astype(jnp.bfloat16)
     low = (rest - middle.astype(jnp.float32)).astype(jnp.bfloat16)
     return high, middle, low
-
-
-def _exact_dot(lhs, rhs):
-    if lhs.dtype == jnp.bfloat16:
-        parts = [jnp.dot(lhs, piece, preferred_element_type=jnp.float32) for piece in _split3(rhs)]
-    else:
-        parts = [jnp.dot(piece, rhs, preferred_element_type=jnp.float32) for piece in _split3(lhs)]
-    return parts[0] + parts[1] + parts[2]
 
 
 def _group_kernel(meta_ref, *refs):
@@ -307,12 +241,13 @@
     )
     dft_cos, dft_sin = dft_tables(img_side, win_side)
     fourier_own = transform(images, rotation, dft_cos, dft_sin)
-    buffer = (
-        jnp.zeros((slot_count, 2, win_side, win_side), jnp.bfloat16).at[slot_place].set(fourier_own)
-    )
+    hits = slot_place[None, :] == jnp.arange(slot_count, dtype=jnp.int32)[:, None]
+    source = jnp.argmax(hits, axis=1)
+    filled = jnp.any(hits, axis=1)
+    buffer = jnp.where(filled[:, None, None, None], fourier_own[source], jnp.zeros((), jnp.bfloat16))
     buffer = buffer.reshape(owners, capacity, 2, win_side, win_side)
+    coeff_block = lax.all_to_all(buffer, "dom", split_axis=0, concat_axis=0, tiled=True)
     ctf_bins = ctf_table(jnp.arange(16, dtype=jnp.int32), win_side)
-    coeff_block = lax.all_to_all(buffer, "dom", split_axis=0, concat_axis=0, tiled=True)
     tag_block = lax.all_to_all(tag_buffer, "dom", split_axis=0, concat_axis=0, tiled=True)
     tag_flat = tag_block.reshape(slot_count, 4).astype(jnp.int32)
     live = (tag_flat[:, 0] > 0).astype(jnp.int32)

time: 126 us -> 129 us (1.024)
  waiting for transfers between devices: 29.8 us -> 33.7 us
  other arithmetic: 27 us -> 30.9 us
  local copies, waits for them, and re-layouts: 20 us -> 16.9 us
  Pallas kernels: 14 us -> 11.9 us
    all_to_all x1, waiting for transfers between devices: 23.2 us -> 27.1 us  [on_device(): lax.all_to_all(buffer, 'dom', split_axis=0, concat_axis=0, tiled=True)]
    select_n x0 -> x2, other arithmetic: none -> 3.14 us  [the longest x1 3.14 us: on_device(): jnp.where(filled[:, None, None, None], fourier_own[source], jnp.zeros((),...]
    scatter x1 -> x0, local copies, waits for them, and re-layouts: 2.97 us -> none  [on_device(): jnp.zeros((slot_count, 2, win_side, win_side), jnp.bfloat16).at[slot_place]]
    gather x0 -> x1, local copies, waits for them, and re-layouts: none -> 2.18 us  [on_device(): fourier_own[source]]
    pallas_call x1, Pallas kernels: 14 us -> 11.9 us  [group_eval(): pl.pallas_call(_group_kernel, grid_spec=grid_spec, out_shape=[jax.ShapeDt...]
    broadcast_in_dim x1, local copies, waits for them, and re-layouts: 1.86 us -> 0.09 us  [on_device(): jnp.where(filled[:, None, None, None], fourier_own[source], jnp.zeros((),...]
  transfers between devices with their start and end apart: 4 -> 4, of which waited for: 2 -> 2; matrix products, arithmetic and copies ran while one was open for 34% -> 28% of each run, Pallas kernels for 0% -> 0%
where the time goes in v4:
time: 129 us; the launch traced here: 128 us
  waiting for transfers between devices  33.7 us (26%)
  other arithmetic  30.9 us (24%)
  starting transfers between devices  17.1 us (13%)
  local copies, waits for them, and re-layouts  16.9 us (13%)
  between operations  14.2 us (11%)
  Pallas kernels  11.9 us (9%)
  matrix products  3.22 us (2%)
    all_to_all x1, waiting for transfers between devices, on_device(): lax.all_to_all(buffer, 'dom', split_axis=0, concat_axis=0, tiled=True)  27.1 us
    pallas_call x1, Pallas kernels, group_eval(): pl.pallas_call(_group_kernel, grid_spec=grid_spec, out_shape=[jax.ShapeDt...  11.9 us
    all_to_all x1, starting transfers between devices, on_device(): lax.all_to_all(tag_buffer, 'dom', split_axis=0, concat_axis=0, tiled=True)  7.28 us
    all_to_all x1, waiting for transfers between devices, on_device(): lax.all_to_all(info.reshape(owners, capacity, 3), 'dom', split_axis=0, co...  6.57 us
    all_to_all x1, starting transfers between devices, on_device(): lax.all_to_all(buffer, 'dom', split_axis=0, concat_axis=0, tiled=True)  5.99 us
    another operation x6, local copies, waits for them, and re-layouts, phase_pack(): return jnp.stack(planes + [flat], axis=1)  5.49 us
    unnamed x6, other arithmetic  4.91 us
    neg x1, other arithmetic, ctf_table(): return -jnp.sin(strength[:, None, None] * radius[None, :, :] + 0.1)  4.49 us
  transfers between devices with their start and end apart: 4, of which 2 were waited for; matrix products, arithmetic and copies ran while one was open for 28% of the time, Pallas kernels for 0%

profile of v4, /device:TPU:0, one launch (start us, length us, event | category | flops | bytes accessed | tf_op | source)
XLA Modules:
  0.0 127.9 jit_solution(8423173875203170923)
XLA Ops:
  7.2 0.8 convert_bitcast_fusion.1
  8.2 0.7 convert.27
  8.9 0.7 convert_bitcast_fusion
  9.7 0.6 scatter_custom_fusion
  10.3 0.7 copy.62
  11.0 7.3 %all-to-all-start = ((bf16[8,4,4]{1,2,0:T(4,128)(2,1)}), bf16[8,4,4]{1,2,0:T(4,128)(2,1)S(1)}, u32[]{:S(2)}, u32[]{:S(2)}) async-start(bf16[8,4,4]{1,2,0:T(4,128)(2,1)} %copy.62), calls=%async_computation | async-start | bytes 16384 | tf_op jit(solution)/shard_map/all_to_all | solution.py:251
  18.3 0.6 multiply_convert_fusion.1
  19.5 0.6 iota_reduce_fusion
  20.5 0.7 and_compare_fusion.2
  21.2 0.8 fusion
  21.9 0.8 select_convert_fusion
  22.7 0.8 fusion.16
  23.6 0.8 fusion.10
  25.0 4.5 %sine_negate_fusion.refs_5_ = f32[16,128,128]{2,1,0:T(8,128)} fusion(f32[128,128]{1,0:T(8,128)S(1)} %add_multiply_fusion, f32[16]{0:T(128)S(1)} %multiply_add_fusion), kind=kLoop, calls=%fused_computation.22 | loop fusion | flops 786432 | bytes 1114176 | tf_op jit(solution)/shard_map/neg | solution.py:40
  29.9 0.6 fusion.54
  30.7 1.6 %sort.17 = (s32[32]{0:T(128)}, s32[32]{0:T(128)S(1)}) sort(s32[32]{0:T(128)S(1)} %get-tuple-element.39, s32[32]{0:T(128)S(1)} %iota.83), dimensions={0}, to_apply=%region_2.3 | sort | flops 160 | bytes 512 | tf_op jit(solution)/shard_map/jit(argsort)/sort | solution.py:254
  32.3 0.6 gather_fusion
  33.1 2.2 %gather_fusion.1 = bf16[32,2,128,128]{3,2,1,0:T(8,128)(2,1)} fusion(bf16[16,2,128,128]{3,2,0,1:T(8,128)(2,1)S(1)} %pad_maximum_fusion.1, s32[1024]{0:T(1024)S(1)} %get-tuple-element.47), kind=kCustom, calls=%fused_computation.1 | custom fusion | bytes 4194432 | tf_op jit(solution)/shard_map/gather | solution.py:247
  35.3 3.1 %broadcast_select_fusion = bf16[8,4,2,128,128]{4,3,2,1,0:T(8,128)(2,1)} fusion(bf16[8,4,2,128,128]{4,3,2,1,0:T(8,128)(2,1)} %bitcast.44, pred[8,4]{1,0:T(8,128)(4,1)S(1)} %broadcast_in_dim.143), kind=kLoop, calls=%fused_computation.13 | loop fusion | flops 1048576 | bytes 4194336 | tf_op jit(solution)/shard_map/jit(_where)/select_n | solution.py:247
  38.5 6.0 %all-to-all-start.1 = ((bf16[8,4,2,128,128]{4,3,2,1,0:T(8,128)(2,1)}), bf16[8,4,2,128,128]{4,3,2,1,0:T(8,128)(2,1)}, u32[]{:S(2)}, u32[]{:S(2)}) async-start(bf16[8,4,2,128,128]{4,3,2,1,0:T(8,128)(2,1)} %broadcast_select_fusion), calls=%async_computation.1 | async-start | bytes 4194304 | tf_op jit(solution)/shard_map/all_to_all | solution.py:249
  44.8 0.6 fusion.40
  45.4 0.6 fusion.44
  46.0 0.6 fusion.39
  46.6 0.6 fusion.43
  47.2 1.3 fusion.42
  48.5 1.3 fusion.46
  49.8 1.2 constant_dynamic-update-slice_fusion.1
  51.0 0.6 sine_convert_fusion
  51.6 1.2 fusion.53
  52.8 0.7 maximum_bitcast_fusion
  53.8 1.3 %copy.68 = bf16[32,1,128,128]{3,2,1,0:T(8,128)(2,1)} copy(bf16[32,1,128,128]{2,3,0,1:T(8,128)(2,1)S(1)} %pad_bitcast_fusion.1) | data formatting | bytes 2097152 | tf_op jit(solution)/shard_map/stack | solution.py:216
  55.1 1.1 pad_bitcast_fusion
  56.2 1.3 %copy.69 = bf16[32,1,128,128]{3,2,1,0:T(8,128)(2,1)} copy(bf16[32,1,128,128]{2,3,0,1:T(8,128)(2,1)S(1)} %pad_bitcast_fusion) | data formatting | bytes 2097152 | tf_op jit(solution)/shard_map/stack | solution.py:216
  57.7 1.3 %copy.67 = bf16[32,1,128,128]{3,2,1,0:T(8,128)(2,1)} copy(bf16[32,1,128,128]{2,3,0,1:T(8,128)(2,1)S(1)} %pad_bitcast_fusion.2) | data formatting | bytes 2097152 | tf_op jit(solution)/shard_map/stack | solution.py:216
  59.0 0.7 pad.27.clone
  59.8 1.0 broadcast_dynamic-update-slice_fusion
  60.8 0.7 pad_add_fusion.meta_ref
  61.5 3.7 %pad_maximum_fusion.refs_6_ = bf16[32,4,128,128]{3,2,1,0:T(8,128)(2,1)} fusion(bf16[32,1,128,128]{3,2,1,0:T(8,128)(2,1)} %bitcast.45, bf16[32,1,128,128]{3,2,1,0:T(8,128)(2,1)} %copy.69, bf16[32,1,128,128]{3,2,1,0:T(8,128)(2,1)} %copy.68, bf16[32,1,128,128]{3,2,1,0:T(8,128)(2,1)} %copy.67), kind=kLoop, calls=%fused_computation.5 | loop fusion | flops 6291456 | bytes 8388608 | tf_op jit(solution)/shard_map/stack | solution.py:216
  65.2 27.1 %all-to-all-done.1 = bf16[8,4,2,128,128]{4,3,2,1,0:T(8,128)(2,1)} async-done(((bf16[8,4,2,128,128]{4,3,2,1,0:T(8,128)(2,1)}), bf16[8,4,2,128,128]{4,3,2,1,0:T(8,128)(2,1)}, u32[]{:S(2)}, u32[]{:S(2)}) %all-to-all-start.1) | async-done | bytes 2097184 | tf_op jit(solution)/shard_map/all_to_all | solution.py:249
  92.2 11.9 %shard_map.77 = (f32[8,3,128,128]{3,2,1,0:T(8,128)}, f32[32,8,128]{2,1,0:T(8,128)}) custom-call(s32[6,32]{1,0:T(8,128)} %pad_add_fusion.meta_ref, bf16[32,2,128,128]{3,2,1,0:T(8,128)(2,1)} %bitcast.11.refs_0_.refs_1_.refs_2_.refs_3_, bf16[32,2,128,128]{3,2,1,0:T(8,128)(2,1)} %bitcast.11.refs_0_.refs_1_.refs_2_.refs_3_, ...), custom_call_target="tpu_custom_call" | custom-call | tf_op jit(solution)/shard_map/pallas_call | solution.py:184
  104.2 0.9 slice.55
  105.1 0.8 scatter_custom_fusion.1
  105.9 0.7 copy.73
  106.6 3.6 %all-to-all-start.2 = ((f32[8,4,3]{1,2,0:T(4,128)}), f32[8,4,3]{1,2,0:T(4,128)S(1)}, u32[]{:S(2)}, u32[]{:S(2)}) async-start(f32[8,4,3]{1,2,0:T(4,128)} %copy.73), calls=%async_computation.3 | async-start | bytes 32768 | tf_op jit(solution)/shard_map/all_to_all | solution.py:272
  110.3 6.6 %all-to-all-done.2 = f32[8,4,3]{1,2,0:T(4,128)S(1)} async-done(((f32[8,4,3]{1,2,0:T(4,128)}), f32[8,4,3]{1,2,0:T(4,128)S(1)}, u32[]{:S(2)}, u32[]{:S(2)}) %all-to-all-start.2) | async-done | bytes 416 | tf_op jit(solution)/shard_map/all_to_all | solution.py:272
  117.5 0.7 copy.76
  118.2 1.0 fusion.26
  119.1 1.9 %slice_divide_fusion = f32[8,2,64,128]{3,2,1,0:T(8,128)} fusion(f32[8,3,64,128]{3,2,1,0:T(8,128)} %reduce-scatter.2.cloned.1.call-done, f32[8,64,128]{2,1,0:T(8,128)S(1)} %fusion.26), kind=kLoop, calls=%fused_computation.35 | loop fusion | flops 131072 | bytes 1310720 | tf_op jit(solution)/shard_map/div | solution.py:277
  (43 shorter events, 4.1 us)
Async XLA Ops:
  7.2 14.0 %copy-start = (bf16[16,256,256]{2,1,0:T(8,128)(2,1)S(1)}, bf16[16,256,256]{2,1,0:T(8,128)(2,1)}, u32[]{:S(2)}) copy-start(bf16[16,256,256]{2,1,0:T(8,128)(2,1)} %param.6) | copy-start | bytes 6291460
  11.0 18.6 %all-to-all-start = ((bf16[8,4,4]{1,2,0:T(4,128)(2,1)}), bf16[8,4,4]{1,2,0:T(4,128)(2,1)S(1)}, u32[]{:S(2)}, u32[]{:S(2)}) async-start(bf16[8,4,4]{1,2,0:T(4,128)(2,1)} %copy.62), calls=%async_computation | async-start | bytes 16384 | tf_op jit(solution)/shard_map/all_to_all | solution.py:251
  32.3 0.6 copy-start.1
  38.5 53.8 %all-to-all-start.1 = ((bf16[8,4,2,128,128]{4,3,2,1,0:T(8,128)(2,1)}), bf16[8,4,2,128,128]{4,3,2,1,0:T(8,128)(2,1)}, u32[]{:S(2)}, u32[]{:S(2)}) async-start(bf16[8,4,2,128,128]{4,3,2,1,0:T(8,128)(2,1)} %broadcast_select_fusion), calls=%async_computation.1 | async-start | bytes 4194304 | tf_op jit(solution)/shard_map/all_to_all | solution.py:249
  44.4 73.7 %reduce-scatter.2.cloned.1.call-start = ((), (), s32[]{:S(2)}) async-start(), calls=%async_computation.4 | async-start | bytes 2359296 | tf_op jit(solution)/shard_map/reduce_scatter | solution.py:275
  106.6 10.2 %all-to-all-start.2 = ((f32[8,4,3]{1,2,0:T(4,128)}), f32[8,4,3]{1,2,0:T(4,128)S(1)}, u32[]{:S(2)}, u32[]{:S(2)}) async-start(f32[8,4,3]{1,2,0:T(4,128)} %copy.73), calls=%async_computation.3 | async-start | bytes 32768 | tf_op jit(solution)/shard_map/all_to_all | solution.py:272
Sparse Core Ops, SparseCore 0:
  104.3 9.8 reduce-scatter.1

commit v5 on v4

--- a/solution.py
+++ b/solution.py
@@ -225,30 +225,29 @@
     capacity = max(2, 2 * part_count // owners)
     slot_count = owners * capacity
     target = particle_class // per_owner
-    local_class = particle_class - target * per_owner
     positions = jnp.arange(part_count, dtype=jnp.int32)
     same_owner = (target[:, None] == target[None, :]) & (positions[None, :] < positions[:, None])
     slot_rank = jnp.sum(same_owner.astype(jnp.int32), axis=1)
     slot_place = target * capacity + slot_rank
-    slot_tags = jnp.stack(
-        [local_class + 1, defocus_bin, window_anchor[0], window_anchor[1]], axis=1
-    ).astype(jnp.bfloat16)
-    tag_buffer = (
-        jnp.zeros((slot_count, 4), jnp.bfloat16)
-        .at[slot_place]
-        .set(slot_tags)
-        .reshape(owners, capacity, 4)
-    )
+    own_meta = jnp.stack([particle_class, defocus_bin, window_anchor[0], window_anchor[1]], axis=1)
+    all_meta = lax.all_gather(own_meta, "dom")
     dft_cos, dft_sin = dft_tables(img_side, win_side)
     fourier_own = transform(images, rotation, dft_cos, dft_sin)
-    hits = slot_place[None, :] == jnp.arange(slot_count, dtype=jnp.int32)[:, None]
-    source = jnp.argmax(hits, axis=1)
-    filled = jnp.any(hits, axis=1)
-    buffer = jnp.where(filled[:, None, None, None], fourier_own[source], jnp.zeros((), jnp.bfloat16))
+    hits = (slot_place[None, :] == jnp.arange(slot_count, dtype=jnp.int32)[:, None]).astype(jnp.bfloat16)
+    buffer = jnp.einsum("qi,irjk->qrjk", hits, fourier_own)
     buffer = buffer.reshape(owners, capacity, 2, win_side, win_side)
     coeff_block = lax.all_to_all(buffer, "dom", split_axis=0, concat_axis=0, tiled=True)
     ctf_bins = ctf_table(jnp.arange(16, dtype=jnp.int32), win_side)
-    tag_block = lax.all_to_all(tag_buffer, "dom", split_axis=0, concat_axis=0, tiled=True)
+    me = lax.axis_index("dom")
+    src_target = all_meta[:, :, 0] // per_owner
+    earlier = positions[None, None, :] < positions[None, :, None]
+    src_rank = jnp.sum(
+        ((src_target[:, :, None] == src_target[:, None, :]) & earlier).astype(jnp.int32), axis=2
+    )
+    ranks = jnp.arange(capacity, dtype=jnp.int32)
+    chosen = (src_target[:, None, :] == me) & (src_rank[:, None, :] == ranks[None, :, None])
+    fields = all_meta.at[:, :, 0].set(all_meta[:, :, 0] - me * per_owner + 1)
+    tag_block = jnp.sum(jnp.where(chosen[..., None], fields[:, None, :, :], 0), axis=2)
     tag_flat = tag_block.reshape(slot_count, 4).astype(jnp.int32)
     live = (tag_flat[:, 0] > 0).astype(jnp.int32)
     order = jnp.argsort(1 - live, stable=True).astype(jnp.int32)

time: 129 us -> 156 us (1.21)
  blocking collectives: 0 us -> 66.8 us
  waiting for transfers between devices: 33.7 us -> 6.52 us
  starting transfers between devices: 17.1 us -> 10.8 us
  other arithmetic: 30.9 us -> 25.2 us
    all_gather x0 -> x1, blocking collectives: none -> 66.8 us  [on_device(): all_meta = lax.all_gather(own_meta, 'dom')]
    all_to_all x1, waiting for transfers between devices: 27.1 us -> 0.01 us  [on_device(): lax.all_to_all(buffer, 'dom', split_axis=0, concat_axis=0, tiled=True)]
    all_to_all x1 -> x0, starting transfers between devices: 7.28 us -> none  [on_device(): lax.all_to_all(tag_buffer, 'dom', split_axis=0, concat_axis=0, tiled=True)]
    select_n x3 -> x2, other arithmetic: 3.15 us -> 0.02 us  [the longest x1 0.02 us: on_device(): particle_info = returned.reshape(slot_count, 3)[slot_place]]
    another operation x5 -> x0, other arithmetic: 2.78 us -> none  [the longest x3 1.49 us: on_device(): jnp.stack([local_class + 1, defocus_bin, window_anchor[0], window_anchor[...]
    gather x1 -> x0, local copies, waits for them, and re-layouts: 2.18 us -> none  [on_device(): fourier_own[source]]
    reshape x1 -> x3, local copies, waits for them, and re-layouts: 0.74 us -> 2.33 us  [the longest x1 2.16 us: on_device(): buffer = buffer.reshape(owners, capacity, 2, win_side, win_side)]
    unnamed x6 -> x7, other arithmetic: 4.91 us -> 4.9 us
  transfers between devices with their start and end apart: 4 -> 3, of which waited for: 2 -> 1; matrix products, arithmetic and copies ran while one was open for 28% -> 21% of each run, Pallas kernels for 0% -> 0%
where the time goes in v5:
time: 156 us; the launch traced here: 155 us
  blocking collectives  66.8 us (43%)
  other arithmetic  25.2 us (16%)
  local copies, waits for them, and re-layouts  15.4 us (10%)
  between operations  14.3 us (9%)
  Pallas kernels  11.9 us (8%)
  starting transfers between devices  10.8 us (7%)
  waiting for transfers between devices  6.52 us (4%)
  matrix products  4.26 us (3%)
    all_gather x1, blocking collectives, on_device(): all_meta = lax.all_gather(own_meta, 'dom')  66.8 us
    pallas_call x1, Pallas kernels, group_eval(): pl.pallas_call(_group_kernel, grid_spec=grid_spec, out_shape=[jax.ShapeDt...  11.9 us
    all_to_all x1, starting transfers between devices, on_device(): lax.all_to_all(buffer, 'dom', split_axis=0, concat_axis=0, tiled=True)  7.41 us
    all_to_all x1, waiting for transfers between devices, on_device(): lax.all_to_all(info.reshape(owners, capacity, 3), 'dom', split_axis=0, co...  6.5 us
    another operation x6, local copies, waits for them, and re-layouts, phase_pack(): return jnp.stack(planes + [flat], axis=1)  5.49 us
    unnamed x7, other arithmetic  4.9 us
    neg x1, other arithmetic, ctf_table(): return -jnp.sin(strength[:, None, None] * radius[None, :, :] + 0.1)  4.49 us
    another operation x1, other arithmetic, phase_pack(): return jnp.stack(planes + [flat], axis=1)  3.54 us
  transfers between devices with their start and end apart: 3, of which 1 were waited for; matrix products, arithmetic and copies ran while one was open for 21% of the time, Pallas kernels for 0%

profile of v5, /device:TPU:0, one launch (start us, length us, event | category | flops | bytes accessed | tf_op | source)
XLA Modules:
  0.0 155.2 jit_solution(13511548620373929392)
XLA Ops:
  7.2 0.6 multiply_convert_fusion.1
  7.8 0.2 rev.9
  8.1 0.2 rev.11
  8.3 0.4 rev.10
  8.8 0.7 and_compare_fusion.2
  9.4 0.8 fusion
  10.2 0.8 select_convert_fusion
  11.0 0.8 fusion.18
  11.9 0.8 fusion.12
  12.9 0.3 fusion.22
  13.3 1.0 fusion.10
  14.3 2.2 %copy.56 = bf16[8,4,2,128,128]{4,3,2,1,0:T(8,128)(2,1)} copy(bf16[8,4,2,128,128]{4,1,0,3,2:T(4,128)(2,1)S(1)} %bitcast.54) | data formatting | bytes 4194304 | tf_op jit(solution)/shard_map/reshape | solution.py:238
  16.5 7.4 %all-to-all-start = ((bf16[8,4,2,128,128]{4,3,2,1,0:T(8,128)(2,1)}), bf16[8,4,2,128,128]{4,3,2,1,0:T(8,128)(2,1)}, u32[]{:S(2)}, u32[]{:S(2)}) async-start(bf16[8,4,2,128,128]{4,3,2,1,0:T(8,128)(2,1)} %copy.56), calls=%async_computation | async-start | bytes 4194304 | tf_op jit(solution)/shard_map/all_to_all | solution.py:239
  24.0 66.8 %all-gather.1 = s32[8,16,4]{1,2,0:T(4,128)S(1)} all-gather(s32[1,16,4]{1,2,0:T(4,128)S(1)} %add_bitcast_fusion), channel_id=2, replica_groups=mesh['copies'=2,'dom'=8,'cls'=2] {'dom'}, dimensions={0}, use_global_device_ids=true | all-gather | bytes 2304 | tf_op jit(solution)/shard_map/all_gather | solution.py:233
  91.1 0.3 convert_reduce_fusion
  91.4 0.4 select_reduce_fusion
  91.9 0.6 fusion.61
  92.7 1.6 %sort.17 = (s32[32]{0:T(128)}, s32[32]{0:T(128)S(1)}) sort(s32[32]{0:T(128)S(1)} %get-tuple-element.49, s32[32]{0:T(128)S(1)} %iota.96), dimensions={0}, to_apply=%region_2.3 | sort | flops 160 | bytes 512 | tf_op jit(solution)/shard_map/jit(argsort)/sort | solution.py:253
  94.3 0.6 gather_fusion
  95.1 0.6 fusion.42
  95.7 0.6 fusion.46
  96.4 0.6 fusion.41
  97.0 0.6 fusion.45
  97.6 1.3 fusion.44
  98.9 1.3 fusion.48
  100.1 1.2 constant_dynamic-update-slice_fusion.1
  101.3 0.6 sine_convert_fusion
  101.9 1.2 fusion.60
  103.2 0.7 maximum_bitcast_fusion
  104.1 1.3 copy.58
  105.4 1.1 pad_bitcast_fusion
  106.5 1.3 copy.59
  108.0 1.3 copy.57
  109.4 0.8 pad.29.clone
  110.2 1.0 broadcast_dynamic-update-slice_fusion
  111.2 0.7 pad_add_fusion.meta_ref
  111.9 4.5 %sine_negate_fusion.refs_5_ = f32[16,128,128]{2,1,0:T(8,128)} fusion(f32[128,128]{1,0:T(8,128)S(1)} %add_multiply_fusion, f32[16]{0:T(128)S(1)} %multiply_add_fusion), kind=kLoop, calls=%fused_computation.21 | loop fusion | flops 786432 | bytes 1114176 | tf_op jit(solution)/shard_map/neg | solution.py:40
  116.4 3.5 %pad_maximum_fusion.refs_6_ = bf16[32,4,128,128]{3,2,1,0:T(8,128)(2,1)} fusion(bf16[32,1,128,128]{3,2,1,0:T(8,128)(2,1)} %bitcast.55, bf16[32,1,128,128]{3,2,1,0:T(8,128)(2,1)} %copy.59, bf16[32,1,128,128]{3,2,1,0:T(8,128)(2,1)S(1)} %copy-done.1, bf16[32,1,128,128]{3,2,1,0:T(8,128)(2,1)} %copy.57), kind=kLoop, calls=%fused_computation.3 | loop fusion | flops 6291456 | bytes 8388608 | tf_op jit(solution)/shard_map/stack | solution.py:216
  120.0 11.9 %shard_map.77 = (f32[8,3,128,128]{3,2,1,0:T(8,128)}, f32[32,8,128]{2,1,0:T(8,128)}) custom-call(s32[6,32]{1,0:T(8,128)} %pad_add_fusion.meta_ref, bf16[32,2,128,128]{3,2,1,0:T(8,128)(2,1)} %bitcast.16.refs_0_.refs_1_.refs_2_.refs_3_, bf16[32,2,128,128]{3,2,1,0:T(8,128)(2,1)} %bitcast.16.refs_0_.refs_1_.refs_2_.refs_3_, ...), custom_call_target="tpu_custom_call" | custom-call | tf_op jit(solution)/shard_map/pallas_call | solution.py:184
  131.9 0.9 slice.78
  132.8 0.7 scatter_custom_fusion
  133.5 0.7 copy.63
  134.2 3.3 %all-to-all-start.1 = ((f32[8,4,3]{1,2,0:T(4,128)}), f32[8,4,3]{1,2,0:T(4,128)S(1)}, u32[]{:S(2)}, u32[]{:S(2)}) async-start(f32[8,4,3]{1,2,0:T(4,128)} %copy.63), calls=%async_computation.2 | async-start | bytes 32768 | tf_op jit(solution)/shard_map/all_to_all | solution.py:271
  137.6 6.5 %all-to-all-done.1 = f32[8,4,3]{1,2,0:T(4,128)S(1)} async-done(((f32[8,4,3]{1,2,0:T(4,128)}), f32[8,4,3]{1,2,0:T(4,128)S(1)}, u32[]{:S(2)}, u32[]{:S(2)}) %all-to-all-start.1) | async-done | bytes 416 | tf_op jit(solution)/shard_map/all_to_all | solution.py:271
  144.2 0.6 gather_fusion.1
  144.8 0.7 copy.66
  145.4 1.0 fusion.28
  146.4 1.9 %slice_divide_fusion = f32[8,2,64,128]{3,2,1,0:T(8,128)} fusion(f32[8,3,64,128]{3,2,1,0:T(8,128)} %reduce-scatter.2.cloned.1.call-done, f32[8,64,128]{2,1,0:T(8,128)S(1)} %fusion.28), kind=kLoop, calls=%fused_computation.34 | loop fusion | flops 131072 | bytes 1310720 | tf_op jit(solution)/shard_map/div | solution.py:276
  (45 shorter events, 1.9 us)
Async XLA Ops:
  7.2 2.3 %copy-start = (bf16[16,256,256]{2,1,0:T(8,128)(2,1)S(1)}, bf16[16,256,256]{2,1,0:T(8,128)(2,1)}, u32[]{:S(2)}) copy-start(bf16[16,256,256]{2,1,0:T(8,128)(2,1)} %param.8) | copy-start | bytes 6291460
  11.9 0.9 copy-start.2
  16.5 7.5 %copy-start.3 = (s32[2,16]{1,0:T(2,128)S(1)}, s32[2,16]{1,0:T(2,128)}, u32[]{:S(2)}) copy-start(s32[2,16]{1,0:T(2,128)} %param.13) | copy-start | bytes 388
  16.5 7.5 %copy-start.4 = (s32[16]{0:T(128)S(1)}, s32[16]{0:T(128)}, u32[]{:S(2)}) copy-start(s32[16]{0:T(128)} %param.12) | copy-start | bytes 196
  16.5 103.5 %all-to-all-start = ((bf16[8,4,2,128,128]{4,3,2,1,0:T(8,128)(2,1)}), bf16[8,4,2,128,128]{4,3,2,1,0:T(8,128)(2,1)}, u32[]{:S(2)}, u32[]{:S(2)}) async-start(bf16[8,4,2,128,128]{4,3,2,1,0:T(8,128)(2,1)} %copy.56), calls=%async_computation | async-start | bytes 4194304 | tf_op jit(solution)/shard_map/all_to_all | solution.py:239
  23.9 121.5 %reduce-scatter.2.cloned.1.call-start = ((), (), s32[]{:S(2)}) async-start(), calls=%async_computation.3 | async-start | bytes 2359296 | tf_op jit(solution)/shard_map/reduce_scatter | solution.py:274
  109.4 7.0 %copy-start.1 = (bf16[32,1,128,128]{3,2,1,0:T(8,128)(2,1)S(1)}, bf16[32,1,128,128]{3,2,1,0:T(8,128)(2,1)}, u32[]{:S(2)}) copy-start(bf16[32,1,128,128]{3,2,1,0:T(8,128)(2,1)} %copy.58) | copy-start | bytes 3145732
  134.2 9.9 %all-to-all-start.1 = ((f32[8,4,3]{1,2,0:T(4,128)}), f32[8,4,3]{1,2,0:T(4,128)S(1)}, u32[]{:S(2)}, u32[]{:S(2)}) async-start(f32[8,4,3]{1,2,0:T(4,128)} %copy.63), calls=%async_computation.2 | async-start | bytes 32768 | tf_op jit(solution)/shard_map/all_to_all | solution.py:271
Sparse Core Ops, SparseCore 0:
  132.0 6.8 reduce-scatter.1

commit v6 on v4

--- a/solution.py
+++ b/solution.py
@@ -241,10 +241,8 @@
     )
     dft_cos, dft_sin = dft_tables(img_side, win_side)
     fourier_own = transform(images, rotation, dft_cos, dft_sin)
-    hits = slot_place[None, :] == jnp.arange(slot_count, dtype=jnp.int32)[:, None]
-    source = jnp.argmax(hits, axis=1)
-    filled = jnp.any(hits, axis=1)
-    buffer = jnp.where(filled[:, None, None, None], fourier_own[source], jnp.zeros((), jnp.bfloat16))
+    hits = (slot_place[None, :] == jnp.arange(slot_count, dtype=jnp.int32)[:, None]).astype(jnp.bfloat16)
+    buffer = jnp.einsum("qi,irjk->qrjk", hits, fourier_own)
     buffer = buffer.reshape(owners, capacity, 2, win_side, win_side)
     coeff_block = lax.all_to_all(buffer, "dom", split_axis=0, concat_axis=0, tiled=True)
     ctf_bins = ctf_table(jnp.arange(16, dtype=jnp.int32), win_side)
@@ -258,7 +256,7 @@
         [tag_sorted.T, jnp.full((1, slot_count), count, jnp.int32)], axis=0
     )
     pack = phase_pack(tag_sorted, img_side, win_side)
-    group = 4 if slot_count % 4 == 0 else 1
+    group = 8 if slot_count % 8 == 0 else 1
     partial_value, info_sorted = group_eval(
         meta,
         order,

time: 129 us -> 119 us (0.922)
  other arithmetic: 30.9 us -> 27 us
  waiting for transfers between devices: 33.7 us -> 30.2 us
  Pallas kernels: 11.9 us -> 9.21 us
    all_to_all x1, waiting for transfers between devices: 27.1 us -> 23.6 us  [on_device(): lax.all_to_all(buffer, 'dom', split_axis=0, concat_axis=0, tiled=True)]
    select_n x2 -> x0, other arithmetic: 3.14 us -> none  [the longest x1 3.14 us: on_device(): jnp.where(filled[:, None, None, None], fourier_own[source], jnp.zeros((),...]
    pallas_call x1, Pallas kernels: 11.9 us -> 9.21 us  [group_eval(): pl.pallas_call(_group_kernel, grid_spec=grid_spec, out_shape=[jax.ShapeDt...]
    gather x1 -> x0, local copies, waits for them, and re-layouts: 2.18 us -> none  [on_device(): fourier_own[source]]
    reshape x0 -> x1, local copies, waits for them, and re-layouts: none -> 2.16 us  [on_device(): buffer = buffer.reshape(owners, capacity, 2, win_side, win_side)]
  transfers between devices with their start and end apart: 4 -> 4, of which waited for: 2 -> 2; matrix products, arithmetic and copies ran while one was open for 28% -> 35% of each run, Pallas kernels for 0% -> 0%
where the time goes in v6:
time: 119 us
  waiting for transfers between devices  30.2 us (25%)
  other arithmetic  27 us (23%)
  starting transfers between devices  17.1 us (14%)
  local copies, waits for them, and re-layouts  16.7 us (14%)
  between operations  14.2 us (12%)
  Pallas kernels  9.21 us (8%)
  matrix products  4.22 us (4%)
    all_to_all x1, waiting for transfers between devices, on_device(): lax.all_to_all(buffer, 'dom', split_axis=0, concat_axis=0, tiled=True)  23.6 us
    pallas_call x1, Pallas kernels, group_eval(): pl.pallas_call(_group_kernel, grid_spec=grid_spec, out_shape=[jax.ShapeDt...  9.21 us
    all_to_all x1, starting transfers between devices, on_device(): lax.all_to_all(tag_buffer, 'dom', split_axis=0, concat_axis=0, tiled=True)  7.28 us
    all_to_all x1, waiting for transfers between devices, on_device(): lax.all_to_all(info.reshape(owners, capacity, 3), 'dom', split_axis=0, co...  6.57 us
    all_to_all x1, starting transfers between devices, on_device(): lax.all_to_all(buffer, 'dom', split_axis=0, concat_axis=0, tiled=True)  5.99 us
    another operation x6, local copies, waits for them, and re-layouts, phase_pack(): return jnp.stack(planes + [flat], axis=1)  5.49 us
    unnamed x6, other arithmetic  4.92 us
    neg x1, other arithmetic, ctf_table(): return -jnp.sin(strength[:, None, None] * radius[None, :, :] + 0.1)  4.49 us
  transfers between devices with their start and end apart: 4, of which 2 were waited for; matrix products, arithmetic and copies ran while one was open for 35% of the time, Pallas kernels for 0%

profile of v6, /device:TPU:0, one launch (start us, length us, event | category | flops | bytes accessed | tf_op | source)
XLA Modules:
  0.0 118.7 jit_solution(6535665459943656699)
XLA Ops:
  7.2 0.8 convert_bitcast_fusion.1
  8.2 0.7 convert.27
  8.9 0.7 convert_bitcast_fusion
  9.7 0.6 scatter_custom_fusion
  10.3 0.7 copy.70
  11.0 7.3 %all-to-all-start = ((bf16[8,4,4]{1,2,0:T(4,128)(2,1)}), bf16[8,4,4]{1,2,0:T(4,128)(2,1)S(1)}, u32[]{:S(2)}, u32[]{:S(2)}) async-start(bf16[8,4,4]{1,2,0:T(4,128)(2,1)} %copy.70), calls=%async_computation | async-start | bytes 16384 | tf_op jit(solution)/shard_map/all_to_all | solution.py:249
  18.3 0.6 multiply_convert_fusion.1
  19.9 0.7 and_compare_fusion.2
  20.6 0.8 fusion
  21.3 0.8 select_convert_fusion
  22.1 0.8 fusion.18
  23.0 0.8 fusion.12
  24.4 1.0 fusion.10
  25.4 4.5 %sine_negate_fusion.refs_9_ = f32[16,128,128]{2,1,0:T(8,128)} fusion(f32[128,128]{1,0:T(8,128)S(1)} %add_multiply_fusion, f32[16]{0:T(128)S(1)} %multiply_add_fusion), kind=kLoop, calls=%fused_computation.22 | loop fusion | flops 786432 | bytes 1114176 | tf_op jit(solution)/shard_map/neg | solution.py:40
  29.9 2.2 %copy.76 = bf16[8,4,2,128,128]{4,3,2,1,0:T(8,128)(2,1)} copy(bf16[8,4,2,128,128]{4,1,0,3,2:T(4,128)(2,1)S(1)} %bitcast.49) | data formatting | bytes 4194304 | tf_op jit(solution)/shard_map/reshape | solution.py:246
  32.0 6.0 %all-to-all-start.1 = ((bf16[8,4,2,128,128]{4,3,2,1,0:T(8,128)(2,1)}), bf16[8,4,2,128,128]{4,3,2,1,0:T(8,128)(2,1)}, u32[]{:S(2)}, u32[]{:S(2)}) async-start(bf16[8,4,2,128,128]{4,3,2,1,0:T(8,128)(2,1)} %copy.76), calls=%async_computation.1 | async-start | bytes 4194304 | tf_op jit(solution)/shard_map/all_to_all | solution.py:247
  38.5 0.6 fusion.58
  39.2 1.6 %sort.17 = (s32[32]{0:T(128)}, s32[32]{0:T(128)S(1)}) sort(s32[32]{0:T(128)S(1)} %get-tuple-element.37, s32[32]{0:T(128)S(1)} %iota.76), dimensions={0}, to_apply=%region_2.3 | sort | flops 160 | bytes 512 | tf_op jit(solution)/shard_map/jit(argsort)/sort | solution.py:252
  40.9 0.6 gather_fusion
  41.8 0.6 fusion.42
  42.4 0.6 fusion.46
  43.0 0.6 fusion.41
  43.6 0.6 fusion.45
  44.3 1.3 %fusion.44 = (bf16[32,48,128]{2,1,0:T(8,128)(2,1)S(1)}, bf16[32,128,128]{2,1,0:T(8,128)(2,1)}) fusion(bf16[32,48,128]{2,1,0:T(8,128)(2,1)S(1)} %fusion.45, s32[128]{0:T(128)S(1)} %iota_add_fusion, s32[32,8]{1,0:T(8,128)S(1)} %get-tuple-element.46), kind=kLoop, calls=%fused_computation.80 | loop fusion | flops 491519 | bytes 147968
  45.5 1.3 %fusion.48 = (bf16[32,48,128]{2,1,0:T(8,128)(2,1)S(1)}, bf16[32,128,128]{2,1,0:T(8,128)(2,1)}) fusion(bf16[32,48,128]{2,1,0:T(8,128)(2,1)S(1)} %get-tuple-element.30, s32[128]{0:T(128)S(1)} %iota_add_fusion, s32[32,8]{1,0:T(8,128)S(1)} %get-tuple-element.46, bf16[32,128,128]{2,1,0:T(8,128)(2,1)} %get-tuple-element.31), kind=kLoop, calls=%fused_computation.84 | loop fusion | flops 491520 | bytes 147968 | tf_op jit(solution)/shard_map/concatenate | solution.py:211
  46.8 1.2 %constant_dynamic-update-slice_fusion.1 = bf16[32,128,128]{2,1,0:T(8,128)(2,1)} fusion(bf16[32,128,128]{2,1,0:T(8,128)(2,1)} %get-tuple-element.29, s32[128]{0:T(128)S(1)} %iota_add_fusion, s32[32,8]{1,0:T(8,128)S(1)} %get-tuple-element.45), kind=kLoop, calls=%fused_computation.87 | loop fusion | flops 491520 | bytes 67072
  48.0 0.6 sine_convert_fusion
  48.6 1.2 %fusion.57 = (bf16[32,8,128]{2,1,0:T(8,128)(2,1)S(1)}, bf16[32,128,128]{2,1,0:T(8,128)(2,1)}) fusion(s32[128]{0:T(128)S(1)} %iota_add_fusion, s32[32,8]{1,0:T(8,128)S(1)} %get-tuple-element.45, bf16[32,128,128]{2,1,0:T(8,128)(2,1)} %constant_dynamic-update-slice_fusion.1), kind=kLoop, calls=%fused_computation.107 | loop fusion | flops 589824 | bytes 132608 | tf_op jit(solution)/shard_map/neg | solution.py:208
  49.8 0.7 maximum_bitcast_fusion
  50.8 1.3 %copy.78 = bf16[32,1,128,128]{3,2,1,0:T(8,128)(2,1)} copy(bf16[32,1,128,128]{2,3,0,1:T(8,128)(2,1)S(1)} %pad_bitcast_fusion.1) | data formatting | bytes 2097152 | tf_op jit(solution)/shard_map/stack | solution.py:216
  52.1 1.1 pad_bitcast_fusion
  53.2 1.3 %copy.79 = bf16[32,1,128,128]{3,2,1,0:T(8,128)(2,1)} copy(bf16[32,1,128,128]{2,3,0,1:T(8,128)(2,1)S(1)} %pad_bitcast_fusion) | data formatting | bytes 2097152 | tf_op jit(solution)/shard_map/stack | solution.py:216
  54.7 1.3 %copy.77 = bf16[32,1,128,128]{3,2,1,0:T(8,128)(2,1)} copy(bf16[32,1,128,128]{2,3,0,1:T(8,128)(2,1)S(1)} %pad_bitcast_fusion.2) | data formatting | bytes 2097152 | tf_op jit(solution)/shard_map/stack | solution.py:216
  56.1 0.7 pad.27.clone
  56.8 1.0 broadcast_dynamic-update-slice_fusion
  57.8 0.7 pad_add_fusion.meta_ref
  58.5 3.7 %pad_maximum_fusion.refs_10_ = bf16[32,4,128,128]{3,2,1,0:T(8,128)(2,1)} fusion(bf16[32,1,128,128]{3,2,1,0:T(8,128)(2,1)} %bitcast.50, bf16[32,1,128,128]{3,2,1,0:T(8,128)(2,1)} %copy.79, bf16[32,1,128,128]{3,2,1,0:T(8,128)(2,1)} %copy.78, bf16[32,1,128,128]{3,2,1,0:T(8,128)(2,1)} %copy.77), kind=kLoop, calls=%fused_computation.4 | loop fusion | flops 6291456 | bytes 8388608 | tf_op jit(solution)/shard_map/stack | solution.py:216
  62.2 23.6 %all-to-all-done.1 = bf16[8,4,2,128,128]{4,3,2,1,0:T(8,128)(2,1)} async-done(((bf16[8,4,2,128,128]{4,3,2,1,0:T(8,128)(2,1)}), bf16[8,4,2,128,128]{4,3,2,1,0:T(8,128)(2,1)}, u32[]{:S(2)}, u32[]{:S(2)}) %all-to-all-start.1) | async-done | bytes 2097184 | tf_op jit(solution)/shard_map/all_to_all | solution.py:247
  85.8 9.2 %shard_map.77 = (f32[8,3,128,128]{3,2,1,0:T(8,128)}, f32[32,8,128]{2,1,0:T(8,128)}) custom-call(s32[6,32]{1,0:T(8,128)} %pad_add_fusion.meta_ref, bf16[32,2,128,128]{3,2,1,0:T(8,128)(2,1)} %bitcast.13.refs_0_.refs_1_.refs_2_.refs_3_.refs_4_.refs_5_.refs_6_.refs_7_, ...), custom_call_target="tpu_custom_call" | custom-call | tf_op jit(solution)/shard_map/pallas_call | solution.py:184
  95.0 0.9 slice.55
  96.0 0.7 scatter_custom_fusion.1
  96.6 0.7 copy.83
  97.4 3.6 %all-to-all-start.2 = ((f32[8,4,3]{1,2,0:T(4,128)}), f32[8,4,3]{1,2,0:T(4,128)S(1)}, u32[]{:S(2)}, u32[]{:S(2)}) async-start(f32[8,4,3]{1,2,0:T(4,128)} %copy.83), calls=%async_computation.3 | async-start | bytes 32768 | tf_op jit(solution)/shard_map/all_to_all | solution.py:270
  101.0 6.6 %all-to-all-done.2 = f32[8,4,3]{1,2,0:T(4,128)S(1)} async-done(((f32[8,4,3]{1,2,0:T(4,128)}), f32[8,4,3]{1,2,0:T(4,128)S(1)}, u32[]{:S(2)}, u32[]{:S(2)}) %all-to-all-start.2) | async-done | bytes 416 | tf_op jit(solution)/shard_map/all_to_all | solution.py:270
  107.7 0.6 gather_fusion.1
  108.3 0.7 copy.86
  108.9 1.0 fusion.28
  109.9 1.9 %slice_divide_fusion = f32[8,2,64,128]{3,2,1,0:T(8,128)} fusion(f32[8,3,64,128]{3,2,1,0:T(8,128)} %reduce-scatter.2.cloned.1.call-done, f32[8,64,128]{2,1,0:T(8,128)S(1)} %fusion.28), kind=kLoop, calls=%fused_computation.35 | loop fusion | flops 131072 | bytes 1310720 | tf_op jit(solution)/shard_map/div | solution.py:275
  (36 shorter events, 3.3 us)
Async XLA Ops:
  7.2 13.4 %copy-start = (bf16[16,256,256]{2,1,0:T(8,128)(2,1)S(1)}, bf16[16,256,256]{2,1,0:T(8,128)(2,1)}, u32[]{:S(2)}) copy-start(bf16[16,256,256]{2,1,0:T(8,128)(2,1)} %param.6) | copy-start | bytes 6291460
  11.0 21.0 %all-to-all-start = ((bf16[8,4,4]{1,2,0:T(4,128)(2,1)}), bf16[8,4,4]{1,2,0:T(4,128)(2,1)S(1)}, u32[]{:S(2)}, u32[]{:S(2)}) async-start(bf16[8,4,4]{1,2,0:T(4,128)(2,1)} %copy.70), calls=%async_computation | async-start | bytes 16384 | tf_op jit(solution)/shard_map/all_to_all | solution.py:249
  32.0 53.8 %all-to-all-start.1 = ((bf16[8,4,2,128,128]{4,3,2,1,0:T(8,128)(2,1)}), bf16[8,4,2,128,128]{4,3,2,1,0:T(8,128)(2,1)}, u32[]{:S(2)}, u32[]{:S(2)}) async-start(bf16[8,4,2,128,128]{4,3,2,1,0:T(8,128)(2,1)} %copy.76), calls=%async_computation.1 | async-start | bytes 4194304 | tf_op jit(solution)/shard_map/all_to_all | solution.py:247
  38.0 70.9 %reduce-scatter.2.cloned.1.call-start = ((), (), s32[]{:S(2)}) async-start(), calls=%async_computation.4 | async-start | bytes 2359296 | tf_op jit(solution)/shard_map/reduce_scatter | solution.py:273
  97.4 10.2 %all-to-all-start.2 = ((f32[8,4,3]{1,2,0:T(4,128)}), f32[8,4,3]{1,2,0:T(4,128)S(1)}, u32[]{:S(2)}, u32[]{:S(2)}) async-start(f32[8,4,3]{1,2,0:T(4,128)} %copy.83), calls=%async_computation.3 | async-start | bytes 32768 | tf_op jit(solution)/shard_map/all_to_all | solution.py:270
Sparse Core Ops, SparseCore 0:
  95.2 9.2 reduce-scatter.1

commit v7 on v6

--- a/solution.py
+++ b/solution.py
@@ -85,6 +85,37 @@
         lane = lax.broadcasted_iota(jnp.int32, (8, 128), 1)
         sub = lax.broadcasted_iota(jnp.int32, (8, 128), 0)
         inside = lane < span
+        win = ctf_ref.shape[1]
+        half = win // 2
+        row = lax.broadcasted_iota(jnp.int32, (win, win), 0)
+        col = lax.broadcasted_iota(jnp.int32, (win, win), 1)
+        mirror = (col == (win - row) % win).astype(jnp.bfloat16)
+        pick = (col == row - half - 1).astype(jnp.bfloat16)
+        upper_rows = row <= half
+        edge = (row > half) & (col == 0)
+        kept = []
+        for j in range(group):
+            block = coef_refs[j][0]
+            spare = jnp.zeros((win - block.shape[1], win), jnp.bfloat16)
+            full_re = jnp.concatenate([block[0], spare], axis=0)
+            full_im = jnp.concatenate([block[1], spare], axis=0)
+            zero = jnp.zeros((), jnp.bfloat16)
+            top_re = jnp.where(upper_rows, full_re, zero)
+            top_im = jnp.where(upper_rows, full_im, zero)
+            turned = jnp.dot(
+                mirror, jnp.concatenate([top_re, top_im], axis=1), preferred_element_type=jnp.float32
+            ).astype(jnp.bfloat16)
+            stacked = jnp.concatenate([turned[:, 0:win], turned[:, win : 2 * win]], axis=0)
+            flipped = jnp.dot(stacked, mirror, preferred_element_type=jnp.float32)
+            column = lax.dot_general(
+                pick, jnp.concatenate([full_re, full_im], axis=0), (((1,), (1,)), ((), ())),
+                preferred_element_type=jnp.float32,
+            )
+            col_re = pltpu.roll(column[:, 0:win], win - half - 1, 1)
+            col_im = pltpu.roll(column[:, win : 2 * win], win - half - 1, 1)
+            coef_re = jnp.where(edge, col_re, jnp.where(upper_rows, top_re.astype(jnp.float32), flipped[0:win]))
+            coef_im = jnp.where(edge, col_im, jnp.where(upper_rows, top_im.astype(jnp.float32), -flipped[win : 2 * win]))
+            kept.append((coef_re, coef_im))
         st = []
         for j in range(group):
             slot = g * group + j
@@ -92,8 +123,7 @@
             cls = jnp.minimum(jnp.maximum(tag - 1, 0), per_owner - 1)
             bin_id = jnp.minimum(jnp.maximum(meta_ref[1, slot], 0), bins - 1)
             keep = (jnp.full((1, 128), tag, jnp.int32) > 0).astype(jnp.float32)
-            coef_re = coef_refs[j][0, 0].astype(jnp.float32)
-            coef_im = coef_refs[j][0, 1].astype(jnp.float32)
+            coef_re, coef_im = kept[j]
             ctf = ctf_ref[bin_id]
             pred_re = ctf * ref_ref[cls, 0].astype(jnp.float32)
             pred_im = ctf * ref_ref[cls, 1].astype(jnp.float32)
@@ -160,7 +190,8 @@
 def group_eval(meta, order, coef, refs, ctf_tab, pack, group, interpret=False):
     slots = coef.shape[0]
     per_owner = refs.shape[0]
-    win = coef.shape[2]
+    win = coef.shape[3]
+    rows_sent = coef.shape[2]
     bins = ctf_tab.shape[0]
     table = jnp.concatenate([meta, order[None]], axis=0)
 
@@ -170,7 +201,7 @@
     grid_spec = pltpu.PrefetchScalarGridSpec(
         num_scalar_prefetch=1,
         grid=(slots // group,),
-        in_specs=[pl.BlockSpec((1, 2, win, win), coef_map(j)) for j in range(group)]
+        in_specs=[pl.BlockSpec((1, 2, rows_sent, win), coef_map(j)) for j in range(group)]
         + [
             pl.BlockSpec((per_owner, 2, win, win), lambda g, table: (0, 0, 0, 0)),
             pl.BlockSpec((bins, win, win), lambda g, table: (0, 0, 0)),
@@ -241,9 +272,13 @@
     )
     dft_cos, dft_sin = dft_tables(img_side, win_side)
     fourier_own = transform(images, rotation, dft_cos, dft_sin)
+    half = win_side // 2
+    edge = fourier_own[:, :, half + 1 :, 0]
+    edge = jnp.pad(edge, ((0, 0), (0, 0), (0, win_side - edge.shape[2])))
+    compact = jnp.concatenate([fourier_own[:, :, : half + 1, :], edge[:, :, None, :]], axis=2)
     hits = (slot_place[None, :] == jnp.arange(slot_count, dtype=jnp.int32)[:, None]).astype(jnp.bfloat16)
-    buffer = jnp.einsum("qi,irjk->qrjk", hits, fourier_own)
-    buffer = buffer.reshape(owners, capacity, 2, win_side, win_side)
+    buffer = jnp.einsum("qi,irjk->qrjk", hits, compact)
+    buffer = buffer.reshape(owners, capacity, 2, half + 2, win_side)
     coeff_block = lax.all_to_all(buffer, "dom", split_axis=0, concat_axis=0, tiled=True)
     ctf_bins = ctf_table(jnp.arange(16, dtype=jnp.int32), win_side)
     tag_block = lax.all_to_all(tag_buffer, "dom", split_axis=0, concat_axis=0, tiled=True)
@@ -260,7 +295,7 @@
     partial_value, info_sorted = group_eval(
         meta,
         order,
-        coeff_block.reshape(slot_count, 2, win_side, win_side),
+        coeff_block.reshape(slot_count, 2, win_side // 2 + 2, win_side),
         references,
         ctf_bins,
         pack,

time: 119 us -> 109 us (0.916)
  waiting for transfers between devices: 30.2 us -> 6.59 us
  local copies, waits for them, and re-layouts: 16.7 us -> 23.7 us
  Pallas kernels: 9.21 us -> 12.8 us
  starting transfers between devices: 17.1 us -> 20.2 us
    all_to_all x1, waiting for transfers between devices: 23.6 us -> 0.01 us  [on_device(): lax.all_to_all(buffer, 'dom', split_axis=0, concat_axis=0, tiled=True)]
    another operation x6, local copies, waits for them, and re-layouts: 5.49 us -> 11.4 us  [phase_pack(): return jnp.stack(planes + [flat], axis=1)]
    pallas_call x1, Pallas kernels: 9.21 us -> 12.8 us  [group_eval(): pl.pallas_call(_group_kernel, grid_spec=grid_spec, out_shape=[jax.ShapeDt...]
    all_to_all x1, starting transfers between devices: 3.64 us -> 6.71 us  [on_device(): lax.all_to_all(info.reshape(owners, capacity, 3), 'dom', split_axis=0, co...]
    all_to_all x0 -> x1, local copies, waits for them, and re-layouts: none -> 1.23 us  [on_device(): lax.all_to_all(buffer, 'dom', split_axis=0, concat_axis=0, tiled=True)]
  transfers between devices with their start and end apart: 4 -> 4, of which waited for: 2 -> 1; matrix products, arithmetic and copies ran while one was open for 35% -> 42% of each run, Pallas kernels for 0% -> 0%
where the time goes in v7:
time: 109 us; the launch traced here: 108 us
  other arithmetic  26.6 us (24%)
  local copies, waits for them, and re-layouts  23.7 us (22%)
  starting transfers between devices  20.2 us (19%)
  between operations  14.3 us (13%)
  Pallas kernels  12.8 us (12%)
  waiting for transfers between devices  6.59 us (6%)
  matrix products  3.77 us (3%)
    pallas_call x1, Pallas kernels, group_eval(): pl.pallas_call(_group_kernel, grid_spec=grid_spec, out_shape=[jax.ShapeDt...  12.8 us
    another operation x6, local copies, waits for them, and re-layouts, phase_pack(): return jnp.stack(planes + [flat], axis=1)  11.4 us
    all_to_all x1, starting transfers between devices, on_device(): lax.all_to_all(tag_buffer, 'dom', split_axis=0, concat_axis=0, tiled=True)  7.28 us
    all_to_all x1, starting transfers between devices, on_device(): lax.all_to_all(info.reshape(owners, capacity, 3), 'dom', split_axis=0, co...  6.71 us
    all_to_all x1, waiting for transfers between devices, on_device(): lax.all_to_all(info.reshape(owners, capacity, 3), 'dom', split_axis=0, co...  6.57 us
    all_to_all x1, starting transfers between devices, on_device(): lax.all_to_all(buffer, 'dom', split_axis=0, concat_axis=0, tiled=True)  5.99 us
    unnamed x6, other arithmetic  4.88 us
    neg x1, other arithmetic, ctf_table(): return -jnp.sin(strength[:, None, None] * radius[None, :, :] + 0.1)  4.43 us
  transfers between devices with their start and end apart: 4, of which 1 were waited for; matrix products, arithmetic and copies ran while one was open for 42% of the time, Pallas kernels for 0%

profile of v7, /device:TPU:0, one launch (start us, length us, event | category | flops | bytes accessed | tf_op | source)
XLA Modules:
  0.0 108.0 jit_solution(9646224453378866445)
XLA Ops:
  7.2 0.8 convert_bitcast_fusion.1
  8.2 0.7 convert.27
  8.9 0.7 convert_bitcast_fusion
  9.7 0.6 scatter_custom_fusion
  10.3 0.7 copy.90
  11.0 7.3 %all-to-all-start = ((bf16[8,4,4]{1,2,0:T(4,128)(2,1)}), bf16[8,4,4]{1,2,0:T(4,128)(2,1)S(1)}, u32[]{:S(2)}, u32[]{:S(2)}) async-start(bf16[8,4,4]{1,2,0:T(4,128)(2,1)} %copy.90), calls=%async_computation | async-start | bytes 16384 | tf_op jit(solution)/shard_map/all_to_all | solution.py:284
  18.3 0.6 multiply_convert_fusion.1
  19.4 0.7 and_compare_fusion.2
  20.5 0.8 fusion
  21.3 0.8 select_convert_fusion
  22.1 0.8 fusion.10
  23.0 0.8 fusion.16
  25.4 4.4 %sine_negate_fusion.refs_9_ = f32[16,128,128]{2,1,0:T(8,128)} fusion(f32[128,128]{1,0:T(8,128)S(1)} %add_multiply_fusion, f32[16]{0:T(128)S(1)} %multiply_add_fusion), kind=kLoop, calls=%fused_computation.21 | loop fusion | flops 786432 | bytes 1114176 | tf_op jit(solution)/shard_map/neg | solution.py:40
  29.8 1.4 %copy.97 = bf16[8,4,2,66,128]{4,1,3,2,0:T(4,128)(2,1)} copy(bf16[8,4,2,66,128]{4,1,0,3,2:T(4,128)(2,1)S(1)} %bitcast.59) | data formatting | bytes 2162688 | tf_op jit(solution)/shard_map/reshape | solution.py:281
  31.2 6.0 %all-to-all-start.1 = ((bf16[8,4,2,66,128]{4,1,3,2,0:T(4,128)(2,1)}), bf16[8,4,2,66,128]{4,1,3,2,0:T(4,128)(2,1)S(1)}, u32[]{:S(2)}, u32[]{:S(2)}) async-start(bf16[8,4,2,66,128]{4,1,3,2,0:T(4,128)(2,1)} %copy.97), calls=%async_computation.1 | async-start | bytes 2162688 | tf_op jit(solution)/shard_map/all_to_all | solution.py:282
  37.7 0.6 fusion.60
  38.5 1.6 %sort.17 = (s32[32]{0:T(128)}, s32[32]{0:T(128)S(1)}) sort(s32[32]{0:T(128)S(1)} %get-tuple-element.39, s32[32]{0:T(128)S(1)} %iota.76), dimensions={0}, to_apply=%region_2.3 | sort | flops 160 | bytes 512 | tf_op jit(solution)/shard_map/jit(argsort)/sort | solution.py:287
  40.1 0.6 gather_fusion
  41.0 0.6 fusion.44
  41.6 0.6 fusion.48
  42.2 0.6 fusion.43
  42.8 0.6 fusion.47
  43.4 1.2 %fusion.46 = (bf16[32,48,128]{2,1,0:T(8,128)(2,1)S(1)}, bf16[32,128,128]{2,1,0:T(8,128)(2,1)}) fusion(bf16[32,48,128]{2,1,0:T(8,128)(2,1)S(1)} %fusion.47, s32[128]{0:T(128)S(1)} %iota_add_fusion, s32[32,8]{1,0:T(8,128)S(1)} %get-tuple-element.48), kind=kLoop, calls=%fused_computation.85 | loop fusion | flops 491519 | bytes 147968
  44.7 1.2 %fusion.50 = (bf16[32,48,128]{2,1,0:T(8,128)(2,1)S(1)}, bf16[32,128,128]{2,1,0:T(8,128)(2,1)}) fusion(bf16[32,48,128]{2,1,0:T(8,128)(2,1)S(1)} %get-tuple-element.32, s32[128]{0:T(128)S(1)} %iota_add_fusion, s32[32,8]{1,0:T(8,128)S(1)} %get-tuple-element.48, bf16[32,128,128]{2,1,0:T(8,128)(2,1)} %get-tuple-element.33), kind=kLoop, calls=%fused_computation.89 | loop fusion | flops 491520 | bytes 147968 | tf_op jit(solution)/shard_map/concatenate | solution.py:242
  45.9 0.7 copy-done.1
  46.7 1.2 %constant_dynamic-update-slice_fusion.1 = bf16[32,128,128]{2,1,0:T(8,128)(2,1)} fusion(bf16[32,128,128]{2,1,0:T(8,128)(2,1)} %get-tuple-element.31, s32[128]{0:T(128)S(1)} %iota_add_fusion, s32[32,8]{1,0:T(8,128)S(1)} %get-tuple-element.47), kind=kLoop, calls=%fused_computation.92 | loop fusion | flops 491520 | bytes 67072
  47.9 0.6 sine_convert_fusion
  48.5 1.2 %fusion.59 = (bf16[32,8,128]{2,1,0:T(8,128)(2,1)S(1)}, bf16[32,128,128]{2,1,0:T(8,128)(2,1)}) fusion(s32[128]{0:T(128)S(1)} %iota_add_fusion, s32[32,8]{1,0:T(8,128)S(1)} %get-tuple-element.47, bf16[32,128,128]{2,1,0:T(8,128)(2,1)} %constant_dynamic-update-slice_fusion.1), kind=kLoop, calls=%fused_computation.113 | loop fusion | flops 589824 | bytes 132608 | tf_op jit(solution)/shard_map/neg | solution.py:239
  49.7 1.2 %pad_bitcast_fusion = bf16[32,1,128,128]{2,3,0,1:T(8,128)(2,1)} fusion(bf16[32,128,16]{1,2,0:T(8,128)(2,1)S(1)} %get-tuple-element.29), kind=kLoop, calls=%fused_computation.18 | loop fusion | bytes 1179648 | tf_op jit(solution)/shard_map/stack | solution.py:247
  50.9 2.3 %copy.101 = bf16[32,1,128,128]{3,2,1,0:T(8,128)(2,1)} copy(bf16[32,1,128,128]{2,3,0,1:T(8,128)(2,1)} %pad_bitcast_fusion) | data formatting | bytes 2097152 | tf_op jit(solution)/shard_map/stack | solution.py:247
  53.2 1.2 %pad_bitcast_fusion.1 = bf16[32,1,128,128]{2,3,0,1:T(8,128)(2,1)} fusion(bf16[32,128,16]{1,2,0:T(8,128)(2,1)S(1)} %get-tuple-element.28), kind=kLoop, calls=%fused_computation.19 | loop fusion | bytes 1179648 | tf_op jit(solution)/shard_map/stack | solution.py:247
  54.4 2.3 %copy.100 = bf16[32,1,128,128]{3,2,1,0:T(8,128)(2,1)} copy(bf16[32,1,128,128]{2,3,0,1:T(8,128)(2,1)} %pad_bitcast_fusion.1) | data formatting | bytes 2097152 | tf_op jit(solution)/shard_map/stack | solution.py:247
  56.7 2.2 %pad_bitcast_fusion.2 = bf16[32,1,128,128]{2,3,0,1:T(8,128)(2,1)} fusion(bf16[32,128,48]{1,2,0:T(8,128)(2,1)} %bitcast.60), kind=kLoop, calls=%fused_computation.20 | loop fusion | bytes 1441792 | tf_op jit(solution)/shard_map/stack | solution.py:247
  58.8 2.2 %copy.99 = bf16[32,1,128,128]{3,2,1,0:T(8,128)(2,1)} copy(bf16[32,1,128,128]{2,3,0,1:T(8,128)(2,1)} %pad_bitcast_fusion.2) | data formatting | bytes 2097152 | tf_op jit(solution)/shard_map/stack | solution.py:247
  61.1 0.7 pad.34.clone
  61.8 1.0 broadcast_dynamic-update-slice_fusion
  62.8 0.7 pad_add_fusion.meta_ref
  63.5 3.7 %pad_maximum_fusion.refs_10_ = bf16[32,4,128,128]{3,2,1,0:T(8,128)(2,1)} fusion(bf16[32,1,128,128]{3,2,1,0:T(8,128)(2,1)} %bitcast.21, bf16[32,1,128,128]{3,2,1,0:T(8,128)(2,1)} %copy.101, bf16[32,1,128,128]{3,2,1,0:T(8,128)(2,1)} %copy.100, bf16[32,1,128,128]{3,2,1,0:T(8,128)(2,1)} %copy.99), kind=kLoop, calls=%fused_computation.4 | loop fusion | flops 6291456 | bytes 8388608 | tf_op jit(solution)/shard_map/stack | solution.py:247
  67.2 1.2 %copy.98 = bf16[8,4,2,66,128]{4,3,2,1,0:T(8,128)(2,1)} copy(bf16[8,4,2,66,128]{4,1,3,2,0:T(4,128)(2,1)S(1)} %all-to-all-done.1) | data formatting | bytes 2162688 | tf_op jit(solution)/shard_map/all_to_all | solution.py:282
  68.4 12.8 %shard_map.77 = (f32[8,3,128,128]{3,2,1,0:T(8,128)}, f32[32,8,128]{2,1,0:T(8,128)}) custom-call(s32[6,32]{1,0:T(8,128)} %pad_add_fusion.meta_ref, bf16[32,2,66,128]{3,2,1,0:T(8,128)(2,1)} %bitcast.51, bf16[32,2,66,128]{3,2,1,0:T(8,128)(2,1)} %bitcast.52, bf16[32,2,66,128]{3,2,1,0:T(8,128)(2,1)} %bitcast.53, bf16[32,2,66,128]{3,2,1,0:T(8,128)(2,1)} %bitcast.54, ...), custom_call_target="tpu_custom_call" | custom-call | tf_op jit(solution)/shard_map/pallas_call | solution.py:215
  81.3 0.9 slice.63
  82.2 0.7 scatter_custom_fusion.1
  82.9 0.7 copy.105
  83.6 6.7 %all-to-all-start.2 = ((f32[8,4,3]{1,2,0:T(4,128)}), f32[8,4,3]{1,2,0:T(4,128)S(1)}, u32[]{:S(2)}, u32[]{:S(2)}) async-start(f32[8,4,3]{1,2,0:T(4,128)} %copy.105), calls=%async_computation.3 | async-start | bytes 32768 | tf_op jit(solution)/shard_map/all_to_all | solution.py:305
  90.3 6.6 %all-to-all-done.2 = f32[8,4,3]{1,2,0:T(4,128)S(1)} async-done(((f32[8,4,3]{1,2,0:T(4,128)}), f32[8,4,3]{1,2,0:T(4,128)S(1)}, u32[]{:S(2)}, u32[]{:S(2)}) %all-to-all-start.2) | async-done | bytes 416 | tf_op jit(solution)/shard_map/all_to_all | solution.py:305
  97.6 0.7 copy.108
  98.3 1.0 fusion.30
  99.2 1.9 %slice_divide_fusion = f32[8,2,64,128]{3,2,1,0:T(8,128)} fusion(f32[8,3,64,128]{3,2,1,0:T(8,128)} %reduce-scatter.2.cloned.1.call-done, f32[8,64,128]{2,1,0:T(8,128)S(1)} %fusion.30), kind=kLoop, calls=%fused_computation.38 | loop fusion | flops 131072 | bytes 1310720 | tf_op jit(solution)/shard_map/div | solution.py:310
  (43 shorter events, 4.5 us)
Async XLA Ops:
  7.2 13.4 %copy-start = (bf16[16,256,256]{2,1,0:T(8,128)(2,1)S(1)}, bf16[16,256,256]{2,1,0:T(8,128)(2,1)}, u32[]{:S(2)}) copy-start(bf16[16,256,256]{2,1,0:T(8,128)(2,1)} %param.6) | copy-start | bytes 6291460
  11.0 20.2 %all-to-all-start = ((bf16[8,4,4]{1,2,0:T(4,128)(2,1)}), bf16[8,4,4]{1,2,0:T(4,128)(2,1)S(1)}, u32[]{:S(2)}, u32[]{:S(2)}) async-start(bf16[8,4,4]{1,2,0:T(4,128)(2,1)} %copy.90), calls=%async_computation | async-start | bytes 16384 | tf_op jit(solution)/shard_map/all_to_all | solution.py:284
  31.2 36.0 %all-to-all-start.1 = ((bf16[8,4,2,66,128]{4,1,3,2,0:T(4,128)(2,1)}), bf16[8,4,2,66,128]{4,1,3,2,0:T(4,128)(2,1)S(1)}, u32[]{:S(2)}, u32[]{:S(2)}) async-start(bf16[8,4,2,66,128]{4,1,3,2,0:T(4,128)(2,1)} %copy.97), calls=%async_computation.1 | async-start | bytes 2162688 | tf_op jit(solution)/shard_map/all_to_all | solution.py:282
  37.2 61.1 %reduce-scatter.2.cloned.1.call-start = ((), (), s32[]{:S(2)}) async-start(), calls=%async_computation.4 | async-start | bytes 2359296 | tf_op jit(solution)/shard_map/reduce_scatter | solution.py:308
  45.9 0.7 copy-start.1
  83.6 13.3 %all-to-all-start.2 = ((f32[8,4,3]{1,2,0:T(4,128)}), f32[8,4,3]{1,2,0:T(4,128)S(1)}, u32[]{:S(2)}, u32[]{:S(2)}) async-start(f32[8,4,3]{1,2,0:T(4,128)} %copy.105), calls=%async_computation.3 | async-start | bytes 32768 | tf_op jit(solution)/shard_map/all_to_all | solution.py:305
Sparse Core Ops, SparseCore 0:
  81.4 12.0 reduce-scatter.1

commit v8 on v7

--- a/solution.py
+++ b/solution.py
@@ -66,9 +66,9 @@
 
 
 def _group_kernel(meta_ref, *refs):
-    group = len(refs) - 5
+    group = len(refs) - 6
     coef_refs = refs[:group]
-    ref_ref, ctf_ref, pack_ref, total_ref, info_ref = refs[group:]
+    ref_ref, ctf_ref, pack_ref, flat_ref, total_ref, info_ref = refs[group:]
     g = pl.program_id(0)
     span = 8
     per_owner = ref_ref.shape[0]
@@ -130,13 +130,18 @@
             prod_re = (coef_re * pred_re + coef_im * pred_im).astype(jnp.bfloat16)
             prod_im = (coef_im * pred_re - coef_re * pred_im).astype(jnp.bfloat16)
             both = jnp.concatenate([prod_re, prod_im], axis=1)
-            mix = jnp.concatenate([pack_ref[j, 1], pack_ref[j, 2]], axis=0)
+            lanes = pack_ref[j].astype(jnp.float32)
+            wide = lax.broadcasted_iota(jnp.int32, lanes.shape, 1)
+            zero = jnp.zeros((), jnp.float32)
+            cols = jnp.where(wide < 2 * span, pltpu.roll(lanes, 128 - 6 * span, 1), zero)
+            cols_b = jnp.where(wide < 2 * span, pltpu.roll(lanes, 128 - 8 * span, 1), zero)
+            mix = jnp.concatenate([cols, cols_b], axis=0).astype(jnp.bfloat16)
             part = jnp.dot(both, mix, preferred_element_type=jnp.float32)
             st.append(dict(slot=slot, cls=cls, keep=keep, ctf=ctf, coef_re=coef_re, coef_im=coef_im, part=part))
         for j, d in enumerate(st):
             p_hi, p_mid, p_lo = [piece.astype(jnp.float32) for piece in _split3(d["part"])]
             packed = (p_hi + pltpu.roll(p_mid, 2 * span, 1) + pltpu.roll(p_lo, 4 * span, 1)).astype(jnp.bfloat16)
-            d["corr3"] = jnp.dot(pack_ref[j, 3][0:16], packed, preferred_element_type=jnp.float32)
+            d["corr3"] = jnp.dot(flat_ref[j][0:16], packed, preferred_element_type=jnp.float32)
         for j, d in enumerate(st):
             corr3 = d["corr3"]
             corr = (corr3 + pltpu.roll(corr3, 128 - 2 * span, 1)) + pltpu.roll(corr3, 128 - 4 * span, 1)
@@ -162,7 +167,7 @@
             shifted = pltpu.roll(weight, span, 1)
             stacked_w = jnp.concatenate([weight, shifted], axis=0)
             pad = jnp.zeros((112, 128), jnp.bfloat16)
-            col_rows = jnp.concatenate([pack_ref[j, 3][16:32], pad], axis=0)
+            col_rows = jnp.concatenate([flat_ref[j][16:32], pad], axis=0)
             w_pieces = jnp.concatenate(_split3(stacked_w), axis=0)
             d["q3"] = jnp.dot(w_pieces, col_rows, preferred_element_type=jnp.float32)
         for j, d in enumerate(st):
@@ -173,8 +178,11 @@
             spare = jnp.zeros((80, 128), jnp.bfloat16)
             rhs_re = jnp.concatenate(list(_split3(jnp.concatenate([q_re, -q_im], axis=0))) + [spare], axis=0)
             rhs_im = jnp.concatenate(list(_split3(jnp.concatenate([q_im, q_re], axis=0))) + [spare], axis=0)
+            lanes = pack_ref[j]
+            wide = lax.broadcasted_iota(jnp.int32, lanes.shape, 1)
+            rows3 = jnp.where(wide < 6 * span, lanes, jnp.zeros((), jnp.bfloat16))
             d["back"] = jnp.dot(
-                pack_ref[j, 0], jnp.concatenate([rhs_re, rhs_im], axis=1), preferred_element_type=jnp.float32
+                rows3, jnp.concatenate([rhs_re, rhs_im], axis=1), preferred_element_type=jnp.float32
             )
         for d in st:
             back_re = d["back"][:, 0:128]
@@ -187,7 +195,7 @@
             total_ref[cls, 2] = total_ref[cls, 2] + ctf * ctf * keep
 
 
-def group_eval(meta, order, coef, refs, ctf_tab, pack, group, interpret=False):
+def group_eval(meta, order, coef, refs, ctf_tab, pack, flat, group, interpret=False):
     slots = coef.shape[0]
     per_owner = refs.shape[0]
     win = coef.shape[3]
@@ -205,7 +213,8 @@
         + [
             pl.BlockSpec((per_owner, 2, win, win), lambda g, table: (0, 0, 0, 0)),
             pl.BlockSpec((bins, win, win), lambda g, table: (0, 0, 0)),
-            pl.BlockSpec((group, 4, win, win), lambda g, table: (g, 0, 0, 0)),
+            pl.BlockSpec((group, win, win), lambda g, table: (g, 0, 0)),
+            pl.BlockSpec((group, flat.shape[1], win), lambda g, table: (g, 0, 0)),
         ],
         out_specs=[
             pl.BlockSpec((per_owner, 3, win, win), lambda g, table: (0, 0, 0, 0)),
@@ -221,7 +230,7 @@
         ],
         compiler_params=pltpu.CompilerParams(dimension_semantics=("arbitrary",)),
         interpret=interpret,
-    )(table, *([coef] * group), refs, ctf_tab, pack)
+    )(table, *([coef] * group), refs, ctf_tab, pack, flat)
 
 
 def phase_rows(anchor, img_side, win_side):
@@ -237,14 +246,10 @@
     rows_t = phase_rows(tag_flat[:, 2], img_side, win_side)
     cols_t = phase_rows(tag_flat[:, 3], img_side, win_side)
     cols_bt = jnp.concatenate([-cols_t[:, TW:], cols_t[:, :TW]], axis=1)
-    spare = jnp.zeros((rows_t.shape[0], win_side - 4 * TW, win_side), jnp.bfloat16)
-    flat = jnp.concatenate([rows_t, cols_t, spare], axis=1)
-    rows3 = jnp.concatenate([rows_t, rows_t, rows_t], axis=1)
-    planes = [
-        jnp.pad(jnp.swapaxes(t, 1, 2), ((0, 0), (0, 0), (0, win_side - t.shape[1])))
-        for t in (rows3, cols_t, cols_bt)
-    ]
-    return jnp.stack(planes + [flat], axis=1)
+    flat = jnp.concatenate([rows_t, cols_t], axis=1)
+    stacked = jnp.concatenate([rows_t, rows_t, rows_t, cols_t, cols_bt], axis=1)
+    stacked = jnp.pad(stacked, ((0, 0), (0, win_side - stacked.shape[1]), (0, 0)))
+    return jnp.swapaxes(stacked, 1, 2), flat[:, : 4 * TW]
 
 
 def on_device(images, references, particle_class, rotation, defocus_bin, window_anchor):
@@ -290,7 +295,7 @@
     meta = jnp.concatenate(
         [tag_sorted.T, jnp.full((1, slot_count), count, jnp.int32)], axis=0
     )
-    pack = phase_pack(tag_sorted, img_side, win_side)
+    pack, flat = phase_pack(tag_sorted, img_side, win_side)
     group = 8 if slot_count % 8 == 0 else 1
     partial_value, info_sorted = group_eval(
         meta,
@@ -299,6 +304,7 @@
         references,
         ctf_bins,
         pack,
+        flat,
         group,
     )
     info = jnp.zeros((slot_count, 3), jnp.float32).at[order].set(info_sorted[:, 0, :3])

time: 109 us -> 102 us (0.936)
  local copies, waits for them, and re-layouts: 23.7 us -> 15.1 us
  other arithmetic: 26.6 us -> 29 us
  waiting for transfers between devices: 6.59 us -> 8.84 us
  starting transfers between devices: 20.2 us -> 18 us
    another operation x6 -> x0, local copies, waits for them, and re-layouts: 11.4 us -> none  [phase_pack(): return jnp.stack(planes + [flat], axis=1)]
    unnamed x6 -> x9, other arithmetic: 4.88 us -> 11 us
    transpose x0 -> x2, local copies, waits for them, and re-layouts: none -> 4.55 us  [phase_pack(): return (jnp.swapaxes(stacked, 1, 2), flat[:, :4 * TW])]
    another operation x2 -> x1, other arithmetic: 4.42 us -> 0.68 us  [the longest x1 3.73 us: phase_pack(): return jnp.stack(planes + [flat], axis=1)]
    all_to_all x1, waiting for transfers between devices: 0.01 us -> 2.25 us  [on_device(): lax.all_to_all(buffer, 'dom', split_axis=0, concat_axis=0, tiled=True)]
    all_to_all x1, starting transfers between devices: 6.71 us -> 4.46 us  [on_device(): lax.all_to_all(info.reshape(owners, capacity, 3), 'dom', split_axis=0, co...]
    neg x1 -> x0, other arithmetic: 1.2 us -> none  [phase_pack(): cols_bt = jnp.concatenate([-cols_t[:, TW:], cols_t[:, :TW]], axis=1)]
  transfers between devices with their start and end apart: 4 -> 4, of which waited for: 1 -> 2; matrix products, arithmetic and copies ran while one was open for 42% -> 39% of each run, Pallas kernels for 0% -> 0%
where the time goes in v8:
time: 102 us
  other arithmetic  29 us (28%)
  starting transfers between devices  18 us (18%)
  local copies, waits for them, and re-layouts  15.1 us (15%)
  between operations  14.2 us (14%)
  Pallas kernels  12.6 us (12%)
  waiting for transfers between devices  8.84 us (9%)
  matrix products  3.76 us (4%)
    pallas_call x1, Pallas kernels, group_eval(): pl.pallas_call(_group_kernel, grid_spec=grid_spec, out_shape=[jax.ShapeDt...  12.6 us
    unnamed x9, other arithmetic  11 us
    all_to_all x1, starting transfers between devices, on_device(): lax.all_to_all(tag_buffer, 'dom', split_axis=0, concat_axis=0, tiled=True)  7.28 us
    all_to_all x1, waiting for transfers between devices, on_device(): lax.all_to_all(info.reshape(owners, capacity, 3), 'dom', split_axis=0, co...  6.57 us
    all_to_all x1, starting transfers between devices, on_device(): lax.all_to_all(buffer, 'dom', split_axis=0, concat_axis=0, tiled=True)  5.99 us
    transpose x2, local copies, waits for them, and re-layouts, phase_pack(): return (jnp.swapaxes(stacked, 1, 2), flat[:, :4 * TW])  4.55 us
    all_to_all x1, starting transfers between devices, on_device(): lax.all_to_all(info.reshape(owners, capacity, 3), 'dom', split_axis=0, co...  4.46 us
    neg x1, other arithmetic, ctf_table(): return -jnp.sin(strength[:, None, None] * radius[None, :, :] + 0.1)  4.4 us
  transfers between devices with their start and end apart: 4, of which 2 were waited for; matrix products, arithmetic and copies ran while one was open for 39% of the time, Pallas kernels for 0%

profile of v8, /device:TPU:0, one launch (start us, length us, event | category | flops | bytes accessed | tf_op | source)
XLA Modules:
  0.0 101.6 jit_solution(11695065039549025589)
XLA Ops:
  7.2 0.8 convert_bitcast_fusion.1
  8.2 0.7 convert.27
  8.9 0.7 convert_bitcast_fusion
  9.7 0.6 scatter_custom_fusion
  10.3 0.7 copy.80
  11.0 7.3 %all-to-all-start = ((bf16[8,4,4]{1,2,0:T(4,128)(2,1)}), bf16[8,4,4]{1,2,0:T(4,128)(2,1)S(1)}, u32[]{:S(2)}, u32[]{:S(2)}) async-start(bf16[8,4,4]{1,2,0:T(4,128)(2,1)} %copy.80), calls=%async_computation | async-start | bytes 16384 | tf_op jit(solution)/shard_map/all_to_all | solution.py:289
  18.3 0.6 multiply_convert_fusion.1
  19.4 0.4 rev.10
  19.9 0.7 and_compare_fusion.2
  20.5 0.8 fusion
  21.3 0.8 select_convert_fusion
  22.1 0.8 fusion.16
  23.0 0.8 fusion.10
  24.8 0.5 fusion.21
  25.3 4.4 %sine_negate_fusion.refs_9_ = f32[16,128,128]{2,1,0:T(8,128)} fusion(f32[128,128]{1,0:T(8,128)S(1)} %add_multiply_fusion, f32[16]{0:T(128)S(1)} %multiply_add_fusion), kind=kLoop, calls=%fused_computation.18 | loop fusion | flops 786432 | bytes 1114176 | tf_op jit(solution)/shard_map/neg | solution.py:40
  29.7 1.4 %copy.87 = bf16[8,4,2,66,128]{4,1,3,2,0:T(4,128)(2,1)} copy(bf16[8,4,2,66,128]{4,1,0,3,2:T(4,128)(2,1)S(1)} %bitcast.49) | data formatting | bytes 2162688 | tf_op jit(solution)/shard_map/reshape | solution.py:286
  31.1 6.0 %all-to-all-start.1 = ((bf16[8,4,2,66,128]{4,1,3,2,0:T(4,128)(2,1)}), bf16[8,4,2,66,128]{4,1,3,2,0:T(4,128)(2,1)S(1)}, u32[]{:S(2)}, u32[]{:S(2)}) async-start(bf16[8,4,2,66,128]{4,1,3,2,0:T(4,128)(2,1)} %copy.87), calls=%async_computation.1 | async-start | bytes 2162688 | tf_op jit(solution)/shard_map/all_to_all | solution.py:287
  37.6 0.6 fusion.51
  38.4 1.6 %sort.17 = (s32[32]{0:T(128)}, s32[32]{0:T(128)S(1)}) sort(s32[32]{0:T(128)S(1)} %get-tuple-element.33, s32[32]{0:T(128)S(1)} %iota.76), dimensions={0}, to_apply=%region_2.3 | sort | flops 160 | bytes 512 | tf_op jit(solution)/shard_map/jit(argsort)/sort | solution.py:292
  40.0 0.6 gather_fusion
  40.8 1.2 %constant_dynamic-update-slice_fusion.8 = bf16[32,80,128]{2,1,0:T(8,128)(2,1)} fusion(s32[128]{0:T(128)S(1)} %iota_add_fusion, s32[32,8]{1,0:T(8,128)S(1)} %get-tuple-element.44), kind=kLoop, calls=%fused_computation.87 | loop fusion | flops 491519 | bytes 67072
  42.0 1.2 %constant_dynamic-update-slice_fusion.7 = bf16[32,80,128]{2,1,0:T(8,128)(2,1)} fusion(bf16[32,80,128]{2,1,0:T(8,128)(2,1)} %constant_dynamic-update-slice_fusion.8, s32[128]{0:T(128)S(1)} %iota_add_fusion, s32[32,8]{1,0:T(8,128)S(1)} %get-tuple-element.44), kind=kLoop, calls=%fused_computation.86 | loop fusion | flops 491520 | bytes 67072
  43.2 1.2 %constant_dynamic-update-slice_fusion.6 = bf16[32,80,128]{2,1,0:T(8,128)(2,1)} fusion(bf16[32,80,128]{2,1,0:T(8,128)(2,1)} %constant_dynamic-update-slice_fusion.7, s32[128]{0:T(128)S(1)} %iota_add_fusion, s32[32,8]{1,0:T(8,128)S(1)} %get-tuple-element.44), kind=kLoop, calls=%fused_computation.85 | loop fusion | flops 491520 | bytes 67072
  44.5 1.2 %constant_dynamic-update-slice_fusion.5 = bf16[32,80,128]{2,1,0:T(8,128)(2,1)} fusion(bf16[32,80,128]{2,1,0:T(8,128)(2,1)} %constant_dynamic-update-slice_fusion.6, s32[128]{0:T(128)S(1)} %iota_add_fusion, s32[32,8]{1,0:T(8,128)S(1)} %get-tuple-element.44), kind=kLoop, calls=%fused_computation.84 | loop fusion | flops 491520 | bytes 67072
  45.7 1.2 %constant_dynamic-update-slice_fusion.4 = bf16[32,80,128]{2,1,0:T(8,128)(2,1)} fusion(bf16[32,80,128]{2,1,0:T(8,128)(2,1)} %constant_dynamic-update-slice_fusion.5, s32[128]{0:T(128)S(1)} %iota_add_fusion, s32[32,8]{1,0:T(8,128)S(1)} %get-tuple-element.44), kind=kLoop, calls=%fused_computation.83 | loop fusion | flops 491520 | bytes 67072
  47.0 1.2 %constant_dynamic-update-slice_fusion.3 = bf16[32,80,128]{2,1,0:T(8,128)(2,1)} fusion(bf16[32,80,128]{2,1,0:T(8,128)(2,1)} %constant_dynamic-update-slice_fusion.4, s32[128]{0:T(128)S(1)} %iota_add_fusion, s32[32,8]{1,0:T(8,128)S(1)} %get-tuple-element.44), kind=kLoop, calls=%fused_computation.82 | loop fusion | flops 491520 | bytes 67072
  48.2 1.2 %constant_dynamic-update-slice_fusion.2 = bf16[32,80,128]{2,1,0:T(8,128)(2,1)} fusion(bf16[32,80,128]{2,1,0:T(8,128)(2,1)} %constant_dynamic-update-slice_fusion.3, s32[128]{0:T(128)S(1)} %iota_add_fusion, s32[32,8]{1,0:T(8,128)S(1)} %get-tuple-element.43), kind=kLoop, calls=%fused_computation.81 | loop fusion | flops 491520 | bytes 67072
  49.4 1.2 %constant_dynamic-update-slice_fusion.1 = bf16[32,80,128]{2,1,0:T(8,128)(2,1)} fusion(bf16[32,80,128]{2,1,0:T(8,128)(2,1)} %constant_dynamic-update-slice_fusion.2, s32[128]{0:T(128)S(1)} %iota_add_fusion, s32[32,8]{1,0:T(8,128)S(1)} %get-tuple-element.43), kind=kLoop, calls=%fused_computation.80 | loop fusion | flops 491520 | bytes 67072
  50.7 1.2 %negate_dynamic-update-slice_fusion = bf16[32,80,128]{2,1,0:T(8,128)(2,1)} fusion(bf16[32,80,128]{2,1,0:T(8,128)(2,1)} %constant_dynamic-update-slice_fusion.1, s32[128]{0:T(128)S(1)} %iota_add_fusion, s32[32,8]{1,0:T(8,128)S(1)} %get-tuple-element.43), kind=kLoop, calls=%fused_computation.77 | loop fusion | flops 589824 | bytes 67072
  51.9 1.2 %constant_dynamic-update-slice_fusion = bf16[32,80,128]{2,1,0:T(8,128)(2,1)} fusion(bf16[32,80,128]{2,1,0:T(8,128)(2,1)} %negate_dynamic-update-slice_fusion, s32[128]{0:T(128)S(1)} %iota_add_fusion, s32[32,8]{1,0:T(8,128)S(1)} %get-tuple-element.43), kind=kLoop, calls=%fused_computation.79 | loop fusion | flops 491520 | bytes 67072 | tf_op jit(solution)/shard_map/concatenate | solution.py:250
  53.1 2.3 %pad_bitcast_fusion = bf16[32,128,128]{1,2,0:T(8,128)(2,1)} fusion(bf16[32,80,128]{2,1,0:T(8,128)(2,1)} %constant_dynamic-update-slice_fusion), kind=kLoop, calls=%fused_computation.17 | loop fusion | bytes 1703936 | tf_op jit(solution)/shard_map/transpose | solution.py:252
  55.4 2.3 %copy.89.refs_10_ = bf16[32,128,128]{2,1,0:T(8,128)(2,1)} copy(bf16[32,128,128]{1,2,0:T(8,128)(2,1)} %pad_bitcast_fusion) | data formatting | bytes 2097152 | tf_op jit(solution)/shard_map/transpose | solution.py:252
  57.6 0.7 pad.21.clone
  58.3 1.2 %cosine_convert_fusion.1 = (bf16[32,8,128]{2,1,0:T(8,128)(2,1)S(1)}, bf16[32,8,128]{2,1,0:T(8,128)(2,1)S(1)}, bf16[32,8,128]{2,1,0:T(8,128)(2,1)S(1)}, bf16[32,8,128]{2,1,0:T(8,128)(2,1)S(1)}) fusion(s32[128]{0:T(128)S(1)} %iota_add_fusion, s32[32,8]{1,0:T(8,128)S(1)} %get-tuple-element.44, s32[32,8]{1,0:T(8,128)S(1)} %get-tuple-element.43), kind=kLoop, calls=%fused_computation.71 | loop fusion | flops 1048576 | bytes 264704 | tf_op jit(solution)/shard_map/convert_element_type | solution.py:241
  59.6 0.8 pad_maximum_fusion.2.refs_11_
  60.3 0.7 pad_add_fusion.meta_ref
  61.0 2.3 %all-to-all-done.1 = bf16[8,4,2,66,128]{4,1,3,2,0:T(4,128)(2,1)S(1)} async-done(((bf16[8,4,2,66,128]{4,1,3,2,0:T(4,128)(2,1)}), bf16[8,4,2,66,128]{4,1,3,2,0:T(4,128)(2,1)S(1)}, u32[]{:S(2)}, u32[]{:S(2)}) %all-to-all-start.1) | async-done | bytes 1081376 | tf_op jit(solution)/shard_map/all_to_all | solution.py:287
  63.2 1.2 %copy.88 = bf16[8,4,2,66,128]{4,3,2,1,0:T(8,128)(2,1)} copy(bf16[8,4,2,66,128]{4,1,3,2,0:T(4,128)(2,1)S(1)} %all-to-all-done.1) | data formatting | bytes 2162688 | tf_op jit(solution)/shard_map/all_to_all | solution.py:287
  64.4 12.6 %shard_map.77 = (f32[8,3,128,128]{3,2,1,0:T(8,128)}, f32[32,8,128]{2,1,0:T(8,128)}) custom-call(s32[6,32]{1,0:T(8,128)} %pad_add_fusion.meta_ref, bf16[32,2,66,128]{3,2,1,0:T(8,128)(2,1)} %bitcast.41, bf16[32,2,66,128]{3,2,1,0:T(8,128)(2,1)} %bitcast.42, bf16[32,2,66,128]{3,2,1,0:T(8,128)(2,1)} %bitcast.43, bf16[32,2,66,128]{3,2,1,0:T(8,128)(2,1)} %bitcast.44, ...), custom_call_target="tpu_custom_call" | custom-call | tf_op jit(solution)/shard_map/pallas_call | solution.py:224
  77.1 0.9 slice.63
  78.0 0.7 scatter_custom_fusion.1
  78.7 0.7 copy.93
  79.4 4.5 %all-to-all-start.2 = ((f32[8,4,3]{1,2,0:T(4,128)}), f32[8,4,3]{1,2,0:T(4,128)S(1)}, u32[]{:S(2)}, u32[]{:S(2)}) async-start(f32[8,4,3]{1,2,0:T(4,128)} %copy.93), calls=%async_computation.3 | async-start | bytes 32768 | tf_op jit(solution)/shard_map/all_to_all | solution.py:311
  83.9 6.6 %all-to-all-done.2 = f32[8,4,3]{1,2,0:T(4,128)S(1)} async-done(((f32[8,4,3]{1,2,0:T(4,128)}), f32[8,4,3]{1,2,0:T(4,128)S(1)}, u32[]{:S(2)}, u32[]{:S(2)}) %all-to-all-start.2) | async-done | bytes 416 | tf_op jit(solution)/shard_map/all_to_all | solution.py:311
  90.6 0.6 gather_fusion.1
  91.2 0.7 copy.96
  91.8 1.0 fusion.30
  92.8 1.9 %slice_divide_fusion = f32[8,2,64,128]{3,2,1,0:T(8,128)} fusion(f32[8,3,64,128]{3,2,1,0:T(8,128)} %reduce-scatter.2.cloned.1.call-done, f32[8,64,128]{2,1,0:T(8,128)S(1)} %fusion.30), kind=kLoop, calls=%fused_computation.35 | loop fusion | flops 131072 | bytes 1310720 | tf_op jit(solution)/shard_map/div | solution.py:316
  (37 shorter events, 2.9 us)
Async XLA Ops:
  7.2 13.4 %copy-start = (bf16[16,256,256]{2,1,0:T(8,128)(2,1)S(1)}, bf16[16,256,256]{2,1,0:T(8,128)(2,1)}, u32[]{:S(2)}) copy-start(bf16[16,256,256]{2,1,0:T(8,128)(2,1)} %param.6) | copy-start | bytes 6291460
  11.0 20.1 %all-to-all-start = ((bf16[8,4,4]{1,2,0:T(4,128)(2,1)}), bf16[8,4,4]{1,2,0:T(4,128)(2,1)S(1)}, u32[]{:S(2)}, u32[]{:S(2)}) async-start(bf16[8,4,4]{1,2,0:T(4,128)(2,1)} %copy.80), calls=%async_computation | async-start | bytes 16384 | tf_op jit(solution)/shard_map/all_to_all | solution.py:289
  31.1 32.1 %all-to-all-start.1 = ((bf16[8,4,2,66,128]{4,1,3,2,0:T(4,128)(2,1)}), bf16[8,4,2,66,128]{4,1,3,2,0:T(4,128)(2,1)S(1)}, u32[]{:S(2)}, u32[]{:S(2)}) async-start(bf16[8,4,2,66,128]{4,1,3,2,0:T(4,128)(2,1)} %copy.87), calls=%async_computation.1 | async-start | bytes 2162688 | tf_op jit(solution)/shard_map/all_to_all | solution.py:287
  37.1 54.7 %reduce-scatter.2.cloned.1.call-start = ((), (), s32[]{:S(2)}) async-start(), calls=%async_computation.4 | async-start | bytes 2359296 | tf_op jit(solution)/shard_map/reduce_scatter | solution.py:314
  79.4 11.0 %all-to-all-start.2 = ((f32[8,4,3]{1,2,0:T(4,128)}), f32[8,4,3]{1,2,0:T(4,128)S(1)}, u32[]{:S(2)}, u32[]{:S(2)}) async-start(f32[8,4,3]{1,2,0:T(4,128)} %copy.93), calls=%async_computation.3 | async-start | bytes 32768 | tf_op jit(solution)/shard_map/all_to_all | solution.py:311
Sparse Core Ops, SparseCore 0:
  77.2 9.7 reduce-scatter.1

commit v9 on v8

--- a/solution.py
+++ b/solution.py
@@ -268,20 +268,18 @@
     slot_place = target * capacity + slot_rank
     slot_tags = jnp.stack(
         [local_class + 1, defocus_bin, window_anchor[0], window_anchor[1]], axis=1
-    ).astype(jnp.bfloat16)
-    tag_buffer = (
-        jnp.zeros((slot_count, 4), jnp.bfloat16)
-        .at[slot_place]
-        .set(slot_tags)
-        .reshape(owners, capacity, 4)
-    )
+    ).astype(jnp.float32)
+    matches = slot_place[None, :] == jnp.arange(slot_count, dtype=jnp.int32)[:, None]
+    tag_buffer = jnp.sum(
+        jnp.where(matches[:, :, None], slot_tags[None, :, :], 0.0), axis=1
+    ).reshape(owners, capacity, 4)
     dft_cos, dft_sin = dft_tables(img_side, win_side)
     fourier_own = transform(images, rotation, dft_cos, dft_sin)
     half = win_side // 2
     edge = fourier_own[:, :, half + 1 :, 0]
     edge = jnp.pad(edge, ((0, 0), (0, 0), (0, win_side - edge.shape[2])))
     compact = jnp.concatenate([fourier_own[:, :, : half + 1, :], edge[:, :, None, :]], axis=2)
-    hits = (slot_place[None, :] == jnp.arange(slot_count, dtype=jnp.int32)[:, None]).astype(jnp.bfloat16)
+    hits = matches.astype(jnp.bfloat16)
     buffer = jnp.einsum("qi,irjk->qrjk", hits, compact)
     buffer = buffer.reshape(owners, capacity, 2, half + 2, win_side)
     coeff_block = lax.all_to_all(buffer, "dom", split_axis=0, concat_axis=0, tiled=True)

time: 102 us -> 102 us (level)
  transfers between devices with their start and end apart: 4 -> 4, of which waited for: 2 -> 2; matrix products, arithmetic and copies ran while one was open for 39% -> 40% of each run, Pallas kernels for 0% -> 0%
where the time goes in v9:
time: 102 us; the launch traced here: 101 us
  other arithmetic  28.5 us (28%)
  starting transfers between devices  17.9 us (18%)
  local copies, waits for them, and re-layouts  15.1 us (15%)
  between operations  14.2 us (14%)
  Pallas kernels  12.6 us (12%)
  waiting for transfers between devices  8.86 us (9%)
  matrix products  3.76 us (4%)
    pallas_call x1, Pallas kernels, group_eval(): pl.pallas_call(_group_kernel, grid_spec=grid_spec, out_shape=[jax.ShapeDt...  12.6 us
    unnamed x9, other arithmetic  11 us
    all_to_all x1, starting transfers between devices, on_device(): lax.all_to_all(tag_buffer, 'dom', split_axis=0, concat_axis=0, tiled=True)  7.28 us
    all_to_all x1, waiting for transfers between devices, on_device(): lax.all_to_all(info.reshape(owners, capacity, 3), 'dom', split_axis=0, co...  6.57 us
    all_to_all x1, starting transfers between devices, on_device(): lax.all_to_all(buffer, 'dom', split_axis=0, concat_axis=0, tiled=True)  5.99 us
    transpose x2, local copies, waits for them, and re-layouts, phase_pack(): return (jnp.swapaxes(stacked, 1, 2), flat[:, :4 * TW])  4.55 us
    all_to_all x1, starting transfers between devices, on_device(): lax.all_to_all(info.reshape(owners, capacity, 3), 'dom', split_axis=0, co...  4.46 us
    neg x1, other arithmetic, ctf_table(): return -jnp.sin(strength[:, None, None] * radius[None, :, :] + 0.1)  4.4 us
  transfers between devices with their start and end apart: 4, of which 2 were waited for; matrix products, arithmetic and copies ran while one was open for 40% of the time, Pallas kernels for 0%

profile of v9, /device:TPU:0, one launch (start us, length us, event | category | flops | bytes accessed | tf_op | source)
XLA Modules:
  0.0 101.0 jit_solution(4948904867640192544)
XLA Ops:
  7.2 0.8 add_bitcast_fusion
  8.3 0.8 slice_bitcast_fusion.1
  9.0 0.7 add_convert_fusion
  9.9 0.6 copy.78
  10.5 7.3 %all-to-all-start = ((f32[8,4,4]{1,2,0:T(4,128)}), f32[8,4,4]{1,2,0:T(4,128)S(1)}, u32[]{:S(2)}, u32[]{:S(2)}) async-start(f32[8,4,4]{1,2,0:T(4,128)} %copy.78), calls=%async_computation | async-start | bytes 32768 | tf_op jit(solution)/shard_map/all_to_all | solution.py:287
  17.8 0.6 multiply_convert_fusion.1
  18.9 0.4 rev.10
  19.3 0.7 and_compare_fusion.2
  20.0 0.8 fusion
  20.8 0.8 select_convert_fusion
  21.6 0.8 fusion.16
  22.4 0.8 fusion.10
  23.7 0.4 fusion.25
  24.2 0.5 fusion.21
  24.8 4.4 %sine_negate_fusion.refs_9_ = f32[16,128,128]{2,1,0:T(8,128)} fusion(f32[128,128]{1,0:T(8,128)S(1)} %add_multiply_fusion, f32[16]{0:T(128)S(1)} %multiply_add_fusion), kind=kLoop, calls=%fused_computation.17 | loop fusion | flops 786432 | bytes 1114176 | tf_op jit(solution)/shard_map/neg | solution.py:40
  29.2 1.4 %copy.85 = bf16[8,4,2,66,128]{4,1,3,2,0:T(4,128)(2,1)} copy(bf16[8,4,2,66,128]{4,1,0,3,2:T(4,128)(2,1)S(1)} %bitcast.49) | data formatting | bytes 2162688 | tf_op jit(solution)/shard_map/reshape | solution.py:284
  30.6 6.0 %all-to-all-start.1 = ((bf16[8,4,2,66,128]{4,1,3,2,0:T(4,128)(2,1)}), bf16[8,4,2,66,128]{4,1,3,2,0:T(4,128)(2,1)S(1)}, u32[]{:S(2)}, u32[]{:S(2)}) async-start(bf16[8,4,2,66,128]{4,1,3,2,0:T(4,128)(2,1)} %copy.85), calls=%async_computation.1 | async-start | bytes 2162688 | tf_op jit(solution)/shard_map/all_to_all | solution.py:285
  37.1 0.6 fusion.47
  37.8 1.6 %sort.17 = (s32[32]{0:T(128)}, s32[32]{0:T(128)S(1)}) sort(s32[32]{0:T(128)S(1)} %get-tuple-element.33, s32[32]{0:T(128)S(1)} %iota.81), dimensions={0}, to_apply=%region_2.3 | sort | flops 160 | bytes 512 | tf_op jit(solution)/shard_map/jit(argsort)/sort | solution.py:290
  39.4 0.6 gather_fusion
  40.3 1.2 %constant_dynamic-update-slice_fusion.8 = bf16[32,80,128]{2,1,0:T(8,128)(2,1)} fusion(s32[128]{0:T(128)S(1)} %iota_add_fusion, s32[32,8]{1,0:T(8,128)S(1)} %get-tuple-element.44), kind=kLoop, calls=%fused_computation.87 | loop fusion | flops 491519 | bytes 67072
  41.5 1.2 %constant_dynamic-update-slice_fusion.7 = bf16[32,80,128]{2,1,0:T(8,128)(2,1)} fusion(bf16[32,80,128]{2,1,0:T(8,128)(2,1)} %constant_dynamic-update-slice_fusion.8, s32[128]{0:T(128)S(1)} %iota_add_fusion, s32[32,8]{1,0:T(8,128)S(1)} %get-tuple-element.44), kind=kLoop, calls=%fused_computation.86 | loop fusion | flops 491520 | bytes 67072
  42.7 1.2 %constant_dynamic-update-slice_fusion.6 = bf16[32,80,128]{2,1,0:T(8,128)(2,1)} fusion(bf16[32,80,128]{2,1,0:T(8,128)(2,1)} %constant_dynamic-update-slice_fusion.7, s32[128]{0:T(128)S(1)} %iota_add_fusion, s32[32,8]{1,0:T(8,128)S(1)} %get-tuple-element.44), kind=kLoop, calls=%fused_computation.85 | loop fusion | flops 491520 | bytes 67072
  43.9 1.2 %constant_dynamic-update-slice_fusion.5 = bf16[32,80,128]{2,1,0:T(8,128)(2,1)} fusion(bf16[32,80,128]{2,1,0:T(8,128)(2,1)} %constant_dynamic-update-slice_fusion.6, s32[128]{0:T(128)S(1)} %iota_add_fusion, s32[32,8]{1,0:T(8,128)S(1)} %get-tuple-element.44), kind=kLoop, calls=%fused_computation.84 | loop fusion | flops 491520 | bytes 67072
  45.1 1.2 %constant_dynamic-update-slice_fusion.4 = bf16[32,80,128]{2,1,0:T(8,128)(2,1)} fusion(bf16[32,80,128]{2,1,0:T(8,128)(2,1)} %constant_dynamic-update-slice_fusion.5, s32[128]{0:T(128)S(1)} %iota_add_fusion, s32[32,8]{1,0:T(8,128)S(1)} %get-tuple-element.44), kind=kLoop, calls=%fused_computation.83 | loop fusion | flops 491520 | bytes 67072
  46.4 1.2 %constant_dynamic-update-slice_fusion.3 = bf16[32,80,128]{2,1,0:T(8,128)(2,1)} fusion(bf16[32,80,128]{2,1,0:T(8,128)(2,1)} %constant_dynamic-update-slice_fusion.4, s32[128]{0:T(128)S(1)} %iota_add_fusion, s32[32,8]{1,0:T(8,128)S(1)} %get-tuple-element.44), kind=kLoop, calls=%fused_computation.82 | loop fusion | flops 491520 | bytes 67072
  47.6 1.2 %constant_dynamic-update-slice_fusion.2 = bf16[32,80,128]{2,1,0:T(8,128)(2,1)} fusion(bf16[32,80,128]{2,1,0:T(8,128)(2,1)} %constant_dynamic-update-slice_fusion.3, s32[128]{0:T(128)S(1)} %iota_add_fusion, s32[32,8]{1,0:T(8,128)S(1)} %get-tuple-element.43), kind=kLoop, calls=%fused_computation.81 | loop fusion | flops 491520 | bytes 67072
  48.9 1.2 %constant_dynamic-update-slice_fusion.1 = bf16[32,80,128]{2,1,0:T(8,128)(2,1)} fusion(bf16[32,80,128]{2,1,0:T(8,128)(2,1)} %constant_dynamic-update-slice_fusion.2, s32[128]{0:T(128)S(1)} %iota_add_fusion, s32[32,8]{1,0:T(8,128)S(1)} %get-tuple-element.43), kind=kLoop, calls=%fused_computation.80 | loop fusion | flops 491520 | bytes 67072
  50.1 1.2 %negate_dynamic-update-slice_fusion = bf16[32,80,128]{2,1,0:T(8,128)(2,1)} fusion(bf16[32,80,128]{2,1,0:T(8,128)(2,1)} %constant_dynamic-update-slice_fusion.1, s32[128]{0:T(128)S(1)} %iota_add_fusion, s32[32,8]{1,0:T(8,128)S(1)} %get-tuple-element.43), kind=kLoop, calls=%fused_computation.76 | loop fusion | flops 589824 | bytes 67072
  51.3 1.2 %constant_dynamic-update-slice_fusion = bf16[32,80,128]{2,1,0:T(8,128)(2,1)} fusion(bf16[32,80,128]{2,1,0:T(8,128)(2,1)} %negate_dynamic-update-slice_fusion, s32[128]{0:T(128)S(1)} %iota_add_fusion, s32[32,8]{1,0:T(8,128)S(1)} %get-tuple-element.43), kind=kLoop, calls=%fused_computation.79 | loop fusion | flops 491520 | bytes 67072 | tf_op jit(solution)/shard_map/concatenate | solution.py:250
  52.5 2.3 %pad_bitcast_fusion = bf16[32,128,128]{1,2,0:T(8,128)(2,1)} fusion(bf16[32,80,128]{2,1,0:T(8,128)(2,1)} %constant_dynamic-update-slice_fusion), kind=kLoop, calls=%fused_computation.16 | loop fusion | bytes 1703936 | tf_op jit(solution)/shard_map/transpose | solution.py:252
  54.8 2.3 %copy.87.refs_10_ = bf16[32,128,128]{2,1,0:T(8,128)(2,1)} copy(bf16[32,128,128]{1,2,0:T(8,128)(2,1)} %pad_bitcast_fusion) | data formatting | bytes 2097152 | tf_op jit(solution)/shard_map/transpose | solution.py:252
  57.1 0.7 pad.21.clone
  57.8 1.2 %cosine_convert_fusion.1 = (bf16[32,8,128]{2,1,0:T(8,128)(2,1)S(1)}, bf16[32,8,128]{2,1,0:T(8,128)(2,1)S(1)}, bf16[32,8,128]{2,1,0:T(8,128)(2,1)S(1)}, bf16[32,8,128]{2,1,0:T(8,128)(2,1)S(1)}) fusion(s32[128]{0:T(128)S(1)} %iota_add_fusion, s32[32,8]{1,0:T(8,128)S(1)} %get-tuple-element.44, s32[32,8]{1,0:T(8,128)S(1)} %get-tuple-element.43), kind=kLoop, calls=%fused_computation.70 | loop fusion | flops 1048576 | bytes 264704 | tf_op jit(solution)/shard_map/convert_element_type | solution.py:241
  59.0 0.8 pad_maximum_fusion.2.refs_11_
  59.8 0.7 pad_add_fusion.meta_ref
  60.4 2.3 %all-to-all-done.1 = bf16[8,4,2,66,128]{4,1,3,2,0:T(4,128)(2,1)S(1)} async-done(((bf16[8,4,2,66,128]{4,1,3,2,0:T(4,128)(2,1)}), bf16[8,4,2,66,128]{4,1,3,2,0:T(4,128)(2,1)S(1)}, u32[]{:S(2)}, u32[]{:S(2)}) %all-to-all-start.1) | async-done | bytes 1081376 | tf_op jit(solution)/shard_map/all_to_all | solution.py:285
  62.7 1.2 %copy.86 = bf16[8,4,2,66,128]{4,3,2,1,0:T(8,128)(2,1)} copy(bf16[8,4,2,66,128]{4,1,3,2,0:T(4,128)(2,1)S(1)} %all-to-all-done.1) | data formatting | bytes 2162688 | tf_op jit(solution)/shard_map/all_to_all | solution.py:285
  63.9 12.6 %shard_map.77 = (f32[8,3,128,128]{3,2,1,0:T(8,128)}, f32[32,8,128]{2,1,0:T(8,128)}) custom-call(s32[6,32]{1,0:T(8,128)} %pad_add_fusion.meta_ref, bf16[32,2,66,128]{3,2,1,0:T(8,128)(2,1)} %bitcast.41, bf16[32,2,66,128]{3,2,1,0:T(8,128)(2,1)} %bitcast.42, bf16[32,2,66,128]{3,2,1,0:T(8,128)(2,1)} %bitcast.43, bf16[32,2,66,128]{3,2,1,0:T(8,128)(2,1)} %bitcast.44, ...), custom_call_target="tpu_custom_call" | custom-call | tf_op jit(solution)/shard_map/pallas_call | solution.py:224
  76.6 0.9 slice.61
  77.5 0.7 scatter_custom_fusion
  78.2 0.7 copy.91
  78.9 4.5 %all-to-all-start.2 = ((f32[8,4,3]{1,2,0:T(4,128)}), f32[8,4,3]{1,2,0:T(4,128)S(1)}, u32[]{:S(2)}, u32[]{:S(2)}) async-start(f32[8,4,3]{1,2,0:T(4,128)} %copy.91), calls=%async_computation.3 | async-start | bytes 32768 | tf_op jit(solution)/shard_map/all_to_all | solution.py:309
  83.4 6.6 %all-to-all-done.2 = f32[8,4,3]{1,2,0:T(4,128)S(1)} async-done(((f32[8,4,3]{1,2,0:T(4,128)}), f32[8,4,3]{1,2,0:T(4,128)S(1)}, u32[]{:S(2)}, u32[]{:S(2)}) %all-to-all-start.2) | async-done | bytes 416 | tf_op jit(solution)/shard_map/all_to_all | solution.py:309
  90.1 0.6 gather_fusion.1
  90.6 0.7 copy.94
  91.3 1.0 fusion.30
  92.3 1.9 %slice_divide_fusion = f32[8,2,64,128]{3,2,1,0:T(8,128)} fusion(f32[8,3,64,128]{3,2,1,0:T(8,128)} %reduce-scatter.2.cloned.1.call-done, f32[8,64,128]{2,1,0:T(8,128)S(1)} %fusion.30), kind=kLoop, calls=%fused_computation.34 | loop fusion | flops 131072 | bytes 1310720 | tf_op jit(solution)/shard_map/div | solution.py:314
  (36 shorter events, 2.6 us)
Async XLA Ops:
  7.2 12.8 %copy-start = (bf16[16,256,256]{2,1,0:T(8,128)(2,1)S(1)}, bf16[16,256,256]{2,1,0:T(8,128)(2,1)}, u32[]{:S(2)}) copy-start(bf16[16,256,256]{2,1,0:T(8,128)(2,1)} %param.6) | copy-start | bytes 6291460
  10.5 20.1 %all-to-all-start = ((f32[8,4,4]{1,2,0:T(4,128)}), f32[8,4,4]{1,2,0:T(4,128)S(1)}, u32[]{:S(2)}, u32[]{:S(2)}) async-start(f32[8,4,4]{1,2,0:T(4,128)} %copy.78), calls=%async_computation | async-start | bytes 32768 | tf_op jit(solution)/shard_map/all_to_all | solution.py:287
  30.6 32.1 %all-to-all-start.1 = ((bf16[8,4,2,66,128]{4,1,3,2,0:T(4,128)(2,1)}), bf16[8,4,2,66,128]{4,1,3,2,0:T(4,128)(2,1)S(1)}, u32[]{:S(2)}, u32[]{:S(2)}) async-start(bf16[8,4,2,66,128]{4,1,3,2,0:T(4,128)(2,1)} %copy.85), calls=%async_computation.1 | async-start | bytes 2162688 | tf_op jit(solution)/shard_map/all_to_all | solution.py:285
  36.6 54.7 %reduce-scatter.2.cloned.1.call-start = ((), (), s32[]{:S(2)}) async-start(), calls=%async_computation.4 | async-start | bytes 2359296 | tf_op jit(solution)/shard_map/reduce_scatter | solution.py:312
  78.9 11.0 %all-to-all-start.2 = ((f32[8,4,3]{1,2,0:T(4,128)}), f32[8,4,3]{1,2,0:T(4,128)S(1)}, u32[]{:S(2)}, u32[]{:S(2)}) async-start(f32[8,4,3]{1,2,0:T(4,128)} %copy.91), calls=%async_computation.3 | async-start | bytes 32768 | tf_op jit(solution)/shard_map/all_to_all | solution.py:309
Sparse Core Ops, SparseCore 0:
  76.7 9.7 reduce-scatter.1

commit v10 on v8

--- a/solution.py
+++ b/solution.py
@@ -93,28 +93,42 @@
         pick = (col == row - half - 1).astype(jnp.bfloat16)
         upper_rows = row <= half
         edge = (row > half) & (col == 0)
-        kept = []
+        tops = []
+        fulls = []
         for j in range(group):
             block = coef_refs[j][0]
             spare = jnp.zeros((win - block.shape[1], win), jnp.bfloat16)
             full_re = jnp.concatenate([block[0], spare], axis=0)
             full_im = jnp.concatenate([block[1], spare], axis=0)
             zero = jnp.zeros((), jnp.bfloat16)
-            top_re = jnp.where(upper_rows, full_re, zero)
-            top_im = jnp.where(upper_rows, full_im, zero)
-            turned = jnp.dot(
-                mirror, jnp.concatenate([top_re, top_im], axis=1), preferred_element_type=jnp.float32
-            ).astype(jnp.bfloat16)
-            stacked = jnp.concatenate([turned[:, 0:win], turned[:, win : 2 * win]], axis=0)
-            flipped = jnp.dot(stacked, mirror, preferred_element_type=jnp.float32)
-            column = lax.dot_general(
-                pick, jnp.concatenate([full_re, full_im], axis=0), (((1,), (1,)), ((), ())),
-                preferred_element_type=jnp.float32,
-            )
+            tops.append((jnp.where(upper_rows, full_re, zero), jnp.where(upper_rows, full_im, zero)))
+            fulls += [full_re, full_im]
+        turned_all = jnp.dot(
+            mirror, jnp.concatenate([t for pair in tops for t in pair], axis=1),
+            preferred_element_type=jnp.float32,
+        ).astype(jnp.bfloat16)
+        column_all = lax.dot_general(
+            pick, jnp.concatenate(fulls, axis=0), (((1,), (1,)), ((), ())),
+            preferred_element_type=jnp.float32,
+        )
+        pieces = [
+            (tops[j][0], tops[j][1], turned_all[:, 2 * j * win : (2 * j + 2) * win],
+             column_all[:, 2 * j * win : (2 * j + 2) * win])
+            for j in range(group)
+        ]
+        stacked = jnp.concatenate(
+            [part for _, _, turned, _ in pieces for part in (turned[:, 0:win], turned[:, win : 2 * win])],
+            axis=0,
+        )
+        flipped_all = jnp.dot(stacked, mirror, preferred_element_type=jnp.float32)
+        kept = []
+        for j, (top_re, top_im, turned, column) in enumerate(pieces):
+            flip_re = flipped_all[(2 * j) * win : (2 * j + 1) * win]
+            flip_im = flipped_all[(2 * j + 1) * win : (2 * j + 2) * win]
             col_re = pltpu.roll(column[:, 0:win], win - half - 1, 1)
             col_im = pltpu.roll(column[:, win : 2 * win], win - half - 1, 1)
-            coef_re = jnp.where(edge, col_re, jnp.where(upper_rows, top_re.astype(jnp.float32), flipped[0:win]))
-            coef_im = jnp.where(edge, col_im, jnp.where(upper_rows, top_im.astype(jnp.float32), -flipped[win : 2 * win]))
+            coef_re = jnp.where(edge, col_re, jnp.where(upper_rows, top_re.astype(jnp.float32), flip_re))
+            coef_im = jnp.where(edge, col_im, jnp.where(upper_rows, top_im.astype(jnp.float32), -flip_im))
             kept.append((coef_re, coef_im))
         st = []
         for j in range(group):

time: 102 us -> 99.6 us (0.976)
  Pallas kernels: 12.6 us -> 10.7 us
    pallas_call x1, Pallas kernels: 12.6 us -> 10.7 us  [group_eval(): pl.pallas_call(_group_kernel, grid_spec=grid_spec, out_shape=[jax.ShapeDt...]
  transfers between devices with their start and end apart: 4 -> 4, of which waited for: 2 -> 2; matrix products, arithmetic and copies ran while one was open for 39% -> 40% of each run, Pallas kernels for 0% -> 0%
where the time goes in v10:
time: 99.6 us; the launch traced here: 99 us
  other arithmetic  29 us (29%)
  starting transfers between devices  17.3 us (17%)
  local copies, waits for them, and re-layouts  15.1 us (15%)
  between operations  14.2 us (14%)
  Pallas kernels  10.7 us (11%)
  waiting for transfers between devices  8.84 us (9%)
  matrix products  3.76 us (4%)
    unnamed x9, other arithmetic  11 us
    pallas_call x1, Pallas kernels, group_eval(): pl.pallas_call(_group_kernel, grid_spec=grid_spec, out_shape=[jax.ShapeDt...  10.7 us
    all_to_all x1, starting transfers between devices, on_device(): lax.all_to_all(tag_buffer, 'dom', split_axis=0, concat_axis=0, tiled=True)  7.28 us
    all_to_all x1, waiting for transfers between devices, on_device(): lax.all_to_all(info.reshape(owners, capacity, 3), 'dom', split_axis=0, co...  6.57 us
    all_to_all x1, starting transfers between devices, on_device(): lax.all_to_all(buffer, 'dom', split_axis=0, concat_axis=0, tiled=True)  5.99 us
    transpose x2, local copies, waits for them, and re-layouts, phase_pack(): return (jnp.swapaxes(stacked, 1, 2), flat[:, :4 * TW])  4.55 us
    neg x1, other arithmetic, ctf_table(): return -jnp.sin(strength[:, None, None] * radius[None, :, :] + 0.1)  4.4 us
    all_to_all x1, starting transfers between devices, on_device(): lax.all_to_all(info.reshape(owners, capacity, 3), 'dom', split_axis=0, co...  3.82 us
  transfers between devices with their start and end apart: 4, of which 2 were waited for; matrix products, arithmetic and copies ran while one was open for 40% of the time, Pallas kernels for 0%

profile of v10, /device:TPU:0, one launch (start us, length us, event | category | flops | bytes accessed | tf_op | source)
XLA Modules:
  0.0 99.0 jit_solution(2197462812243519513)
XLA Ops:
  7.2 0.8 convert_bitcast_fusion.1
  8.2 0.7 convert.27
  8.9 0.7 convert_bitcast_fusion
  9.7 0.6 scatter_custom_fusion
  10.3 0.7 copy.80
  11.0 7.3 %all-to-all-start = ((bf16[8,4,4]{1,2,0:T(4,128)(2,1)}), bf16[8,4,4]{1,2,0:T(4,128)(2,1)S(1)}, u32[]{:S(2)}, u32[]{:S(2)}) async-start(bf16[8,4,4]{1,2,0:T(4,128)(2,1)} %copy.80), calls=%async_computation | async-start | bytes 16384 | tf_op jit(solution)/shard_map/all_to_all | solution.py:303
  18.3 0.6 multiply_convert_fusion.1
  19.4 0.4 rev.10
  19.9 0.7 and_compare_fusion.2
  20.5 0.8 fusion
  21.3 0.8 select_convert_fusion
  22.1 0.8 fusion.16
  23.0 0.8 fusion.10
  24.8 0.5 fusion.21
  25.3 4.4 %sine_negate_fusion.refs_9_ = f32[16,128,128]{2,1,0:T(8,128)} fusion(f32[128,128]{1,0:T(8,128)S(1)} %add_multiply_fusion, f32[16]{0:T(128)S(1)} %multiply_add_fusion), kind=kLoop, calls=%fused_computation.18 | loop fusion | flops 786432 | bytes 1114176 | tf_op jit(solution)/shard_map/neg | solution.py:40
  29.7 1.4 %copy.87 = bf16[8,4,2,66,128]{4,1,3,2,0:T(4,128)(2,1)} copy(bf16[8,4,2,66,128]{4,1,0,3,2:T(4,128)(2,1)S(1)} %bitcast.49) | data formatting | bytes 2162688 | tf_op jit(solution)/shard_map/reshape | solution.py:300
  31.1 6.0 %all-to-all-start.1 = ((bf16[8,4,2,66,128]{4,1,3,2,0:T(4,128)(2,1)}), bf16[8,4,2,66,128]{4,1,3,2,0:T(4,128)(2,1)S(1)}, u32[]{:S(2)}, u32[]{:S(2)}) async-start(bf16[8,4,2,66,128]{4,1,3,2,0:T(4,128)(2,1)} %copy.87), calls=%async_computation.1 | async-start | bytes 2162688 | tf_op jit(solution)/shard_map/all_to_all | solution.py:301
  37.6 0.6 fusion.51
  38.4 1.6 %sort.17 = (s32[32]{0:T(128)}, s32[32]{0:T(128)S(1)}) sort(s32[32]{0:T(128)S(1)} %get-tuple-element.33, s32[32]{0:T(128)S(1)} %iota.76), dimensions={0}, to_apply=%region_2.3 | sort | flops 160 | bytes 512 | tf_op jit(solution)/shard_map/jit(argsort)/sort | solution.py:306
  40.0 0.6 gather_fusion
  40.8 1.2 %constant_dynamic-update-slice_fusion.8 = bf16[32,80,128]{2,1,0:T(8,128)(2,1)} fusion(s32[128]{0:T(128)S(1)} %iota_add_fusion, s32[32,8]{1,0:T(8,128)S(1)} %get-tuple-element.44), kind=kLoop, calls=%fused_computation.87 | loop fusion | flops 491519 | bytes 67072
  42.0 1.2 %constant_dynamic-update-slice_fusion.7 = bf16[32,80,128]{2,1,0:T(8,128)(2,1)} fusion(bf16[32,80,128]{2,1,0:T(8,128)(2,1)} %constant_dynamic-update-slice_fusion.8, s32[128]{0:T(128)S(1)} %iota_add_fusion, s32[32,8]{1,0:T(8,128)S(1)} %get-tuple-element.44), kind=kLoop, calls=%fused_computation.86 | loop fusion | flops 491520 | bytes 67072
  43.2 1.2 %constant_dynamic-update-slice_fusion.6 = bf16[32,80,128]{2,1,0:T(8,128)(2,1)} fusion(bf16[32,80,128]{2,1,0:T(8,128)(2,1)} %constant_dynamic-update-slice_fusion.7, s32[128]{0:T(128)S(1)} %iota_add_fusion, s32[32,8]{1,0:T(8,128)S(1)} %get-tuple-element.44), kind=kLoop, calls=%fused_computation.85 | loop fusion | flops 491520 | bytes 67072
  44.5 1.2 %constant_dynamic-update-slice_fusion.5 = bf16[32,80,128]{2,1,0:T(8,128)(2,1)} fusion(bf16[32,80,128]{2,1,0:T(8,128)(2,1)} %constant_dynamic-update-slice_fusion.6, s32[128]{0:T(128)S(1)} %iota_add_fusion, s32[32,8]{1,0:T(8,128)S(1)} %get-tuple-element.44), kind=kLoop, calls=%fused_computation.84 | loop fusion | flops 491520 | bytes 67072
  45.7 1.2 %constant_dynamic-update-slice_fusion.4 = bf16[32,80,128]{2,1,0:T(8,128)(2,1)} fusion(bf16[32,80,128]{2,1,0:T(8,128)(2,1)} %constant_dynamic-update-slice_fusion.5, s32[128]{0:T(128)S(1)} %iota_add_fusion, s32[32,8]{1,0:T(8,128)S(1)} %get-tuple-element.44), kind=kLoop, calls=%fused_computation.83 | loop fusion | flops 491520 | bytes 67072
  47.0 1.2 %constant_dynamic-update-slice_fusion.3 = bf16[32,80,128]{2,1,0:T(8,128)(2,1)} fusion(bf16[32,80,128]{2,1,0:T(8,128)(2,1)} %constant_dynamic-update-slice_fusion.4, s32[128]{0:T(128)S(1)} %iota_add_fusion, s32[32,8]{1,0:T(8,128)S(1)} %get-tuple-element.44), kind=kLoop, calls=%fused_computation.82 | loop fusion | flops 491520 | bytes 67072
  48.2 1.2 %constant_dynamic-update-slice_fusion.2 = bf16[32,80,128]{2,1,0:T(8,128)(2,1)} fusion(bf16[32,80,128]{2,1,0:T(8,128)(2,1)} %constant_dynamic-update-slice_fusion.3, s32[128]{0:T(128)S(1)} %iota_add_fusion, s32[32,8]{1,0:T(8,128)S(1)} %get-tuple-element.43), kind=kLoop, calls=%fused_computation.81 | loop fusion | flops 491520 | bytes 67072
  49.4 1.2 %constant_dynamic-update-slice_fusion.1 = bf16[32,80,128]{2,1,0:T(8,128)(2,1)} fusion(bf16[32,80,128]{2,1,0:T(8,128)(2,1)} %constant_dynamic-update-slice_fusion.2, s32[128]{0:T(128)S(1)} %iota_add_fusion, s32[32,8]{1,0:T(8,128)S(1)} %get-tuple-element.43), kind=kLoop, calls=%fused_computation.80 | loop fusion | flops 491520 | bytes 67072
  50.7 1.2 %negate_dynamic-update-slice_fusion = bf16[32,80,128]{2,1,0:T(8,128)(2,1)} fusion(bf16[32,80,128]{2,1,0:T(8,128)(2,1)} %constant_dynamic-update-slice_fusion.1, s32[128]{0:T(128)S(1)} %iota_add_fusion, s32[32,8]{1,0:T(8,128)S(1)} %get-tuple-element.43), kind=kLoop, calls=%fused_computation.77 | loop fusion | flops 589824 | bytes 67072
  51.9 1.2 %constant_dynamic-update-slice_fusion = bf16[32,80,128]{2,1,0:T(8,128)(2,1)} fusion(bf16[32,80,128]{2,1,0:T(8,128)(2,1)} %negate_dynamic-update-slice_fusion, s32[128]{0:T(128)S(1)} %iota_add_fusion, s32[32,8]{1,0:T(8,128)S(1)} %get-tuple-element.43), kind=kLoop, calls=%fused_computation.79 | loop fusion | flops 491520 | bytes 67072 | tf_op jit(solution)/shard_map/concatenate | solution.py:264
  53.1 2.3 %pad_bitcast_fusion = bf16[32,128,128]{1,2,0:T(8,128)(2,1)} fusion(bf16[32,80,128]{2,1,0:T(8,128)(2,1)} %constant_dynamic-update-slice_fusion), kind=kLoop, calls=%fused_computation.17 | loop fusion | bytes 1703936 | tf_op jit(solution)/shard_map/transpose | solution.py:266
  55.4 2.3 %copy.89.refs_10_ = bf16[32,128,128]{2,1,0:T(8,128)(2,1)} copy(bf16[32,128,128]{1,2,0:T(8,128)(2,1)} %pad_bitcast_fusion) | data formatting | bytes 2097152 | tf_op jit(solution)/shard_map/transpose | solution.py:266
  57.6 0.7 pad.21.clone
  58.3 1.2 %cosine_convert_fusion.1 = (bf16[32,8,128]{2,1,0:T(8,128)(2,1)S(1)}, bf16[32,8,128]{2,1,0:T(8,128)(2,1)S(1)}, bf16[32,8,128]{2,1,0:T(8,128)(2,1)S(1)}, bf16[32,8,128]{2,1,0:T(8,128)(2,1)S(1)}) fusion(s32[128]{0:T(128)S(1)} %iota_add_fusion, s32[32,8]{1,0:T(8,128)S(1)} %get-tuple-element.44, s32[32,8]{1,0:T(8,128)S(1)} %get-tuple-element.43), kind=kLoop, calls=%fused_computation.71 | loop fusion | flops 1048576 | bytes 264704 | tf_op jit(solution)/shard_map/convert_element_type | solution.py:255
  59.6 0.8 pad_maximum_fusion.2.refs_11_
  60.3 0.7 pad_add_fusion.meta_ref
  61.0 2.3 %all-to-all-done.1 = bf16[8,4,2,66,128]{4,1,3,2,0:T(4,128)(2,1)S(1)} async-done(((bf16[8,4,2,66,128]{4,1,3,2,0:T(4,128)(2,1)}), bf16[8,4,2,66,128]{4,1,3,2,0:T(4,128)(2,1)S(1)}, u32[]{:S(2)}, u32[]{:S(2)}) %all-to-all-start.1) | async-done | bytes 1081376 | tf_op jit(solution)/shard_map/all_to_all | solution.py:301
  63.2 1.2 %copy.88 = bf16[8,4,2,66,128]{4,3,2,1,0:T(8,128)(2,1)} copy(bf16[8,4,2,66,128]{4,1,3,2,0:T(4,128)(2,1)S(1)} %all-to-all-done.1) | data formatting | bytes 2162688 | tf_op jit(solution)/shard_map/all_to_all | solution.py:301
  64.4 10.7 %shard_map.77 = (f32[8,3,128,128]{3,2,1,0:T(8,128)}, f32[32,8,128]{2,1,0:T(8,128)}) custom-call(s32[6,32]{1,0:T(8,128)} %pad_add_fusion.meta_ref, bf16[32,2,66,128]{3,2,1,0:T(8,128)(2,1)} %bitcast.41, bf16[32,2,66,128]{3,2,1,0:T(8,128)(2,1)} %bitcast.42, bf16[32,2,66,128]{3,2,1,0:T(8,128)(2,1)} %bitcast.43, bf16[32,2,66,128]{3,2,1,0:T(8,128)(2,1)} %bitcast.44, ...), custom_call_target="tpu_custom_call" | custom-call | tf_op jit(solution)/shard_map/pallas_call | solution.py:238
  75.2 0.9 slice.63
  76.1 0.7 scatter_custom_fusion.1
  76.8 0.7 copy.93
  77.5 3.8 %all-to-all-start.2 = ((f32[8,4,3]{1,2,0:T(4,128)}), f32[8,4,3]{1,2,0:T(4,128)S(1)}, u32[]{:S(2)}, u32[]{:S(2)}) async-start(f32[8,4,3]{1,2,0:T(4,128)} %copy.93), calls=%async_computation.3 | async-start | bytes 32768 | tf_op jit(solution)/shard_map/all_to_all | solution.py:325
  81.3 6.6 %all-to-all-done.2 = f32[8,4,3]{1,2,0:T(4,128)S(1)} async-done(((f32[8,4,3]{1,2,0:T(4,128)}), f32[8,4,3]{1,2,0:T(4,128)S(1)}, u32[]{:S(2)}, u32[]{:S(2)}) %all-to-all-start.2) | async-done | bytes 416 | tf_op jit(solution)/shard_map/all_to_all | solution.py:325
  88.0 0.6 gather_fusion.1
  88.6 0.7 copy.96
  89.2 1.0 fusion.30
  90.2 1.9 %slice_divide_fusion = f32[8,2,64,128]{3,2,1,0:T(8,128)} fusion(f32[8,3,64,128]{3,2,1,0:T(8,128)} %reduce-scatter.2.cloned.1.call-done, f32[8,64,128]{2,1,0:T(8,128)S(1)} %fusion.30), kind=kLoop, calls=%fused_computation.35 | loop fusion | flops 131072 | bytes 1310720 | tf_op jit(solution)/shard_map/div | solution.py:330
  (37 shorter events, 2.9 us)
Async XLA Ops:
  7.2 13.4 %copy-start = (bf16[16,256,256]{2,1,0:T(8,128)(2,1)S(1)}, bf16[16,256,256]{2,1,0:T(8,128)(2,1)}, u32[]{:S(2)}) copy-start(bf16[16,256,256]{2,1,0:T(8,128)(2,1)} %param.6) | copy-start | bytes 6291460
  11.0 20.1 %all-to-all-start = ((bf16[8,4,4]{1,2,0:T(4,128)(2,1)}), bf16[8,4,4]{1,2,0:T(4,128)(2,1)S(1)}, u32[]{:S(2)}, u32[]{:S(2)}) async-start(bf16[8,4,4]{1,2,0:T(4,128)(2,1)} %copy.80), calls=%async_computation | async-start | bytes 16384 | tf_op jit(solution)/shard_map/all_to_all | solution.py:303
  31.1 32.1 %all-to-all-start.1 = ((bf16[8,4,2,66,128]{4,1,3,2,0:T(4,128)(2,1)}), bf16[8,4,2,66,128]{4,1,3,2,0:T(4,128)(2,1)S(1)}, u32[]{:S(2)}, u32[]{:S(2)}) async-start(bf16[8,4,2,66,128]{4,1,3,2,0:T(4,128)(2,1)} %copy.87), calls=%async_computation.1 | async-start | bytes 2162688 | tf_op jit(solution)/shard_map/all_to_all | solution.py:301
  37.1 52.2 %reduce-scatter.2.cloned.1.call-start = ((), (), s32[]{:S(2)}) async-start(), calls=%async_computation.4 | async-start | bytes 2359296 | tf_op jit(solution)/shard_map/reduce_scatter | solution.py:328
  77.5 10.4 %all-to-all-start.2 = ((f32[8,4,3]{1,2,0:T(4,128)}), f32[8,4,3]{1,2,0:T(4,128)S(1)}, u32[]{:S(2)}, u32[]{:S(2)}) async-start(f32[8,4,3]{1,2,0:T(4,128)} %copy.93), calls=%async_computation.3 | async-start | bytes 32768 | tf_op jit(solution)/shard_map/all_to_all | solution.py:325
Sparse Core Ops, SparseCore 0:
  75.3 9.1 reduce-scatter.1

commit v11 on v8

--- a/solution.py
+++ b/solution.py
@@ -93,7 +93,7 @@
         pick = (col == row - half - 1).astype(jnp.bfloat16)
         upper_rows = row <= half
         edge = (row > half) & (col == 0)
-        kept = []
+        pieces = []
         for j in range(group):
             block = coef_refs[j][0]
             spare = jnp.zeros((win - block.shape[1], win), jnp.bfloat16)
@@ -105,16 +105,24 @@
             turned = jnp.dot(
                 mirror, jnp.concatenate([top_re, top_im], axis=1), preferred_element_type=jnp.float32
             ).astype(jnp.bfloat16)
-            stacked = jnp.concatenate([turned[:, 0:win], turned[:, win : 2 * win]], axis=0)
-            flipped = jnp.dot(stacked, mirror, preferred_element_type=jnp.float32)
             column = lax.dot_general(
                 pick, jnp.concatenate([full_re, full_im], axis=0), (((1,), (1,)), ((), ())),
                 preferred_element_type=jnp.float32,
             )
+            pieces.append((top_re, top_im, turned, column))
+        stacked = jnp.concatenate(
+            [part for _, _, turned, _ in pieces for part in (turned[:, 0:win], turned[:, win : 2 * win])],
+            axis=0,
+        )
+        flipped_all = jnp.dot(stacked, mirror, preferred_element_type=jnp.float32)
+        kept = []
+        for j, (top_re, top_im, turned, column) in enumerate(pieces):
+            flip_re = flipped_all[(2 * j) * win : (2 * j + 1) * win]
+            flip_im = flipped_all[(2 * j + 1) * win : (2 * j + 2) * win]
             col_re = pltpu.roll(column[:, 0:win], win - half - 1, 1)
             col_im = pltpu.roll(column[:, win : 2 * win], win - half - 1, 1)
-            coef_re = jnp.where(edge, col_re, jnp.where(upper_rows, top_re.astype(jnp.float32), flipped[0:win]))
-            coef_im = jnp.where(edge, col_im, jnp.where(upper_rows, top_im.astype(jnp.float32), -flipped[win : 2 * win]))
+            coef_re = jnp.where(edge, col_re, jnp.where(upper_rows, top_re.astype(jnp.float32), flip_re))
+            coef_im = jnp.where(edge, col_im, jnp.where(upper_rows, top_im.astype(jnp.float32), -flip_im))
             kept.append((coef_re, coef_im))
         st = []
         for j in range(group):
@@ -296,7 +304,7 @@
         [tag_sorted.T, jnp.full((1, slot_count), count, jnp.int32)], axis=0
     )
     pack, flat = phase_pack(tag_sorted, img_side, win_side)
-    group = 8 if slot_count % 8 == 0 else 1
+    group = 16 if slot_count % 16 == 0 else 1
     partial_value, info_sorted = group_eval(
         meta,
         order,

time: 102 us -> 99.5 us (0.975)
  Pallas kernels: 12.6 us -> 11 us
    pallas_call x1, Pallas kernels: 12.6 us -> 11 us  [group_eval(): pl.pallas_call(_group_kernel, grid_spec=grid_spec, out_shape=[jax.ShapeDt...]
  transfers between devices with their start and end apart: 4 -> 4, of which waited for: 2 -> 2; matrix products, arithmetic and copies ran while one was open for 39% -> 40% of each run, Pallas kernels for 0% -> 0%
where the time goes in v11:
time: 99.5 us; the launch traced here: 98.9 us
  other arithmetic  29 us (29%)
  starting transfers between devices  17 us (17%)
  local copies, waits for them, and re-layouts  15.1 us (15%)
  between operations  14.2 us (14%)
  Pallas kernels  11 us (11%)
  waiting for transfers between devices  8.84 us (9%)
  matrix products  3.76 us (4%)
    unnamed x9, other arithmetic  11 us
    pallas_call x1, Pallas kernels, group_eval(): pl.pallas_call(_group_kernel, grid_spec=grid_spec, out_shape=[jax.ShapeDt...  11 us
    all_to_all x1, starting transfers between devices, on_device(): lax.all_to_all(tag_buffer, 'dom', split_axis=0, concat_axis=0, tiled=True)  7.28 us
    all_to_all x1, waiting for transfers between devices, on_device(): lax.all_to_all(info.reshape(owners, capacity, 3), 'dom', split_axis=0, co...  6.57 us
    all_to_all x1, starting transfers between devices, on_device(): lax.all_to_all(buffer, 'dom', split_axis=0, concat_axis=0, tiled=True)  5.99 us
    transpose x2, local copies, waits for them, and re-layouts, phase_pack(): return (jnp.swapaxes(stacked, 1, 2), flat[:, :4 * TW])  4.55 us
    neg x1, other arithmetic, ctf_table(): return -jnp.sin(strength[:, None, None] * radius[None, :, :] + 0.1)  4.4 us
    all_to_all x1, starting transfers between devices, on_device(): lax.all_to_all(info.reshape(owners, capacity, 3), 'dom', split_axis=0, co...  3.52 us
  transfers between devices with their start and end apart: 4, of which 2 were waited for; matrix products, arithmetic and copies ran while one was open for 40% of the time, Pallas kernels for 0%

profile of v11, /device:TPU:0, one launch (start us, length us, event | category | flops | bytes accessed | tf_op | source)
XLA Modules:
  0.0 98.9 jit_solution(634037999738413775)
XLA Ops:
  7.2 0.8 convert_bitcast_fusion.1
  8.2 0.7 convert.27
  8.9 0.7 convert_bitcast_fusion
  9.7 0.6 scatter_custom_fusion
  10.3 0.7 copy.80
  11.0 7.3 %all-to-all-start = ((bf16[8,4,4]{1,2,0:T(4,128)(2,1)}), bf16[8,4,4]{1,2,0:T(4,128)(2,1)S(1)}, u32[]{:S(2)}, u32[]{:S(2)}) async-start(bf16[8,4,4]{1,2,0:T(4,128)(2,1)} %copy.80), calls=%async_computation | async-start | bytes 16384 | tf_op jit(solution)/shard_map/all_to_all | solution.py:297
  18.3 0.6 multiply_convert_fusion.1
  19.4 0.4 rev.10
  19.9 0.7 and_compare_fusion.2
  20.5 0.8 fusion
  21.3 0.8 select_convert_fusion
  22.1 0.8 fusion.16
  23.0 0.8 fusion.10
  24.8 0.5 fusion.21
  25.3 4.4 %sine_negate_fusion.refs_17_ = f32[16,128,128]{2,1,0:T(8,128)} fusion(f32[128,128]{1,0:T(8,128)S(1)} %add_multiply_fusion, f32[16]{0:T(128)S(1)} %multiply_add_fusion), kind=kLoop, calls=%fused_computation.18 | loop fusion | flops 786432 | bytes 1114176 | tf_op jit(solution)/shard_map/neg | solution.py:40
  29.7 1.4 %copy.87 = bf16[8,4,2,66,128]{4,1,3,2,0:T(4,128)(2,1)} copy(bf16[8,4,2,66,128]{4,1,0,3,2:T(4,128)(2,1)S(1)} %bitcast.57) | data formatting | bytes 2162688 | tf_op jit(solution)/shard_map/reshape | solution.py:294
  31.1 6.0 %all-to-all-start.1 = ((bf16[8,4,2,66,128]{4,1,3,2,0:T(4,128)(2,1)}), bf16[8,4,2,66,128]{4,1,3,2,0:T(4,128)(2,1)S(1)}, u32[]{:S(2)}, u32[]{:S(2)}) async-start(bf16[8,4,2,66,128]{4,1,3,2,0:T(4,128)(2,1)} %copy.87), calls=%async_computation.1 | async-start | bytes 2162688 | tf_op jit(solution)/shard_map/all_to_all | solution.py:295
  37.6 0.6 fusion.51
  38.4 1.6 %sort.17 = (s32[32]{0:T(128)}, s32[32]{0:T(128)S(1)}) sort(s32[32]{0:T(128)S(1)} %get-tuple-element.33, s32[32]{0:T(128)S(1)} %iota.76), dimensions={0}, to_apply=%region_2.3 | sort | flops 160 | bytes 512 | tf_op jit(solution)/shard_map/jit(argsort)/sort | solution.py:300
  40.0 0.6 gather_fusion
  40.8 1.2 %constant_dynamic-update-slice_fusion.8 = bf16[32,80,128]{2,1,0:T(8,128)(2,1)} fusion(s32[128]{0:T(128)S(1)} %iota_add_fusion, s32[32,8]{1,0:T(8,128)S(1)} %get-tuple-element.44), kind=kLoop, calls=%fused_computation.87 | loop fusion | flops 491519 | bytes 67072
  42.0 1.2 %constant_dynamic-update-slice_fusion.7 = bf16[32,80,128]{2,1,0:T(8,128)(2,1)} fusion(bf16[32,80,128]{2,1,0:T(8,128)(2,1)} %constant_dynamic-update-slice_fusion.8, s32[128]{0:T(128)S(1)} %iota_add_fusion, s32[32,8]{1,0:T(8,128)S(1)} %get-tuple-element.44), kind=kLoop, calls=%fused_computation.86 | loop fusion | flops 491520 | bytes 67072
  43.2 1.2 %constant_dynamic-update-slice_fusion.6 = bf16[32,80,128]{2,1,0:T(8,128)(2,1)} fusion(bf16[32,80,128]{2,1,0:T(8,128)(2,1)} %constant_dynamic-update-slice_fusion.7, s32[128]{0:T(128)S(1)} %iota_add_fusion, s32[32,8]{1,0:T(8,128)S(1)} %get-tuple-element.44), kind=kLoop, calls=%fused_computation.85 | loop fusion | flops 491520 | bytes 67072
  44.5 1.2 %constant_dynamic-update-slice_fusion.5 = bf16[32,80,128]{2,1,0:T(8,128)(2,1)} fusion(bf16[32,80,128]{2,1,0:T(8,128)(2,1)} %constant_dynamic-update-slice_fusion.6, s32[128]{0:T(128)S(1)} %iota_add_fusion, s32[32,8]{1,0:T(8,128)S(1)} %get-tuple-element.44), kind=kLoop, calls=%fused_computation.84 | loop fusion | flops 491520 | bytes 67072
  45.7 1.2 %constant_dynamic-update-slice_fusion.4 = bf16[32,80,128]{2,1,0:T(8,128)(2,1)} fusion(bf16[32,80,128]{2,1,0:T(8,128)(2,1)} %constant_dynamic-update-slice_fusion.5, s32[128]{0:T(128)S(1)} %iota_add_fusion, s32[32,8]{1,0:T(8,128)S(1)} %get-tuple-element.44), kind=kLoop, calls=%fused_computation.83 | loop fusion | flops 491520 | bytes 67072
  47.0 1.2 %constant_dynamic-update-slice_fusion.3 = bf16[32,80,128]{2,1,0:T(8,128)(2,1)} fusion(bf16[32,80,128]{2,1,0:T(8,128)(2,1)} %constant_dynamic-update-slice_fusion.4, s32[128]{0:T(128)S(1)} %iota_add_fusion, s32[32,8]{1,0:T(8,128)S(1)} %get-tuple-element.44), kind=kLoop, calls=%fused_computation.82 | loop fusion | flops 491520 | bytes 67072
  48.2 1.2 %constant_dynamic-update-slice_fusion.2 = bf16[32,80,128]{2,1,0:T(8,128)(2,1)} fusion(bf16[32,80,128]{2,1,0:T(8,128)(2,1)} %constant_dynamic-update-slice_fusion.3, s32[128]{0:T(128)S(1)} %iota_add_fusion, s32[32,8]{1,0:T(8,128)S(1)} %get-tuple-element.43), kind=kLoop, calls=%fused_computation.81 | loop fusion | flops 491520 | bytes 67072
  49.4 1.2 %constant_dynamic-update-slice_fusion.1 = bf16[32,80,128]{2,1,0:T(8,128)(2,1)} fusion(bf16[32,80,128]{2,1,0:T(8,128)(2,1)} %constant_dynamic-update-slice_fusion.2, s32[128]{0:T(128)S(1)} %iota_add_fusion, s32[32,8]{1,0:T(8,128)S(1)} %get-tuple-element.43), kind=kLoop, calls=%fused_computation.80 | loop fusion | flops 491520 | bytes 67072
  50.7 1.2 %negate_dynamic-update-slice_fusion = bf16[32,80,128]{2,1,0:T(8,128)(2,1)} fusion(bf16[32,80,128]{2,1,0:T(8,128)(2,1)} %constant_dynamic-update-slice_fusion.1, s32[128]{0:T(128)S(1)} %iota_add_fusion, s32[32,8]{1,0:T(8,128)S(1)} %get-tuple-element.43), kind=kLoop, calls=%fused_computation.77 | loop fusion | flops 589824 | bytes 67072
  51.9 1.2 %constant_dynamic-update-slice_fusion = bf16[32,80,128]{2,1,0:T(8,128)(2,1)} fusion(bf16[32,80,128]{2,1,0:T(8,128)(2,1)} %negate_dynamic-update-slice_fusion, s32[128]{0:T(128)S(1)} %iota_add_fusion, s32[32,8]{1,0:T(8,128)S(1)} %get-tuple-element.43), kind=kLoop, calls=%fused_computation.79 | loop fusion | flops 491520 | bytes 67072 | tf_op jit(solution)/shard_map/concatenate | solution.py:258
  53.1 2.3 %pad_bitcast_fusion = bf16[32,128,128]{1,2,0:T(8,128)(2,1)} fusion(bf16[32,80,128]{2,1,0:T(8,128)(2,1)} %constant_dynamic-update-slice_fusion), kind=kLoop, calls=%fused_computation.17 | loop fusion | bytes 1703936 | tf_op jit(solution)/shard_map/transpose | solution.py:260
  55.4 2.3 %copy.89.refs_18_ = bf16[32,128,128]{2,1,0:T(8,128)(2,1)} copy(bf16[32,128,128]{1,2,0:T(8,128)(2,1)} %pad_bitcast_fusion) | data formatting | bytes 2097152 | tf_op jit(solution)/shard_map/transpose | solution.py:260
  57.6 0.7 pad.21.clone
  58.3 1.2 %cosine_convert_fusion.1 = (bf16[32,8,128]{2,1,0:T(8,128)(2,1)S(1)}, bf16[32,8,128]{2,1,0:T(8,128)(2,1)S(1)}, bf16[32,8,128]{2,1,0:T(8,128)(2,1)S(1)}, bf16[32,8,128]{2,1,0:T(8,128)(2,1)S(1)}) fusion(s32[128]{0:T(128)S(1)} %iota_add_fusion, s32[32,8]{1,0:T(8,128)S(1)} %get-tuple-element.44, s32[32,8]{1,0:T(8,128)S(1)} %get-tuple-element.43), kind=kLoop, calls=%fused_computation.71 | loop fusion | flops 1048576 | bytes 264704 | tf_op jit(solution)/shard_map/convert_element_type | solution.py:249
  59.6 0.8 pad_maximum_fusion.2.refs_19_
  60.3 0.7 pad_add_fusion.meta_ref
  61.0 2.3 %all-to-all-done.1 = bf16[8,4,2,66,128]{4,1,3,2,0:T(4,128)(2,1)S(1)} async-done(((bf16[8,4,2,66,128]{4,1,3,2,0:T(4,128)(2,1)}), bf16[8,4,2,66,128]{4,1,3,2,0:T(4,128)(2,1)S(1)}, u32[]{:S(2)}, u32[]{:S(2)}) %all-to-all-start.1) | async-done | bytes 1081376 | tf_op jit(solution)/shard_map/all_to_all | solution.py:295
  63.2 1.2 %copy.88 = bf16[8,4,2,66,128]{4,3,2,1,0:T(8,128)(2,1)} copy(bf16[8,4,2,66,128]{4,1,3,2,0:T(4,128)(2,1)S(1)} %all-to-all-done.1) | data formatting | bytes 2162688 | tf_op jit(solution)/shard_map/all_to_all | solution.py:295
  64.4 11.0 %shard_map.77 = (f32[8,3,128,128]{3,2,1,0:T(8,128)}, f32[32,8,128]{2,1,0:T(8,128)}) custom-call(s32[6,32]{1,0:T(8,128)} %pad_add_fusion.meta_ref, bf16[32,2,66,128]{3,2,1,0:T(8,128)(2,1)} %bitcast.41, bf16[32,2,66,128]{3,2,1,0:T(8,128)(2,1)} %bitcast.42, bf16[32,2,66,128]{3,2,1,0:T(8,128)(2,1)} %bitcast.43, bf16[32,2,66,128]{3,2,1,0:T(8,128)(2,1)} %bitcast.44, ...), custom_call_target="tpu_custom_call" | custom-call | tf_op jit(solution)/shard_map/pallas_call | solution.py:232
  75.4 0.9 slice.63
  76.3 0.7 scatter_custom_fusion.1
  77.0 0.7 copy.93
  77.8 3.5 %all-to-all-start.2 = ((f32[8,4,3]{1,2,0:T(4,128)}), f32[8,4,3]{1,2,0:T(4,128)S(1)}, u32[]{:S(2)}, u32[]{:S(2)}) async-start(f32[8,4,3]{1,2,0:T(4,128)} %copy.93), calls=%async_computation.3 | async-start | bytes 32768 | tf_op jit(solution)/shard_map/all_to_all | solution.py:319
  81.3 6.6 %all-to-all-done.2 = f32[8,4,3]{1,2,0:T(4,128)S(1)} async-done(((f32[8,4,3]{1,2,0:T(4,128)}), f32[8,4,3]{1,2,0:T(4,128)S(1)}, u32[]{:S(2)}, u32[]{:S(2)}) %all-to-all-start.2) | async-done | bytes 416 | tf_op jit(solution)/shard_map/all_to_all | solution.py:319
  88.0 0.6 gather_fusion.1
  88.6 0.7 copy.96
  89.2 1.0 fusion.30
  90.2 1.9 %slice_divide_fusion = f32[8,2,64,128]{3,2,1,0:T(8,128)} fusion(f32[8,3,64,128]{3,2,1,0:T(8,128)} %reduce-scatter.2.cloned.1.call-done, f32[8,64,128]{2,1,0:T(8,128)S(1)} %fusion.30), kind=kLoop, calls=%fused_computation.35 | loop fusion | flops 131072 | bytes 1310720 | tf_op jit(solution)/shard_map/div | solution.py:324
  (37 shorter events, 2.9 us)
Async XLA Ops:
  7.2 13.4 %copy-start = (bf16[16,256,256]{2,1,0:T(8,128)(2,1)S(1)}, bf16[16,256,256]{2,1,0:T(8,128)(2,1)}, u32[]{:S(2)}) copy-start(bf16[16,256,256]{2,1,0:T(8,128)(2,1)} %param.6) | copy-start | bytes 6291460
  11.0 20.1 %all-to-all-start = ((bf16[8,4,4]{1,2,0:T(4,128)(2,1)}), bf16[8,4,4]{1,2,0:T(4,128)(2,1)S(1)}, u32[]{:S(2)}, u32[]{:S(2)}) async-start(bf16[8,4,4]{1,2,0:T(4,128)(2,1)} %copy.80), calls=%async_computation | async-start | bytes 16384 | tf_op jit(solution)/shard_map/all_to_all | solution.py:297
  31.1 32.1 %all-to-all-start.1 = ((bf16[8,4,2,66,128]{4,1,3,2,0:T(4,128)(2,1)}), bf16[8,4,2,66,128]{4,1,3,2,0:T(4,128)(2,1)S(1)}, u32[]{:S(2)}, u32[]{:S(2)}) async-start(bf16[8,4,2,66,128]{4,1,3,2,0:T(4,128)(2,1)} %copy.87), calls=%async_computation.1 | async-start | bytes 2162688 | tf_op jit(solution)/shard_map/all_to_all | solution.py:295
  37.1 52.1 %reduce-scatter.2.cloned.1.call-start = ((), (), s32[]{:S(2)}) async-start(), calls=%async_computation.4 | async-start | bytes 2359296 | tf_op jit(solution)/shard_map/reduce_scatter | solution.py:322
  77.8 10.1 %all-to-all-start.2 = ((f32[8,4,3]{1,2,0:T(4,128)}), f32[8,4,3]{1,2,0:T(4,128)S(1)}, u32[]{:S(2)}, u32[]{:S(2)}) async-start(f32[8,4,3]{1,2,0:T(4,128)} %copy.93), calls=%async_computation.3 | async-start | bytes 32768 | tf_op jit(solution)/shard_map/all_to_all | solution.py:319
Sparse Core Ops, SparseCore 0:
  75.6 7.0 reduce-scatter.1
